TPU v7x, 32 devices: a whole 2x2x4 slice. The times are simulated.
32 devices in a mesh: ctx: 16 (over z, y, x), head: 2 (over core).
Axes of the slice: x: 2, y: 2, z: 4, core: 2. Of those that a mesh axis runs over, the one named last changes fastest.
Arguments:
- activations: bfloat16 [7168, 4096], P('ctx'), may hold values from -150 to 150
- query_weight: bfloat16 [4096, 2048], P('ctx', 'head'), may hold values from -0.09375 to 0.09375
- keyval_weight: bfloat16 [4096, 2, 2048], P('ctx', None, 'head'), may hold values from -0.09375 to 0.09375
- out_weight: bfloat16 [2048, 4096], P('head', 'ctx'), may hold values from -0.125 to 0.125
- norm_gain: float32 [4096], replicated, may hold values from 0.1 to 1.9
- vocab_weight: bfloat16 [63488, 4096], P(('ctx', 'head')), may hold values from -15 to 15
- mask_positions: int32 [16, 16], P('ctx'), may hold values from 0 to 447, as said below
- mask_count: int32 [16], P('ctx'), may hold values from 1 to 16, as said below
- targets: int32 [16, 16], P('ctx'), may hold values from 0 to 63487
Outputs:
- loss: float32 [16, 16], P('ctx')
Inputs may be any that keep to these rules, and one draw needn't show every extreme that they name: `mask_positions`: the 16 entries of a row are distinct; the first mask_count[c] of row c are the masked positions of block c, the others unused. `mask_count`: some block has all 16 slots used.
All inputs are finite; a program needn't handle non-finite values.
Results may differ from a plain program's by a relative error of at most 0.0098.
Values may be sent and summed in bfloat16 or wider, within the bound.
No kernel may reach another device: no remote copies, remote signals or barrier semaphores. Data moves between devices by JAX's collectives and lax.ppermute only.
A program may use at most 128 MiB of HBM per device.

v0:
```python
import jax
import jax.numpy as jnp
from jax import lax
from jax.sharding import PartitionSpec as P

HDIM = 128


def shards(
    activations,
    query_weight,
    keyval_weight,
    out_weight,
    norm_gain,
    vocab_weight,
    mask_positions,
    mask_count,
    targets,
):
    ctx_count = lax.axis_size("ctx")
    block_len = activations.shape[0]
    slot_count = mask_positions.shape[1]
    total_rows = ctx_count * slot_count
    head_columns = query_weight.shape[1]
    heads_here = head_columns // HDIM
    feature_cols = activations
    keyval = jnp.einsum(
        "td,djc->tjc",
        feature_cols,
        lax.all_gather(keyval_weight, "ctx", axis=0, tiled=True),
        preferred_element_type=jnp.float32,
    ).astype(jnp.bfloat16)
    key_heads = keyval[:, 0].reshape(block_len, heads_here, HDIM)
    value_heads = keyval[:, 1].reshape(block_len, heads_here, HDIM)
    rows_here = jnp.take(activations, mask_positions[0], axis=0)
    feature_cols = rows_here
    own_queries = jnp.dot(
        feature_cols,
        lax.all_gather(query_weight, "ctx", axis=0, tiled=True),
        preferred_element_type=jnp.float32,
    ).astype(jnp.bfloat16)
    queries = lax.all_gather(own_queries, "ctx", axis=0, tiled=True)
    query_heads = queries.reshape(total_rows, heads_here, HDIM)
    scores = jnp.einsum(
        "rhc,thc->hrt", query_heads, key_heads, preferred_element_type=jnp.float32
    ) * HDIM ** (-0.5)
    highest = lax.pmax(jnp.max(scores, axis=2), "ctx")
    exponent = jnp.exp(scores - highest[:, :, None])
    weights = exponent.astype(jnp.bfloat16)
    numerator = jnp.einsum(
        "hrt,thc->rhc", weights, value_heads, preferred_element_type=jnp.float32
    ).reshape(total_rows, head_columns)
    denominator = jnp.sum(exponent, axis=2).T
    numerator, denominator = (
        lax.psum_scatter(numerator, "ctx", scatter_dimension=0, tiled=True),
        lax.psum_scatter(denominator, "ctx", scatter_dimension=0, tiled=True),
    )
    attended = (
        (numerator.reshape(slot_count, heads_here, HDIM) / denominator[:, :, None])
        .reshape(slot_count, head_columns)
        .astype(jnp.bfloat16)
    )
    branch_part = jnp.dot(
        attended,
        lax.all_gather(out_weight, "ctx", axis=1, tiled=True),
        preferred_element_type=jnp.float32,
    )
    wanted = lax.all_gather(targets, "ctx", axis=0, tiled=True)
    branch = lax.psum_scatter(branch_part, "head", scatter_dimension=0, tiled=True)
    meansquare = jnp.mean(branch * branch, axis=1, keepdims=True)
    hidden = (branch * lax.rsqrt(meansquare + 1e-06) * norm_gain).astype(jnp.bfloat16)
    gathered = lax.all_gather(hidden, ("ctx", "head"), axis=0, tiled=True)
    logits = lax.dot_general(
        gathered, vocab_weight, (((1,), (1,)), ((), ())), preferred_element_type=jnp.float32
    )
    vocab_start = lax.axis_index(("ctx", "head")) * vocab_weight.shape[0]
    vocab_ids = vocab_start + jnp.arange(vocab_weight.shape[0], dtype=jnp.int32)
    wanted_rows = wanted.reshape(total_rows)
    largest = lax.pmax(jnp.max(logits, axis=1), ("ctx", "head"))
    expsum = jnp.sum(jnp.exp(logits - largest[:, None]), axis=1)
    picked = jnp.sum(jnp.where(vocab_ids[None, :] == wanted_rows[:, None], logits, 0.0), axis=1)
    expsum, picked = lax.psum((expsum, picked), ("ctx", "head"))
    losses = (largest + jnp.log(expsum) - picked).reshape(ctx_count, slot_count)
    block_losses = lax.dynamic_slice_in_dim(losses, lax.axis_index("ctx"), 1, 0)[0]
    active = jnp.arange(slot_count, dtype=jnp.int32) < mask_count[0]
    return jnp.where(active, block_losses, jnp.zeros_like(block_losses))[None, :]


def solution(mesh):
    in_specs = (
        P("ctx", None),
        P("ctx", "head"),
        P("ctx", None, "head"),
        P("head", "ctx"),
        P(),
        P(("ctx", "head"), None),
        P("ctx", None),
        P("ctx"),
        P("ctx", None),
    )
    out_specs = P("ctx", None)
    return jax.shard_map(shards, mesh=mesh, in_specs=in_specs, out_specs=out_specs, check_vma=False)
```

profile of v0, /device:TPU:0, one launch (start us, length us, event | category | flops | bytes accessed | tf_op | source)
XLA Modules:
  0.0 831.2 jit_solution(3566141470585280756)
XLA Ops:
  7.3 2.6 copy.14
  10.0 3.3 gather_fusion
  13.3 112.4 %all-gather.8.cloned.1.call-done = bf16[4096,1024]{1,0:T(8,128)(2,1)} async-done(((bf16[256,1024]{1,0:T(8,128)(2,1)}), bf16[4096,1024]{1,0:T(8,128)(2,1)}) %all-gather.8.cloned.1.call-update) | async-done | bytes 8388624 | tf_op jit(solution)/shard_map/all_gather | solution.py:39
  125.7 4.6 convolution_convert_fusion
  130.3 44.7 %all_gather.20 = bf16[256,1024]{1,0:T(8,128)(2,1)S(1)} all-gather(bf16[16,1024]{1,0:T(8,128)(2,1)S(1)} %convolution_convert_fusion), channel_id=1, replica_groups=mesh['ctx'=16,'head'=2] {'ctx'}, dimensions={0}, use_global_device_ids=true | all-gather | bytes 557056 | tf_op jit(solution)/shard_map/all_gather | solution.py:42
  175.0 147.0 %all-gather.6.cloned.1.call-done = bf16[4096,2,1024]{2,0,1:T(8,128)(2,1)} async-done(((bf16[256,2,1024]{2,0,1:T(8,128)(2,1)}), bf16[4096,2,1024]{2,0,1:T(8,128)(2,1)}) %all-gather.6.cloned.1.call-update) | async-done | bytes 16777232 | tf_op jit(solution)/shard_map/all_gather | solution.py:30
  322.0 12.6 %fusion.8 = bf16[448,2,1024]{2,0,1:T(8,128)(2,1)S(1)} fusion(bf16[4096,2,1024]{2,0,1:T(8,128)(2,1)} %all-gather.6.cloned.1.call-done, bf16[448,4096]{1,0:T(8,128)(2,1)} %param.9), kind=kOutput, calls=%fused_computation.12 | convolution fusion | flops 7517110272 | bytes 22282240 | tf_op jit(solution)/shard_map/td,djc->tjc/dot_general | solution.py:27
  334.9 2.4 multiply_reduce_fusion
  337.4 39.4 %pmax.14 = f32[8,256]{1,0:T(8,128)S(1)} all-reduce(f32[8,256]{1,0:T(8,128)S(1)} %get-tuple-element.11), channel_id=1, replica_groups=mesh['ctx'=16,'head'=2] {'ctx'}, use_global_device_ids=true, to_apply=%region_1.2 | all-reduce | flops 2048 | bytes 16384 | tf_op jit(solution)/shard_map/pmax | solution.py:47
  376.9 2.7 fusion.2
  380.5 2.9 fusion.4
  383.4 1.4 copy.18
  385.4 66.8 %reduce-scatter.12.cloned.1.call-done = f32[16,8]{1,0:T(8,128)} async-done(((f32[256,8]{1,0:T(8,128)}), f32[16,8]{1,0:T(8,128)}) %reduce-scatter.12.cloned.1.call-update) | async-done | bytes 528
  453.0 75.5 %reduce-scatter.10.cloned.1.call-done = f32[16,1024]{1,0:T(8,128)} async-done(((f32[256,1024]{1,0:T(8,128)}), f32[16,1024]{1,0:T(8,128)}) %reduce-scatter.10.cloned.1.call-update) | async-done | bytes 65552
  529.6 133.2 %all-gather.10.cloned.1.call-done = bf16[1024,4096]{1,0:T(8,128)(2,1)} async-done(((bf16[1024,256]{1,0:T(8,128)(2,1)}), bf16[1024,4096]{1,0:T(8,128)(2,1)}) %all-gather.10.cloned.1.call-update) | async-done | bytes 8388624 | tf_op jit(solution)/shard_map/all_gather | solution.py:65
  662.8 5.3 fusion.24
  668.2 6.0 reduce-scatter.8.cloned.1.call-done
  674.2 1.0 multiply_reduce_fusion.1
  675.2 1.6 multiply_convert_fusion
  676.9 40.8 %all-gather = s32[16,1,16]{2,1,0:T(1,128)S(1)} all-gather(s32[1,1,16]{2,1,0:T(1,128)S(1)} %bitcast.53), channel_id=1, replica_groups=mesh['ctx'=16,'head'=2] {'ctx'}, dimensions={0}, use_global_device_ids=true | all-gather | bytes 1088 | tf_op jit(solution)/shard_map/all_gather | solution.py:68
  719.6 15.4 %all-gather.12.cloned.1.call-done = bf16[256,4096]{1,0:T(8,128)(2,1)} async-done(((bf16[8,4096]{1,0:T(8,128)(2,1)}), bf16[256,4096]{1,0:T(8,128)(2,1)}) %all-gather.12.cloned.1.call-update) | async-done | bytes 2097168 | tf_op jit(solution)/shard_map/all_gather | solution.py:72
  735.0 8.6 %fusion.23 = (f32[256]{0:T(256)S(1)}, f32[256,1984]{0,1:T(8,128)S(1)}) fusion(bf16[256,4096]{1,0:T(8,128)(2,1)} %all-gather.12.cloned.1.call-done, bf16[1984,4096]{1,0:T(8,128)(2,1)} %param.14), kind=kOutput, calls=%fused_computation.39 | convolution fusion | flops 4161257216 | bytes 20382720 | tf_op jit(solution)/shard_map/dot_general | solution.py:73
  743.6 38.7 %pmax.15 = f32[256]{0:T(256)S(1)} all-reduce(f32[256]{0:T(256)S(1)} %get-tuple-element.13), channel_id=1, replica_groups=mesh['ctx'=16,'head'=2] {'ctx','head'}, use_global_device_ids=true, to_apply=%region_8.9 | all-reduce | flops 256 | bytes 2048 | tf_op jit(solution)/shard_map/pmax | solution.py:79
  783.2 40.5 %all-reduce = (f32[256]{0:T(256)S(1)}, f32[256]{0:T(256)S(1)}) all-reduce(f32[256]{0:T(256)S(1)} %get-tuple-element.6, f32[256]{0:T(256)S(1)} %get-tuple-element.5), channel_id=1, replica_groups=mesh['ctx'=16,'head'=2] {'ctx','head'}, use_global_device_ids=true, to_apply=%region_12.13 | all-reduce | flops 512 | bytes 4096 | tf_op jit(solution)/shard_map/psum | solution.py:82
  (39 shorter events, 7.7 us)
Async XLA Ops:
  6.5 3.4 copy-start.2
  6.5 119.2 %all-gather.8.cloned.1.call-start = ((), (), s32[]{:S(2)}) async-start(), calls=%async_computation.4 | async-start | bytes 8912896 | tf_op jit(solution)/shard_map/all_gather | solution.py:39
  7.3 314.7 %all-gather.6.cloned.1.call-start = ((), (), s32[]{:S(2)}) async-start(), calls=%async_computation.3 | async-start | bytes 17825792 | tf_op jit(solution)/shard_map/all_gather | solution.py:30
  9.9 442.4 %reduce-scatter.12.cloned.1.call-start = ((), (), s32[]{:S(2)}) async-start(), calls=%async_computation.9 | async-start | bytes 139264
  380.4 148.1 %reduce-scatter.10.cloned.1.call-start = ((), (), s32[]{:S(2)}) async-start(), calls=%async_computation.8 | async-start | bytes 1114112
  384.8 278.0 %all-gather.10.cloned.1.call-start = ((), (), s32[]{:S(2)}) async-start(), calls=%async_computation.5 | async-start | bytes 8912896 | tf_op jit(solution)/shard_map/all_gather | solution.py:65
  385.4 288.8 %reduce-scatter.8.cloned.1.call-start = ((), (), s32[]{:S(2)}) async-start(), calls=%async_computation.6 | async-start | bytes 393216 | tf_op jit(solution)/shard_map/reduce_scatter | solution.py:69
  529.6 145.6 %copy-start = (f32[4096]{0:T(1024)S(1)}, f32[4096]{0:T(1024)}, u32[]{:S(2)}) copy-start(f32[4096]{0:T(1024)} %param.13) | copy-start | bytes 49156
  529.6 147.3 %copy-start.1 = (s32[1,16]{1,0:T(1,128)S(1)}, s32[1,16]{1,0:T(1,128)}, u32[]{:S(2)}) copy-start(s32[1,16]{1,0:T(1,128)} %param.17) | copy-start | bytes 196
  668.2 66.9 %all-gather.12.cloned.1.call-start = ((), (), s32[]{:S(2)}) async-start(), calls=%async_computation.7 | async-start | bytes 2162688 | tf_op jit(solution)/shard_map/all_gather | solution.py:72
Sparse Core Ops, SparseCore 0:
  10.1 115.5 all-gather.7
  128.5 193.4 all-gather.5
  380.5 71.6 reduce-scatter.11
  454.5 74.0 reduce-scatter.9
  531.1 131.7 all-gather.9
  668.3 5.8 reduce-scatter.7
  677.4 57.5 all-gather.11
where the time goes:
time: 832 us; the launch traced here: 831 us
  waiting for transfers between devices  558 us (67%)
  blocking collectives  204 us (25%)
  matrix products  36.4 us (4%)
  between operations  14.3 us (2%)
  local copies, waits for them, and re-layouts  11.1 us (1%)
    all_gather x1, waiting for transfers between devices, shards(): lax.all_gather(keyval_weight, 'ctx', axis=0, tiled=True)  147 us
    unnamed x9, waiting for transfers between devices  144 us
    all_gather x1, waiting for transfers between devices, shards(): lax.all_gather(out_weight, 'ctx', axis=1, tiled=True)  133 us
    all_gather x1, waiting for transfers between devices, shards(): lax.all_gather(query_weight, 'ctx', axis=0, tiled=True)  112 us
    all_gather x1, blocking collectives, shards(): queries = lax.all_gather(own_queries, 'ctx', axis=0, tiled=True)  44.7 us
    all_gather x1, blocking collectives, shards(): wanted = lax.all_gather(targets, 'ctx', axis=0, tiled=True)  40.8 us
    psum x1, blocking collectives, shards(): expsum, picked = lax.psum((expsum, picked), ('ctx', 'head'))  40.5 us
    pmax x1, blocking collectives, shards(): highest = lax.pmax(jnp.max(scores, axis=2), 'ctx')  39.4 us
  transfers between devices with their start and end apart: 7, of which 7 were waited for; matrix products, arithmetic and copies ran while one was open for 2% of the time, Pallas kernels for 0%

commit v1 on v0

v1 whole, which is shorter than its diff:
```python
import jax
import jax.numpy as jnp
from jax import lax
from jax.sharding import PartitionSpec as P

HDIM = 128


def _bits(n):
    b = n.bit_length() - 1
    assert 1 << b == n
    return b


def _swap(x, axis, n, k):
    return lax.ppermute(x, axis, [(j, j ^ k) for j in range(n)])


def _all_reduce(x, axis, n, combine):
    k = 1
    while k < n:
        x = combine(x, _swap(x, axis, n, k))
        k *= 2
    return x


def _reduce_scatter(x, axis, n, combine):
    nb = _bits(n)
    idx = lax.axis_index(axis)
    rest = x.shape[1:]
    x = x.reshape((2,) * nb + rest)
    for p in range(nb):
        pos = nb - 1 - p
        bit = (idx // (1 << p)) % 2
        keep = lax.dynamic_index_in_dim(x, bit, pos, keepdims=False)
        send = lax.dynamic_index_in_dim(x, 1 - bit, pos, keepdims=False)
        x = combine(keep, _swap(send, axis, n, 1 << p))
    return x


def _all_gather(x, axis, n):
    nb = _bits(n)
    idx = lax.axis_index(axis)
    rest = x.shape
    for r, p in enumerate(reversed(range(nb))):
        y = _swap(x, axis, n, 1 << p)
        bit = (idx // (1 << p)) % 2
        x = jnp.where(bit == 0, jnp.stack([x, y], axis=r), jnp.stack([y, x], axis=r))
    return x.reshape((n,) + rest)


def _add(a, b):
    return a + b


def shards(
    activations,
    query_weight,
    keyval_weight,
    out_weight,
    norm_gain,
    vocab_weight,
    mask_positions,
    mask_count,
    targets,
):
    n_ctx = lax.axis_size("ctx")
    n_head = lax.axis_size("head")
    block_len = activations.shape[0]
    width = activations.shape[1]
    slot_count = mask_positions.shape[1]
    total_rows = n_ctx * slot_count
    head_columns = query_weight.shape[1]
    heads_here = head_columns // HDIM
    in_rows = query_weight.shape[0]
    col_block = out_weight.shape[1]

    kv_weight = lax.all_gather(keyval_weight, "ctx", axis=0, tiled=True)

    rows_here = jnp.take(activations, mask_positions[0], axis=0)
    row_blocks = lax.all_to_all(rows_here, "ctx", 1, 0, tiled=True)
    partial_q = jnp.dot(row_blocks, query_weight, preferred_element_type=jnp.float32)
    own_q = _reduce_scatter(
        partial_q.reshape(n_ctx, slot_count, head_columns), "ctx", n_ctx, _add
    ).astype(jnp.bfloat16)
    queries = _all_gather(own_q, "ctx", n_ctx).reshape(total_rows, head_columns)

    wanted = _all_gather(targets[0], "ctx", n_ctx).reshape(total_rows)
    out_full = _all_gather(out_weight, "head", n_head).reshape(n_head * head_columns, col_block)

    keyval = jnp.einsum(
        "td,djc->tjc", activations, kv_weight, preferred_element_type=jnp.float32
    ).astype(jnp.bfloat16)
    key_heads = keyval[:, 0].reshape(block_len, heads_here, HDIM)
    value_heads = keyval[:, 1].reshape(block_len, heads_here, HDIM)
    query_heads = queries.reshape(total_rows, heads_here, HDIM)
    scores = jnp.einsum(
        "rhc,thc->hrt", query_heads, key_heads, preferred_element_type=jnp.float32
    ) * HDIM ** (-0.5)
    local_top = jnp.max(scores, axis=2)
    exponent = jnp.exp(scores - local_top[:, :, None])
    weights = exponent.astype(jnp.bfloat16)
    numerator = jnp.einsum(
        "hrt,thc->rhc", weights, value_heads, preferred_element_type=jnp.float32
    ).reshape(total_rows, head_columns)
    denominator = jnp.sum(exponent, axis=2).T
    packed = jnp.concatenate([numerator, local_top.T, denominator], axis=1)

    def att_combine(a, b):
        na, ma, da = jnp.split(a, [head_columns, head_columns + heads_here], axis=-1)
        nb_, mb, db = jnp.split(b, [head_columns, head_columns + heads_here], axis=-1)
        top = jnp.maximum(ma, mb)
        sa = jnp.exp(ma - top)
        sb = jnp.exp(mb - top)
        lead = na.shape[:-1]
        num = (
            na.reshape(lead + (heads_here, HDIM)) * sa[..., None]
            + nb_.reshape(lead + (heads_here, HDIM)) * sb[..., None]
        ).reshape(lead + (head_columns,))
        return jnp.concatenate([num, top, da * sa + db * sb], axis=-1)

    combined = _reduce_scatter(
        packed.reshape(n_ctx, slot_count, packed.shape[1]), "ctx", n_ctx, att_combine
    )
    num = combined[:, :head_columns].reshape(slot_count, heads_here, HDIM)
    den = combined[:, head_columns + heads_here :]
    attended = (num / den[:, :, None]).reshape(slot_count, head_columns).astype(jnp.bfloat16)
    attended = _all_gather(attended, "ctx", n_ctx).reshape(total_rows, head_columns)
    attended = _all_gather(attended, "head", n_head)
    attended = attended.transpose(1, 0, 2).reshape(total_rows, n_head * head_columns)

    share = total_rows // n_head
    head_idx = lax.axis_index("head")
    my_rows = lax.dynamic_slice_in_dim(attended, head_idx * share, share, 0)
    branch = jnp.dot(my_rows, out_full, preferred_element_type=jnp.float32)
    sumsq = _all_reduce(jnp.sum(branch * branch, axis=1), "ctx", n_ctx, _add)
    gain = lax.dynamic_slice_in_dim(norm_gain, lax.axis_index("ctx") * col_block, col_block, 0)
    hidden = (
        branch * lax.rsqrt(sumsq / width + 1e-06)[:, None] * gain
    ).astype(jnp.bfloat16)
    hidden = _all_gather(hidden, "ctx", n_ctx).transpose(1, 0, 2).reshape(share, width)
    hidden = _all_gather(hidden, "head", n_head).reshape(total_rows, width)

    logits = lax.dot_general(
        hidden, vocab_weight, (((1,), (1,)), ((), ())), preferred_element_type=jnp.float32
    )
    vocab_start = lax.axis_index(("ctx", "head")) * vocab_weight.shape[0]
    vocab_ids = vocab_start + jnp.arange(vocab_weight.shape[0], dtype=jnp.int32)
    local_max = jnp.max(logits, axis=1)
    expsum = jnp.sum(jnp.exp(logits - local_max[:, None]), axis=1)
    picked = jnp.sum(jnp.where(vocab_ids[None, :] == wanted[:, None], logits, 0.0), axis=1)
    stats = jnp.stack([local_max, expsum, picked])

    def lse_combine(a, b):
        top = jnp.maximum(a[0], b[0])
        total = a[1] * jnp.exp(a[0] - top) + b[1] * jnp.exp(b[0] - top)
        return jnp.stack([top, total, a[2] + b[2]])

    stats = _all_reduce(stats, "head", n_head, lse_combine)
    stats = _all_reduce(stats, "ctx", n_ctx, lse_combine)
    losses = (stats[0] + jnp.log(stats[1]) - stats[2]).reshape(n_ctx, slot_count)
    block_losses = lax.dynamic_slice_in_dim(losses, lax.axis_index("ctx"), 1, 0)[0]
    active = jnp.arange(slot_count, dtype=jnp.int32) < mask_count[0]
    return jnp.where(active, block_losses, jnp.zeros_like(block_losses))[None, :]


def solution(mesh):
    in_specs = (
        P("ctx", None),
        P("ctx", "head"),
        P("ctx", None, "head"),
        P("head", "ctx"),
        P(),
        P(("ctx", "head"), None),
        P("ctx", None),
        P("ctx"),
        P("ctx", None),
    )
    out_specs = P("ctx", None)
    return jax.shard_map(shards, mesh=mesh, in_specs=in_specs, out_specs=out_specs, check_vma=False)
```

time: 832 us -> 392 us (0.47)
  waiting for transfers between devices: 558 us -> 279 us
  blocking collectives: 204 us -> 0 us
  starting transfers between devices: 0.25 us -> 43.7 us
  matrix products: 36.4 us -> 26.5 us
  local copies, waits for them, and re-layouts: 11.1 us -> 19.5 us
    all_gather x4 -> x1, waiting for transfers between devices: 408 us -> 116 us  [shards(): kv_weight = lax.all_gather(keyval_weight, 'ctx', axis=0, tiled=True)]
    ppermute x0 -> x36, waiting for transfers between devices: none -> 154 us  [_swap(): return lax.ppermute(x, axis, [(j, j ^ k) for j in range(n)])]
    unnamed x9 -> x1, waiting for transfers between devices: 144 us -> 0.02 us
    all_gather x2 -> x0, blocking collectives: 85.5 us -> none  [the longest x1 44.7 us: shards(): queries = lax.all_gather(own_queries, 'ctx', axis=0, tiled=True)]
    pmax x2 -> x0, blocking collectives: 78.1 us -> none  [the longest x1 39.4 us: shards(): highest = lax.pmax(jnp.max(scores, axis=2), 'ctx')]
    psum x1 -> x0, blocking collectives: 40.5 us -> none  [shards(): expsum, picked = lax.psum((expsum, picked), ('ctx', 'head'))]
    ppermute x0 -> x36, starting transfers between devices: none -> 35.3 us  [_swap(): return lax.ppermute(x, axis, [(j, j ^ k) for j in range(n)])]
    all_to_all x0 -> x1, waiting for transfers between devices: none -> 9.43 us  [shards(): row_blocks = lax.all_to_all(rows_here, 'ctx', 1, 0, tiled=True)]
  transfers between devices with their start and end apart: 7 -> 38, of which waited for: 7 -> 36; matrix products, arithmetic and copies ran while one was open for 2% -> 2% of each run, Pallas kernels for 0% -> 0%
where the time goes in v1:
time: 392 us
  waiting for transfers between devices  279 us (71%)
  starting transfers between devices  43.7 us (11%)
  matrix products  26.5 us (7%)
  local copies, waits for them, and re-layouts  19.5 us (5%)
  between operations  14.8 us (4%)
  other arithmetic  8.61 us (2%)
    ppermute x36, waiting for transfers between devices, _swap(): return lax.ppermute(x, axis, [(j, j ^ k) for j in range(n)])  154 us
    all_gather x1, waiting for transfers between devices, shards(): kv_weight = lax.all_gather(keyval_weight, 'ctx', axis=0, tiled=True)  116 us
    ppermute x36, starting transfers between devices, _swap(): return lax.ppermute(x, axis, [(j, j ^ k) for j in range(n)])  35.3 us
    dot_general x1, matrix products, shards(): jnp.einsum('td,djc->tjc', activations, kv_weight, preferred_element_type=...  12.5 us
    all_to_all x1, waiting for transfers between devices, shards(): row_blocks = lax.all_to_all(rows_here, 'ctx', 1, 0, tiled=True)  9.43 us
    dot_general x1, matrix products, shards(): lax.dot_general(hidden, vocab_weight, (((1,), (1,)), ((), ())), preferred...  8.62 us
    all_to_all x1, starting transfers between devices, shards(): row_blocks = lax.all_to_all(rows_here, 'ctx', 1, 0, tiled=True)  8.31 us
  transfers between devices with their start and end apart: 38, of which 36 were waited for; matrix products, arithmetic and copies ran while one was open for 2% of the time, Pallas kernels for 0%

profile of v1, /device:TPU:0, one launch (start us, length us, event | category | flops | bytes accessed | tf_op | source)
XLA Modules:
  0.0 392.0 jit_solution(965090385289847711)
XLA Ops:
  13.8 8.3 %all-to-all-start = ((bf16[16,16,256]{2,0,1:T(8,128)(2,1)}), bf16[16,16,256]{2,0,1:T(8,128)(2,1)S(1)}, u32[]{:S(2)}, u32[]{:S(2)}) async-start(bf16[16,16,256]{2,0,1:T(8,128)(2,1)} %bitcast_select_fusion), calls=%async_computation | async-start | bytes 262144 | tf_op jit(solution)/shard_map/all_to_all | solution.py:81
  22.1 9.4 %all-to-all-done = bf16[16,16,256]{2,0,1:T(8,128)(2,1)S(1)} async-done(((bf16[16,16,256]{2,0,1:T(8,128)(2,1)}), bf16[16,16,256]{2,0,1:T(8,128)(2,1)S(1)}, u32[]{:S(2)}, u32[]{:S(2)}) %all-to-all-start) | async-done | bytes 131104 | tf_op jit(solution)/shard_map/all_to_all | solution.py:81
  33.2 11.3 %collective-permute-done = f32[2,2,2,16,1024]{4,3,2,1,0:T(8,128)S(1)} collective-permute-done((f32[2,2,2,16,1024]{4,3,2,1,0:T(8,128)S(1)}, f32[2,2,2,16,1024]{4,3,2,1,0:T(8,128)S(1)}, u32[]{:S(2)}, u32[]{:S(2)}) %collective-permute-start) | collective-permute-done | bytes 524320 | tf_op jit(solution)/shard_map/ppermute | solution.py:16
  46.2 4.9 %collective-permute-done.1 = f32[2,2,16,1024]{3,2,1,0:T(8,128)S(1)} collective-permute-done((f32[2,2,16,1024]{3,2,1,0:T(8,128)S(1)}, f32[2,2,16,1024]{3,2,1,0:T(8,128)S(1)}, u32[]{:S(2)}, u32[]{:S(2)}) %collective-permute-start.1) | collective-permute-done | bytes 262176 | tf_op jit(solution)/shard_map/ppermute | solution.py:16
  56.2 3.8 collective-permute-start.3
  60.0 6.7 %collective-permute-done.3 = f32[16,1024]{1,0:T(8,128)S(1)} collective-permute-done((f32[16,1024]{1,0:T(8,128)S(1)}, f32[16,1024]{1,0:T(8,128)S(1)}, u32[]{:S(2)}, u32[]{:S(2)}) %collective-permute-start.3) | collective-permute-done | bytes 65568 | tf_op jit(solution)/shard_map/ppermute | solution.py:16
  66.9 7.3 %collective-permute-done.4 = bf16[16,1024]{1,0:T(8,128)(2,1)S(1)} collective-permute-done((bf16[16,1024]{1,0:T(8,128)(2,1)S(1)}, bf16[16,1024]{1,0:T(8,128)(2,1)S(1)}, u32[]{:S(2)}, u32[]{:S(2)}) %collective-permute-start.4) | collective-permute-done | bytes 32800 | tf_op jit(solution)/shard_map/ppermute | solution.py:16
  74.9 7.7 %collective-permute-done.5 = bf16[2,16,1024]{2,1,0:T(8,128)(2,1)S(1)} collective-permute-done((bf16[2,16,1024]{2,1,0:T(8,128)(2,1)S(1)}, bf16[2,16,1024]{2,1,0:T(8,128)(2,1)S(1)}, u32[]{:S(2)}, u32[]{:S(2)}) %collective-permute-start.5) | collective-permute-done | bytes 65568 | tf_op jit(solution)/shard_map/ppermute | solution.py:16
  88.1 6.0 %collective-permute-done.7 = bf16[2,2,2,16,1024]{4,3,0,1,2:T(8,128)(2,1)S(1)} collective-permute-done((bf16[2,2,2,16,1024]{4,3,0,1,2:T(8,128)(2,1)S(1)}, bf16[2,2,2,16,1024]{4,3,0,1,2:T(8,128)(2,1)S(1)}, u32[]{:S(2)}, u32[]{:S(2)}) %collective-permute-start.7) | collective-permute-done | bytes 262176 | tf_op jit(solution)/shard_map/ppermute | solution.py:16
  94.4 115.7 %all-gather.2.cloned.1.call-done = bf16[4096,2,1024]{2,0,1:T(8,128)(2,1)} async-done(((bf16[256,2,1024]{2,0,1:T(8,128)(2,1)}), bf16[4096,2,1024]{2,0,1:T(8,128)(2,1)}) %all-gather.2.cloned.1.call-update) | async-done | bytes 16777232 | tf_op jit(solution)/shard_map/all_gather | solution.py:78
  210.0 12.5 %fusion.8 = bf16[448,2,1024]{2,0,1:T(8,128)(2,1)S(1)} fusion(bf16[4096,2,1024]{2,0,1:T(8,128)(2,1)} %all-gather.2.cloned.1.call-done, bf16[448,4096]{1,0:T(8,128)(2,1)} %param.9), kind=kOutput, calls=%fused_computation.13 | convolution fusion | flops 7517110272 | bytes 22282240 | tf_op jit(solution)/shard_map/td,djc->tjc/dot_general | solution.py:91
  231.6 13.6 %collective-permute-done.8 = f32[2,2,2,16,1040]{4,3,2,1,0:T(8,128)S(1)} collective-permute-done((f32[2,2,2,16,1040]{4,3,2,1,0:T(8,128)S(1)}, f32[2,2,2,16,1040]{4,3,2,1,0:T(8,128)S(1)}, u32[]{:S(2)}, u32[]{:S(2)}) %collective-permute-start.8) | collective-permute-done | bytes 532512 | tf_op jit(solution)/shard_map/ppermute | solution.py:16
  247.6 5.9 %collective-permute-done.9 = f32[2,2,16,1040]{3,2,1,0:T(8,128)S(1)} collective-permute-done((f32[2,2,16,1040]{3,2,1,0:T(8,128)S(1)}, f32[2,2,16,1040]{3,2,1,0:T(8,128)S(1)}, u32[]{:S(2)}, u32[]{:S(2)}) %collective-permute-start.9) | collective-permute-done | bytes 266272 | tf_op jit(solution)/shard_map/ppermute | solution.py:16
  254.3 5.1 %collective-permute-done.10 = f32[2,16,1040]{2,1,0:T(8,128)S(1)} collective-permute-done((f32[2,16,1040]{2,1,0:T(8,128)S(1)}, f32[2,16,1040]{2,1,0:T(8,128)S(1)}, u32[]{:S(2)}, u32[]{:S(2)}) %collective-permute-start.10) | collective-permute-done | bytes 133152 | tf_op jit(solution)/shard_map/ppermute | solution.py:16
  261.5 5.1 %collective-permute-done.11 = f32[16,1040]{1,0:T(8,128)S(1)} collective-permute-done((f32[16,1040]{1,0:T(8,128)S(1)}, f32[16,1040]{1,0:T(8,128)S(1)}, u32[]{:S(2)}, u32[]{:S(2)}) %collective-permute-start.11) | collective-permute-done | bytes 66592 | tf_op jit(solution)/shard_map/ppermute | solution.py:16
  267.2 4.6 %collective-permute-done.12 = bf16[16,1024]{1,0:T(8,128)(2,1)S(1)} collective-permute-done((bf16[16,1024]{1,0:T(8,128)(2,1)S(1)}, bf16[16,1024]{1,0:T(8,128)(2,1)S(1)}, u32[]{:S(2)}, u32[]{:S(2)}) %collective-permute-start.12) | collective-permute-done | bytes 32800 | tf_op jit(solution)/shard_map/ppermute | solution.py:16
  272.1 4.0 %collective-permute-done.13 = bf16[2,16,1024]{2,1,0:T(8,128)(2,1)S(1)} collective-permute-done((bf16[2,16,1024]{2,1,0:T(8,128)(2,1)S(1)}, bf16[2,16,1024]{2,1,0:T(8,128)(2,1)S(1)}, u32[]{:S(2)}, u32[]{:S(2)}) %collective-permute-start.13) | collective-permute-done | bytes 65568 | tf_op jit(solution)/shard_map/ppermute | solution.py:16
  282.5 5.2 %collective-permute-done.15 = bf16[2,2,2,16,1024]{4,3,2,1,0:T(8,128)(2,1)S(1)} collective-permute-done((bf16[2,2,2,16,1024]{4,3,2,1,0:T(8,128)(2,1)S(1)}, bf16[2,2,2,16,1024]{4,3,2,1,0:T(8,128)(2,1)S(1)}, u32[]{:S(2)}, u32[]{:S(2)}) %collective-permute-start.15) | collective-permute-done | bytes 262176 | tf_op jit(solution)/shard_map/ppermute | solution.py:16
  309.2 4.5 %collective-permute-done.22 = bf16[128,256]{1,0:T(8,128)(2,1)S(1)} collective-permute-done((bf16[128,256]{1,0:T(8,128)(2,1)S(1)}, bf16[128,256]{1,0:T(8,128)(2,1)S(1)}, u32[]{:S(2)}, u32[]{:S(2)}) %collective-permute-start.22) | collective-permute-done | bytes 65568 | tf_op jit(solution)/shard_map/ppermute | solution.py:16
  314.2 4.5 %collective-permute-done.23 = bf16[2,128,256]{2,1,0:T(8,128)(2,1)S(1)} collective-permute-done((bf16[2,128,256]{2,1,0:T(8,128)(2,1)S(1)}, bf16[2,128,256]{2,1,0:T(8,128)(2,1)S(1)}, u32[]{:S(2)}, u32[]{:S(2)}) %collective-permute-start.23) | collective-permute-done | bytes 131104 | tf_op jit(solution)/shard_map/ppermute | solution.py:16
  320.3 4.8 %collective-permute-done.24 = bf16[2,2,128,256]{3,2,0,1:T(8,128)(2,1)S(1)} collective-permute-done((bf16[2,2,128,256]{3,2,0,1:T(8,128)(2,1)S(1)}, bf16[2,2,128,256]{3,2,0,1:T(8,128)(2,1)S(1)}, u32[]{:S(2)}, u32[]{:S(2)}) %collective-permute-start.24) | collective-permute-done | bytes 262176 | tf_op jit(solution)/shard_map/ppermute | solution.py:16
  326.6 7.9 %collective-permute-done.25 = bf16[2,2,2,128,256]{4,3,0,1,2:T(8,128)(2,1)S(1)} collective-permute-done((bf16[2,2,2,128,256]{4,3,0,1,2:T(8,128)(2,1)S(1)}, bf16[2,2,2,128,256]{4,3,0,1,2:T(8,128)(2,1)S(1)}, u32[]{:S(2)}, u32[]{:S(2)}) %collective-permute-start.25) | collective-permute-done | bytes 524320 | tf_op jit(solution)/shard_map/ppermute | solution.py:16
  336.3 3.7 collective-permute-done.27
  357.5 8.6 %fusion.55 = (f32[256]{0:T(256)S(1)}, f32[256,1984]{0,1:T(8,128)S(1)}) fusion(bf16[256,4096]{1,0:T(8,128)(2,1)} %bitcast.203, bf16[1984,4096]{1,0:T(8,128)(2,1)} %param.14), kind=kOutput, calls=%fused_computation.192 | convolution fusion | flops 4161257216 | bytes 20382720 | tf_op jit(solution)/shard_map/dot_general | solution.py:144
  (221 shorter events, 106.1 us)
Async XLA Ops:
  6.5 203.5 %all-gather.2.cloned.1.call-start = ((), (), s32[]{:S(2)}) async-start(), calls=%async_computation.1 | async-start | bytes 17825792 | tf_op jit(solution)/shard_map/all_gather | solution.py:78
  13.8 17.8 %all-to-all-start = ((bf16[16,16,256]{2,0,1:T(8,128)(2,1)}), bf16[16,16,256]{2,0,1:T(8,128)(2,1)S(1)}, u32[]{:S(2)}, u32[]{:S(2)}) async-start(bf16[16,16,256]{2,0,1:T(8,128)(2,1)} %bitcast_select_fusion), calls=%async_computation | async-start | bytes 262144 | tf_op jit(solution)/shard_map/all_to_all | solution.py:81
  31.9 12.6 %collective-permute-start = (f32[2,2,2,16,1024]{4,3,2,1,0:T(8,128)S(1)}, f32[2,2,2,16,1024]{4,3,2,1,0:T(8,128)S(1)}, u32[]{:S(2)}, u32[]{:S(2)}) collective-permute-start(f32[2,2,2,16,1024]{4,3,2,1,0:T(8,128)S(1)} %dynamic-slice_bitcast_fusion.2), channel_id=1, source_target_pairs={{0,2},{2,0},{4,6},{6,4},{8,10},{10,8},{12,14},{14,12},{16,18},{18,... | collective-permute-start | bytes 1572872 | tf_op jit(solution)/shard_map/ppermute | solution.py:16
  44.6 6.4 %collective-permute-start.1 = (f32[2,2,16,1024]{3,2,1,0:T(8,128)S(1)}, f32[2,2,16,1024]{3,2,1,0:T(8,128)S(1)}, u32[]{:S(2)}, u32[]{:S(2)}) collective-permute-start(f32[2,2,16,1024]{3,2,1,0:T(8,128)S(1)} %dynamic-slice_bitcast_fusion.5), channel_id=1, source_target_pairs={{0,4},{2,6},{4,0},{6,2},{8,12},{10,14},{12,8},{14,10},{16,20},{18,... | collective-permute-start | bytes 786440 | tf_op jit(solution)/shard_map/ppermute | solution.py:16
  51.1 5.0 %collective-permute-start.2 = (f32[2,16,1024]{2,1,0:T(8,128)S(1)}, f32[2,16,1024]{2,1,0:T(8,128)S(1)}, u32[]{:S(2)}, u32[]{:S(2)}) collective-permute-start(f32[2,16,1024]{2,1,0:T(8,128)S(1)} %dynamic-slice_bitcast_fusion.8), channel_id=1, source_target_pairs={{0,8},{2,10},{4,12},{6,14},{8,0},{10,2},{12,4},{14,6},{16,24},{18,... | collective-permute-start | bytes 393224 | tf_op jit(solution)/shard_map/ppermute | solution.py:16
  56.2 10.4 %collective-permute-start.3 = (f32[16,1024]{1,0:T(8,128)S(1)}, f32[16,1024]{1,0:T(8,128)S(1)}, u32[]{:S(2)}, u32[]{:S(2)}) collective-permute-start(f32[16,1024]{1,0:T(8,128)S(1)} %dynamic-slice_bitcast_fusion.11), channel_id=1, source_target_pairs={{0,16},{2,18},{4,20},{6,22},{8,24},{10,26},{12,28},{14,30},{16,0},... | collective-permute-start | bytes 196616 | tf_op jit(solution)/shard_map/ppermute | solution.py:16
  66.6 7.6 %collective-permute-start.4 = (bf16[16,1024]{1,0:T(8,128)(2,1)S(1)}, bf16[16,1024]{1,0:T(8,128)(2,1)S(1)}, u32[]{:S(2)}, u32[]{:S(2)}) collective-permute-start(bf16[16,1024]{1,0:T(8,128)(2,1)S(1)} %fusion.29), channel_id=1, source_target_pairs={{0,16},{2,18},{4,20},{6,22},{8,24},{10,26},{12,28},{14,30},{16,0},... | collective-permute-start | bytes 98312 | tf_op jit(solution)/shard_map/ppermute | solution.py:16
  74.3 8.3 %collective-permute-start.5 = (bf16[2,16,1024]{2,1,0:T(8,128)(2,1)S(1)}, bf16[2,16,1024]{2,1,0:T(8,128)(2,1)S(1)}, u32[]{:S(2)}, u32[]{:S(2)}) collective-permute-start(bf16[2,16,1024]{2,1,0:T(8,128)(2,1)S(1)} %maximum_select_fusion.19), channel_id=1, source_target_pairs={{0,8},{2,10},{4,12},{6,14},{8,0},{10,2},{12,4},{14,6},{16,24},{18,... | collective-permute-start | bytes 196616 | tf_op jit(solution)/shard_map/ppermute | solution.py:16
  82.6 5.0 %collective-permute-start.6 = (bf16[2,2,16,1024]{3,2,0,1:T(8,128)(2,1)S(1)}, bf16[2,2,16,1024]{3,2,0,1:T(8,128)(2,1)S(1)}, u32[]{:S(2)}, u32[]{:S(2)}) collective-permute-start(bf16[2,2,16,1024]{3,2,0,1:T(8,128)(2,1)S(1)} %maximum_select_fusion.14), channel_id=1, source_target_pairs={{0,4},{2,6},{4,0},{6,2},{8,12},{10,14},{12,8},{14,10},{16,20},{18,... | collective-permute-start | bytes 393224 | tf_op jit(solution)/shard_map/ppermute | solution.py:16
  87.7 6.4 %collective-permute-start.7 = (bf16[2,2,2,16,1024]{4,3,0,1,2:T(8,128)(2,1)S(1)}, bf16[2,2,2,16,1024]{4,3,0,1,2:T(8,128)(2,1)S(1)}, u32[]{:S(2)}, u32[]{:S(2)}) collective-permute-start(bf16[2,2,2,16,1024]{4,3,0,1,2:T(8,128)(2,1)S(1)} %maximum_select_fusion.9), channel_id=1, source_target_pairs={{0,2},{2,0},{4,6},{6,4},{8,10},{10,8},{12,14},{14,12},{16,18},{18,... | collective-permute-start | bytes 786440 | tf_op jit(solution)/shard_map/ppermute | solution.py:16
  230.4 14.7 %collective-permute-start.8 = (f32[2,2,2,16,1040]{4,3,2,1,0:T(8,128)S(1)}, f32[2,2,2,16,1040]{4,3,2,1,0:T(8,128)S(1)}, u32[]{:S(2)}, u32[]{:S(2)}) collective-permute-start(f32[2,2,2,16,1040]{4,3,2,1,0:T(8,128)S(1)} %get-tuple-element.53), channel_id=1, source_target_pairs={{0,2},{2,0},{4,6},{6,4},{8,10},{10,8},{12,14},{14,12},{16,18},{18,... | collective-permute-start | bytes 1597448 | tf_op jit(solution)/shard_map/ppermute | solution.py:16
  246.1 7.5 %collective-permute-start.9 = (f32[2,2,16,1040]{3,2,1,0:T(8,128)S(1)}, f32[2,2,16,1040]{3,2,1,0:T(8,128)S(1)}, u32[]{:S(2)}, u32[]{:S(2)}) collective-permute-start(f32[2,2,16,1040]{3,2,1,0:T(8,128)S(1)} %get-tuple-element.55), channel_id=1, source_target_pairs={{0,4},{2,6},{4,0},{6,2},{8,12},{10,14},{12,8},{14,10},{16,20},{18,... | collective-permute-start | bytes 798728 | tf_op jit(solution)/shard_map/ppermute | solution.py:16
  254.2 5.2 %collective-permute-start.10 = (f32[2,16,1040]{2,1,0:T(8,128)S(1)}, f32[2,16,1040]{2,1,0:T(8,128)S(1)}, u32[]{:S(2)}, u32[]{:S(2)}) collective-permute-start(f32[2,16,1040]{2,1,0:T(8,128)S(1)} %get-tuple-element.57), channel_id=1, source_target_pairs={{0,8},{2,10},{4,12},{6,14},{8,0},{10,2},{12,4},{14,6},{16,24},{18,... | collective-permute-start | bytes 399368 | tf_op jit(solution)/shard_map/ppermute | solution.py:16
  259.9 6.6 %collective-permute-start.11 = (f32[16,1040]{1,0:T(8,128)S(1)}, f32[16,1040]{1,0:T(8,128)S(1)}, u32[]{:S(2)}, u32[]{:S(2)}) collective-permute-start(f32[16,1040]{1,0:T(8,128)S(1)} %get-tuple-element.61), channel_id=1, source_target_pairs={{0,16},{2,18},{4,20},{6,22},{8,24},{10,26},{12,28},{14,30},{16,0},... | collective-permute-start | bytes 199688 | tf_op jit(solution)/shard_map/ppermute | solution.py:16
  266.9 4.9 %collective-permute-start.12 = (bf16[16,1024]{1,0:T(8,128)(2,1)S(1)}, bf16[16,1024]{1,0:T(8,128)(2,1)S(1)}, u32[]{:S(2)}, u32[]{:S(2)}) collective-permute-start(bf16[16,1024]{1,0:T(8,128)(2,1)S(1)} %fusion.26), channel_id=1, source_target_pairs={{0,16},{2,18},{4,20},{6,22},{8,24},{10,26},{12,28},{14,30},{16,0},... | collective-permute-start | bytes 98312 | tf_op jit(solution)/shard_map/ppermute | solution.py:16
  267.2 20.6 %collective-permute-start.17 = (bf16[1024,256]{1,0:T(8,128)(2,1)S(1)}, bf16[1024,256]{1,0:T(8,128)(2,1)S(1)}, u32[]{:S(2)}, u32[]{:S(2)}) collective-permute-start(bf16[1024,256]{1,0:T(8,128)(2,1)S(1)} %copy-done.5), channel_id=1, source_target_pairs={{0,1},{1,0},{2,3},{3,2},{4,5},{5,4},{6,7},{7,6},{8,9},{9,8},{10,11... | collective-permute-start | bytes 1572872 | tf_op jit(solution)/shard_map/ppermute | solution.py:16
  276.2 5.0 %collective-permute-start.14 = (bf16[2,2,16,1024]{3,2,1,0:T(8,128)(2,1)S(1)}, bf16[2,2,16,1024]{3,2,1,0:T(8,128)(2,1)S(1)}, u32[]{:S(2)}, u32[]{:S(2)}) collective-permute-start(bf16[2,2,16,1024]{3,2,1,0:T(8,128)(2,1)S(1)} %maximum_select_fusion.15), channel_id=1, source_target_pairs={{0,4},{2,6},{4,0},{6,2},{8,12},{10,14},{12,8},{14,10},{16,20},{18,... | collective-permute-start | bytes 393224 | tf_op jit(solution)/shard_map/ppermute | solution.py:16
  281.2 6.4 %collective-permute-start.15 = (bf16[2,2,2,16,1024]{4,3,2,1,0:T(8,128)(2,1)S(1)}, bf16[2,2,2,16,1024]{4,3,2,1,0:T(8,128)(2,1)S(1)}, u32[]{:S(2)}, u32[]{:S(2)}) collective-permute-start(bf16[2,2,2,16,1024]{4,3,2,1,0:T(8,128)(2,1)S(1)} %maximum_select_fusion.10), channel_id=1, source_target_pairs={{0,2},{2,0},{4,6},{6,4},{8,10},{10,8},{12,14},{14,12},{16,18},{18,... | collective-permute-start | bytes 786440 | tf_op jit(solution)/shard_map/ppermute | solution.py:16
  307.9 5.7 %collective-permute-start.22 = (bf16[128,256]{1,0:T(8,128)(2,1)S(1)}, bf16[128,256]{1,0:T(8,128)(2,1)S(1)}, u32[]{:S(2)}, u32[]{:S(2)}) collective-permute-start(bf16[128,256]{1,0:T(8,128)(2,1)S(1)} %multiply_convert_fusion), channel_id=1, source_target_pairs={{0,16},{2,18},{4,20},{6,22},{8,24},{10,26},{12,28},{14,30},{16,0},... | collective-permute-start | bytes 196616 | tf_op jit(solution)/shard_map/ppermute | solution.py:16
  313.7 5.0 %collective-permute-start.23 = (bf16[2,128,256]{2,1,0:T(8,128)(2,1)S(1)}, bf16[2,128,256]{2,1,0:T(8,128)(2,1)S(1)}, u32[]{:S(2)}, u32[]{:S(2)}) collective-permute-start(bf16[2,128,256]{2,1,0:T(8,128)(2,1)S(1)} %maximum_select_fusion.17), channel_id=1, source_target_pairs={{0,8},{2,10},{4,12},{6,14},{8,0},{10,2},{12,4},{14,6},{16,24},{18,... | collective-permute-start | bytes 393224 | tf_op jit(solution)/shard_map/ppermute | solution.py:16
  318.7 6.4 %collective-permute-start.24 = (bf16[2,2,128,256]{3,2,0,1:T(8,128)(2,1)S(1)}, bf16[2,2,128,256]{3,2,0,1:T(8,128)(2,1)S(1)}, u32[]{:S(2)}, u32[]{:S(2)}) collective-permute-start(bf16[2,2,128,256]{3,2,0,1:T(8,128)(2,1)S(1)} %maximum_select_fusion.12), channel_id=1, source_target_pairs={{0,4},{2,6},{4,0},{6,2},{8,12},{10,14},{12,8},{14,10},{16,20},{18,... | collective-permute-start | bytes 786440 | tf_op jit(solution)/shard_map/ppermute | solution.py:16
  325.2 9.2 %collective-permute-start.25 = (bf16[2,2,2,128,256]{4,3,0,1,2:T(8,128)(2,1)S(1)}, bf16[2,2,2,128,256]{4,3,0,1,2:T(8,128)(2,1)S(1)}, u32[]{:S(2)}, u32[]{:S(2)}) collective-permute-start(bf16[2,2,2,128,256]{4,3,0,1,2:T(8,128)(2,1)S(1)} %maximum_select_fusion.7), channel_id=1, source_target_pairs={{0,2},{2,0},{4,6},{6,4},{8,10},{10,8},{12,14},{14,12},{16,18},{18,... | collective-permute-start | bytes 1572872 | tf_op jit(solution)/shard_map/ppermute | solution.py:16
  335.4 15.7 %collective-permute-start.26 = (bf16[128,4096]{0,1:T(8,128)(2,1)S(1)}, bf16[128,4096]{0,1:T(8,128)(2,1)S(1)}, u32[]{:S(2)}, u32[]{:S(2)}) collective-permute-start(bf16[128,4096]{0,1:T(8,128)(2,1)S(1)} %bitcast.193), channel_id=1, source_target_pairs={{0,1},{1,0},{2,3},{3,2},{4,5},{5,4},{6,7},{7,6},{8,9},{9,8},{10,11... | collective-permute-start | bytes 3145736 | tf_op jit(solution)/shard_map/ppermute | solution.py:16
  379.7 4.6 %collective-permute-start.35 = (f32[3,256]{1,0:T(4,128)S(1)}, f32[3,256]{1,0:T(4,128)S(1)}, u32[]{:S(2)}, u32[]{:S(2)}) collective-permute-start(f32[3,256]{1,0:T(4,128)S(1)} %pad_maximum_fusion.8), channel_id=1, source_target_pairs={{0,16},{2,18},{4,20},{6,22},{8,24},{10,26},{12,28},{14,30},{16,0},... | collective-permute-start | bytes 9224 | tf_op jit(solution)/shard_map/ppermute | solution.py:16
  (22 other events, 156.9 us)
Sparse Core Ops, SparseCore 0:
  10.1 199.8 all-gather.1

commit v2 on v1

--- a/solution.py
+++ b/solution.py
@@ -6,46 +6,68 @@
 HDIM = 128
 
 
-def _bits(n):
+def _digits(n):
     b = n.bit_length() - 1
     assert 1 << b == n
-    return b
+    out, p = [], 0
+    while p < b:
+        r = 4 if b - p >= 2 else 2
+        out.append((p, r))
+        p += r.bit_length() - 1
+    return out
 
 
 def _swap(x, axis, n, k):
     return lax.ppermute(x, axis, [(j, j ^ k) for j in range(n)])
 
 
+def _exchange(x_for, axis, n, p, r, digit):
+    return [None] + [_swap(x_for(s), axis, n, s << p) for s in range(1, r)]
+
+
 def _all_reduce(x, axis, n, combine):
-    k = 1
-    while k < n:
-        x = combine(x, _swap(x, axis, n, k))
-        k *= 2
+    idx = lax.axis_index(axis)
+    for p, r in _digits(n):
+        digit = (idx // (1 << p)) % r
+        got = _exchange(lambda s: x, axis, n, p, r, digit)
+        got[0] = x
+        stacked = jnp.stack(got)
+        acc = lax.dynamic_index_in_dim(stacked, digit, 0, keepdims=False)
+        for a in range(1, r):
+            acc = combine(acc, lax.dynamic_index_in_dim(stacked, a ^ digit, 0, keepdims=False))
+        x = acc
     return x
 
 
 def _reduce_scatter(x, axis, n, combine):
-    nb = _bits(n)
     idx = lax.axis_index(axis)
     rest = x.shape[1:]
-    x = x.reshape((2,) * nb + rest)
-    for p in range(nb):
-        pos = nb - 1 - p
-        bit = (idx // (1 << p)) % 2
-        keep = lax.dynamic_index_in_dim(x, bit, pos, keepdims=False)
-        send = lax.dynamic_index_in_dim(x, 1 - bit, pos, keepdims=False)
-        x = combine(keep, _swap(send, axis, n, 1 << p))
-    return x
+    for p, r in _digits(n):
+        digit = (idx // (1 << p)) % r
+        x = x.reshape((x.shape[0] // r, r) + rest)
+        got = _exchange(
+            lambda s: lax.dynamic_index_in_dim(x, digit ^ s, 1, keepdims=False),
+            axis, n, p, r, digit,
+        )
+        acc = lax.dynamic_index_in_dim(x, digit, 1, keepdims=False)
+        for s in range(1, r):
+            acc = combine(acc, got[s])
+        x = acc
+    return x[0]
 
 
 def _all_gather(x, axis, n):
-    nb = _bits(n)
     idx = lax.axis_index(axis)
     rest = x.shape
-    for r, p in enumerate(reversed(range(nb))):
-        y = _swap(x, axis, n, 1 << p)
-        bit = (idx // (1 << p)) % 2
-        x = jnp.where(bit == 0, jnp.stack([x, y], axis=r), jnp.stack([y, x], axis=r))
+    for k, (p, r) in enumerate(reversed(_digits(n))):
+        digit = (idx // (1 << p)) % r
+        got = _exchange(lambda s: x, axis, n, p, r, digit)
+        got[0] = x
+        stacked = jnp.stack(got)
+        x = jnp.stack(
+            [lax.dynamic_index_in_dim(stacked, a ^ digit, 0, keepdims=False) for a in range(r)],
+            axis=k,
+        )
     return x.reshape((n,) + rest)
 
 

time: 392 us -> 374 us (0.954)
  waiting for transfers between devices: 279 us -> 231 us
  starting transfers between devices: 43.7 us -> 72.5 us
    ppermute x36 -> x52, waiting for transfers between devices: 154 us -> 83.5 us  [_swap(): return lax.ppermute(x, axis, [(j, j ^ k) for j in range(n)])]
    ppermute x36 -> x52, starting transfers between devices: 35.3 us -> 64.2 us  [_swap(): return lax.ppermute(x, axis, [(j, j ^ k) for j in range(n)])]
    all_gather x1, waiting for transfers between devices: 116 us -> 138 us  [shards(): kv_weight = lax.all_gather(keyval_weight, 'ctx', axis=0, tiled=True)]
  transfers between devices with their start and end apart: 38 -> 54, of which waited for: 36 -> 43; matrix products, arithmetic and copies ran while one was open for 2% -> 2% of each run, Pallas kernels for 0% -> 0%
where the time goes in v2:
time: 374 us
  waiting for transfers between devices  231 us (62%)
  starting transfers between devices  72.5 us (19%)
  matrix products  26.5 us (7%)
  local copies, waits for them, and re-layouts  20.6 us (6%)
  between operations  14.9 us (4%)
  other arithmetic  8.3 us (2%)
    all_gather x1, waiting for transfers between devices, shards(): kv_weight = lax.all_gather(keyval_weight, 'ctx', axis=0, tiled=True)  138 us
    ppermute x52, waiting for transfers between devices, _swap(): return lax.ppermute(x, axis, [(j, j ^ k) for j in range(n)])  83.5 us
    ppermute x52, starting transfers between devices, _swap(): return lax.ppermute(x, axis, [(j, j ^ k) for j in range(n)])  64.2 us
    dot_general x1, matrix products, shards(): jnp.einsum('td,djc->tjc', activations, kv_weight, preferred_element_type=...  12.5 us
    all_to_all x1, waiting for transfers between devices, shards(): row_blocks = lax.all_to_all(rows_here, 'ctx', 1, 0, tiled=True)  9.41 us
    dot_general x1, matrix products, shards(): lax.dot_general(hidden, vocab_weight, (((1,), (1,)), ((), ())), preferred...  8.63 us
    all_to_all x1, starting transfers between devices, shards(): row_blocks = lax.all_to_all(rows_here, 'ctx', 1, 0, tiled=True)  8.31 us
  transfers between devices with their start and end apart: 54, of which 43 were waited for; matrix products, arithmetic and copies ran while one was open for 2% of the time, Pallas kernels for 0%

profile of v2, /device:TPU:0, one launch (start us, length us, event | category | flops | bytes accessed | tf_op | source)
XLA Modules:
  0.0 373.8 jit_solution(14141467707106676743)
XLA Ops:
  6.5 2.6 copy.107
  9.8 3.3 gather_fusion
  13.8 8.3 %all-to-all-start = ((bf16[16,16,256]{2,0,1:T(8,128)(2,1)}), bf16[16,16,256]{2,0,1:T(8,128)(2,1)S(1)}, u32[]{:S(2)}, u32[]{:S(2)}) async-start(bf16[16,16,256]{2,0,1:T(8,128)(2,1)} %bitcast_select_fusion), calls=%async_computation | async-start | bytes 262144 | tf_op jit(solution)/shard_map/all_to_all | solution.py:103
  22.2 9.4 %all-to-all-done = bf16[16,16,256]{2,0,1:T(8,128)(2,1)S(1)} async-done(((bf16[16,16,256]{2,0,1:T(8,128)(2,1)}), bf16[16,16,256]{2,0,1:T(8,128)(2,1)S(1)}, u32[]{:S(2)}, u32[]{:S(2)}) %all-to-all-start) | async-done | bytes 131104 | tf_op jit(solution)/shard_map/all_to_all | solution.py:103
  35.5 5.8 %collective-permute-done = f32[4,16,1024]{2,1,0:T(8,128)S(1)} collective-permute-done((f32[4,16,1024]{2,1,0:T(8,128)S(1)}, f32[4,16,1024]{2,1,0:T(8,128)S(1)}, u32[]{:S(2)}, u32[]{:S(2)}) %collective-permute-start) | collective-permute-done | bytes 262176 | tf_op jit(solution)/shard_map/ppermute | solution.py:21
  41.5 4.0 %collective-permute-done.2 = f32[4,16,1024]{2,1,0:T(8,128)S(1)} collective-permute-done((f32[4,16,1024]{2,1,0:T(8,128)S(1)}, f32[4,16,1024]{2,1,0:T(8,128)S(1)}, u32[]{:S(2)}, u32[]{:S(2)}) %collective-permute-start.2) | collective-permute-done | bytes 262176 | tf_op jit(solution)/shard_map/ppermute | solution.py:21
  50.2 4.7 %collective-permute-done.4 = f32[1,16,1024]{2,1,0:T(8,128)S(1)} collective-permute-done((f32[1,16,1024]{2,1,0:T(8,128)S(1)}, f32[1,16,1024]{2,1,0:T(8,128)S(1)}, u32[]{:S(2)}, u32[]{:S(2)}) %collective-permute-start.4) | collective-permute-done | bytes 65568 | tf_op jit(solution)/shard_map/ppermute | solution.py:21
  57.4 2.7 collective-permute-start.8
  66.9 5.6 %collective-permute-done.9 = bf16[4,16,1024]{2,1,0:T(8,128)(2,1)S(1)} collective-permute-done((bf16[4,16,1024]{2,1,0:T(8,128)(2,1)S(1)}, bf16[4,16,1024]{2,1,0:T(8,128)(2,1)S(1)}, u32[]{:S(2)}, u32[]{:S(2)}) %collective-permute-start.9) | collective-permute-done | bytes 131104 | tf_op jit(solution)/shard_map/ppermute | solution.py:21
  74.3 3.6 collective-permute-done.11
  78.2 138.2 %all-gather.2.cloned.1.call-done = bf16[4096,2,1024]{2,0,1:T(8,128)(2,1)} async-done(((bf16[256,2,1024]{2,0,1:T(8,128)(2,1)}), bf16[4096,2,1024]{2,0,1:T(8,128)(2,1)}) %all-gather.2.cloned.1.call-update) | async-done | bytes 16777232 | tf_op jit(solution)/shard_map/all_gather | solution.py:100
  216.3 12.5 %fusion.8 = bf16[448,2,1024]{2,0,1:T(8,128)(2,1)S(1)} fusion(bf16[4096,2,1024]{2,0,1:T(8,128)(2,1)} %all-gather.2.cloned.1.call-done, bf16[448,4096]{1,0:T(8,128)(2,1)} %param.9), kind=kOutput, calls=%fused_computation.17 | convolution fusion | flops 7517110272 | bytes 22282240 | tf_op jit(solution)/shard_map/td,djc->tjc/dot_general | solution.py:113
  232.7 2.9 fusion.11
  240.9 6.7 %collective-permute-done.12 = f32[4,16,1040]{2,1,0:T(8,128)S(1)} collective-permute-done((f32[4,16,1040]{2,1,0:T(8,128)}, f32[4,16,1040]{2,1,0:T(8,128)S(1)}, u32[]{:S(2)}, u32[]{:S(2)}) %collective-permute-start.12) | collective-permute-done | bytes 266272 | tf_op jit(solution)/shard_map/ppermute | solution.py:21
  247.9 5.3 %collective-permute-done.14 = f32[4,16,1040]{2,1,0:T(8,128)S(1)} collective-permute-done((f32[4,16,1040]{2,1,0:T(8,128)S(1)}, f32[4,16,1040]{2,1,0:T(8,128)S(1)}, u32[]{:S(2)}, u32[]{:S(2)}) %collective-permute-start.14) | collective-permute-done | bytes 266272 | tf_op jit(solution)/shard_map/ppermute | solution.py:21
  255.0 2.6 collective-permute-start.16
  260.7 3.0 collective-permute-done.17
  270.5 3.2 collective-permute-done.20
  299.8 3.4 collective-permute-done.31
  308.6 3.2 collective-permute-done.34
  315.5 2.9 collective-permute-done.35
  318.5 3.4 collective-permute-done.36
  337.2 2.8 copy.133
  340.0 8.6 %fusion.127 = (f32[256]{0:T(256)S(1)}, f32[256,1984]{0,1:T(8,128)S(1)}) fusion(bf16[256,4096]{1,0:T(8,128)(2,1)} %bitcast.351, bf16[1984,4096]{1,0:T(8,128)(2,1)} %param.14), kind=kOutput, calls=%fused_computation.306 | convolution fusion | flops 4161257216 | bytes 20382720 | tf_op jit(solution)/shard_map/dot_general | solution.py:166
  (240 shorter events, 110.2 us)
Async XLA Ops:
  6.5 209.8 %all-gather.2.cloned.1.call-start = ((), (), s32[]{:S(2)}) async-start(), calls=%async_computation.1 | async-start | bytes 17825792 | tf_op jit(solution)/shard_map/all_gather | solution.py:100
  13.8 17.8 %all-to-all-start = ((bf16[16,16,256]{2,0,1:T(8,128)(2,1)}), bf16[16,16,256]{2,0,1:T(8,128)(2,1)S(1)}, u32[]{:S(2)}, u32[]{:S(2)}) async-start(bf16[16,16,256]{2,0,1:T(8,128)(2,1)} %bitcast_select_fusion), calls=%async_computation | async-start | bytes 262144 | tf_op jit(solution)/shard_map/all_to_all | solution.py:103
  32.0 9.3 %collective-permute-start = (f32[4,16,1024]{2,1,0:T(8,128)S(1)}, f32[4,16,1024]{2,1,0:T(8,128)S(1)}, u32[]{:S(2)}, u32[]{:S(2)}) collective-permute-start(f32[4,16,1024]{2,1,0:T(8,128)S(1)} %get-tuple-element.50), channel_id=1, source_target_pairs={{0,2},{2,0},{4,6},{6,4},{8,10},{10,8},{12,14},{14,12},{16,18},{18,... | collective-permute-start | bytes 786440 | tf_op jit(solution)/shard_map/ppermute | solution.py:21
  33.3 8.2 %collective-permute-start.1 = (f32[4,16,1024]{2,1,0:T(8,128)S(1)}, f32[4,16,1024]{2,1,0:T(8,128)S(1)}, u32[]{:S(2)}, u32[]{:S(2)}) collective-permute-start(f32[4,16,1024]{2,1,0:T(8,128)S(1)} %get-tuple-element.52), channel_id=1, source_target_pairs={{0,4},{2,6},{4,0},{6,2},{8,12},{10,14},{12,8},{14,10},{16,20},{18,... | collective-permute-start | bytes 786440 | tf_op jit(solution)/shard_map/ppermute | solution.py:21
  33.6 11.8 %collective-permute-start.2 = (f32[4,16,1024]{2,1,0:T(8,128)S(1)}, f32[4,16,1024]{2,1,0:T(8,128)S(1)}, u32[]{:S(2)}, u32[]{:S(2)}) collective-permute-start(f32[4,16,1024]{2,1,0:T(8,128)S(1)} %get-tuple-element.51), channel_id=1, source_target_pairs={{0,6},{2,4},{4,2},{6,0},{8,14},{10,12},{12,10},{14,8},{16,22},{18,... | collective-permute-start | bytes 786440 | tf_op jit(solution)/shard_map/ppermute | solution.py:21
  47.1 7.8 %collective-permute-start.4 = (f32[1,16,1024]{2,1,0:T(8,128)S(1)}, f32[1,16,1024]{2,1,0:T(8,128)S(1)}, u32[]{:S(2)}, u32[]{:S(2)}) collective-permute-start(f32[1,16,1024]{2,1,0:T(8,128)S(1)} %get-tuple-element.76), channel_id=1, source_target_pairs={{0,16},{2,18},{4,20},{6,22},{8,24},{10,26},{12,28},{14,30},{16,0},... | collective-permute-start | bytes 196616 | tf_op jit(solution)/shard_map/ppermute | solution.py:21
  49.5 6.2 %collective-permute-start.5 = (f32[1,16,1024]{2,1,0:T(8,128)S(1)}, f32[1,16,1024]{2,1,0:T(8,128)S(1)}, u32[]{:S(2)}, u32[]{:S(2)}) collective-permute-start(f32[1,16,1024]{2,1,0:T(8,128)S(1)} %get-tuple-element.75), channel_id=1, source_target_pairs={{0,24},{2,26},{4,28},{6,30},{8,16},{10,18},{12,20},{14,22},{16,8},... | collective-permute-start | bytes 196616 | tf_op jit(solution)/shard_map/ppermute | solution.py:21
  57.4 5.9 %collective-permute-start.8 = (bf16[16,1024]{1,0:T(8,128)(2,1)S(1)}, bf16[16,1024]{1,0:T(8,128)(2,1)S(1)}, u32[]{:S(2)}, u32[]{:S(2)}) collective-permute-start(bf16[16,1024]{1,0:T(8,128)(2,1)S(1)} %bitcast.371), channel_id=1, source_target_pairs={{0,24},{2,26},{4,28},{6,30},{8,16},{10,18},{12,20},{14,22},{16,8},... | collective-permute-start | bytes 98312 | tf_op jit(solution)/shard_map/ppermute | solution.py:21
  63.4 9.2 %collective-permute-start.9 = (bf16[4,16,1024]{2,1,0:T(8,128)(2,1)S(1)}, bf16[4,16,1024]{2,1,0:T(8,128)(2,1)S(1)}, u32[]{:S(2)}, u32[]{:S(2)}) collective-permute-start(bf16[4,16,1024]{2,1,0:T(8,128)(2,1)S(1)} %get-tuple-element.84), channel_id=1, source_target_pairs={{0,2},{2,0},{4,6},{6,4},{8,10},{10,8},{12,14},{14,12},{16,18},{18,... | collective-permute-start | bytes 393224 | tf_op jit(solution)/shard_map/ppermute | solution.py:21
  64.7 9.5 %collective-permute-start.10 = (bf16[4,16,1024]{2,1,0:T(8,128)(2,1)S(1)}, bf16[4,16,1024]{2,1,0:T(8,128)(2,1)S(1)}, u32[]{:S(2)}, u32[]{:S(2)}) collective-permute-start(bf16[4,16,1024]{2,1,0:T(8,128)(2,1)S(1)} %get-tuple-element.84), channel_id=1, source_target_pairs={{0,4},{2,6},{4,0},{6,2},{8,12},{10,14},{12,8},{14,10},{16,20},{18,... | collective-permute-start | bytes 393224 | tf_op jit(solution)/shard_map/ppermute | solution.py:21
  66.4 11.4 %collective-permute-start.11 = (bf16[4,16,1024]{2,1,0:T(8,128)(2,1)S(1)}, bf16[4,16,1024]{2,1,0:T(8,128)(2,1)S(1)}, u32[]{:S(2)}, u32[]{:S(2)}) collective-permute-start(bf16[4,16,1024]{2,1,0:T(8,128)(2,1)S(1)} %get-tuple-element.84), channel_id=1, source_target_pairs={{0,6},{2,4},{4,2},{6,0},{8,14},{10,12},{12,10},{14,8},{16,22},{18,... | collective-permute-start | bytes 393224 | tf_op jit(solution)/shard_map/ppermute | solution.py:21
  237.4 10.2 %collective-permute-start.12 = (f32[4,16,1040]{2,1,0:T(8,128)}, f32[4,16,1040]{2,1,0:T(8,128)S(1)}, u32[]{:S(2)}, u32[]{:S(2)}) collective-permute-start(f32[4,16,1040]{2,1,0:T(8,128)} %get-tuple-element.43), channel_id=1, source_target_pairs={{0,2},{2,0},{4,6},{6,4},{8,10},{10,8},{12,14},{14,12},{16,18},{18,... | collective-permute-start | bytes 798728 | tf_op jit(solution)/shard_map/ppermute | solution.py:21
  238.5 9.4 %collective-permute-start.13 = (f32[4,16,1040]{2,1,0:T(8,128)S(1)}, f32[4,16,1040]{2,1,0:T(8,128)S(1)}, u32[]{:S(2)}, u32[]{:S(2)}) collective-permute-start(f32[4,16,1040]{2,1,0:T(8,128)S(1)} %get-tuple-element.42), channel_id=1, source_target_pairs={{0,4},{2,6},{4,0},{6,2},{8,12},{10,14},{12,8},{14,10},{16,20},{18,... | collective-permute-start | bytes 798728 | tf_op jit(solution)/shard_map/ppermute | solution.py:21
  239.5 13.7 %collective-permute-start.14 = (f32[4,16,1040]{2,1,0:T(8,128)S(1)}, f32[4,16,1040]{2,1,0:T(8,128)S(1)}, u32[]{:S(2)}, u32[]{:S(2)}) collective-permute-start(f32[4,16,1040]{2,1,0:T(8,128)S(1)} %get-tuple-element.41), channel_id=1, source_target_pairs={{0,6},{2,4},{4,2},{6,0},{8,14},{10,12},{12,10},{14,8},{16,22},{18,... | collective-permute-start | bytes 798728 | tf_op jit(solution)/shard_map/ppermute | solution.py:21
  255.0 5.5 %collective-permute-start.16 = (f32[1,16,1040]{2,1,0:T(8,128)S(1)}, f32[1,16,1040]{2,1,0:T(8,128)S(1)}, u32[]{:S(2)}, u32[]{:S(2)}) collective-permute-start(f32[1,16,1040]{2,1,0:T(8,128)S(1)} %get-tuple-element.67), channel_id=1, source_target_pairs={{0,16},{2,18},{4,20},{6,22},{8,24},{10,26},{12,28},{14,30},{16,0},... | collective-permute-start | bytes 199688 | tf_op jit(solution)/shard_map/ppermute | solution.py:21
  257.5 6.2 %collective-permute-start.17 = (f32[1,16,1040]{2,1,0:T(8,128)S(1)}, f32[1,16,1040]{2,1,0:T(8,128)S(1)}, u32[]{:S(2)}, u32[]{:S(2)}) collective-permute-start(f32[1,16,1040]{2,1,0:T(8,128)S(1)} %get-tuple-element.66), channel_id=1, source_target_pairs={{0,24},{2,26},{4,28},{6,30},{8,16},{10,18},{12,20},{14,22},{16,8},... | collective-permute-start | bytes 199688 | tf_op jit(solution)/shard_map/ppermute | solution.py:21
  268.0 5.7 %collective-permute-start.20 = (bf16[16,1024]{1,0:T(8,128)(2,1)S(1)}, bf16[16,1024]{1,0:T(8,128)(2,1)S(1)}, u32[]{:S(2)}, u32[]{:S(2)}) collective-permute-start(bf16[16,1024]{1,0:T(8,128)(2,1)S(1)} %fusion.38), channel_id=1, source_target_pairs={{0,24},{2,26},{4,28},{6,30},{8,16},{10,18},{12,20},{14,22},{16,8},... | collective-permute-start | bytes 98312 | tf_op jit(solution)/shard_map/ppermute | solution.py:21
  276.0 5.9 %collective-permute-start.23 = (bf16[4,16,1024]{2,1,0:T(8,128)(2,1)S(1)}, bf16[4,16,1024]{2,1,0:T(8,128)(2,1)S(1)}, u32[]{:S(2)}, u32[]{:S(2)}) collective-permute-start(bf16[4,16,1024]{2,1,0:T(8,128)(2,1)S(1)} %get-tuple-element.78), channel_id=1, source_target_pairs={{0,6},{2,4},{4,2},{6,0},{8,14},{10,12},{12,10},{14,8},{16,22},{18,... | collective-permute-start | bytes 393224 | tf_op jit(solution)/shard_map/ppermute | solution.py:21
  305.8 6.1 %collective-permute-start.34 = (bf16[128,256]{1,0:T(8,128)(2,1)S(1)}, bf16[128,256]{1,0:T(8,128)(2,1)S(1)}, u32[]{:S(2)}, u32[]{:S(2)}) collective-permute-start(bf16[128,256]{1,0:T(8,128)(2,1)S(1)} %multiply_convert_fusion), channel_id=1, source_target_pairs={{0,24},{2,26},{4,28},{6,30},{8,16},{10,18},{12,20},{14,22},{16,8},... | collective-permute-start | bytes 196616 | tf_op jit(solution)/shard_map/ppermute | solution.py:21
  312.0 6.5 %collective-permute-start.35 = (bf16[4,128,256]{2,1,0:T(8,128)(2,1)S(1)}, bf16[4,128,256]{2,1,0:T(8,128)(2,1)S(1)}, u32[]{:S(2)}, u32[]{:S(2)}) collective-permute-start(bf16[4,128,256]{2,1,0:T(8,128)(2,1)S(1)} %get-tuple-element.69), channel_id=1, source_target_pairs={{0,2},{2,0},{4,6},{6,4},{8,10},{10,8},{12,14},{14,12},{16,18},{18,... | collective-permute-start | bytes 786440 | tf_op jit(solution)/shard_map/ppermute | solution.py:21
  312.7 9.2 %collective-permute-start.36 = (bf16[4,128,256]{2,1,0:T(8,128)(2,1)S(1)}, bf16[4,128,256]{2,1,0:T(8,128)(2,1)S(1)}, u32[]{:S(2)}, u32[]{:S(2)}) collective-permute-start(bf16[4,128,256]{2,1,0:T(8,128)(2,1)S(1)} %get-tuple-element.69), channel_id=1, source_target_pairs={{0,4},{2,6},{4,0},{6,2},{8,12},{10,14},{12,8},{14,10},{16,20},{18,... | collective-permute-start | bytes 786440 | tf_op jit(solution)/shard_map/ppermute | solution.py:21
  314.2 7.7 %collective-permute-start.37 = (bf16[4,128,256]{2,1,0:T(8,128)(2,1)S(1)}, bf16[4,128,256]{2,1,0:T(8,128)(2,1)S(1)}, u32[]{:S(2)}, u32[]{:S(2)}) collective-permute-start(bf16[4,128,256]{2,1,0:T(8,128)(2,1)S(1)} %get-tuple-element.69), channel_id=1, source_target_pairs={{0,6},{2,4},{4,2},{6,0},{8,14},{10,12},{12,10},{14,8},{16,22},{18,... | collective-permute-start | bytes 786440 | tf_op jit(solution)/shard_map/ppermute | solution.py:21
  322.9 13.3 %collective-permute-start.38 = (bf16[128,4096]{0,1:T(8,128)(2,1)S(1)}, bf16[128,4096]{0,1:T(8,128)(2,1)S(1)}, u32[]{:S(2)}, u32[]{:S(2)}) collective-permute-start(bf16[128,4096]{0,1:T(8,128)(2,1)S(1)} %bitcast.343), channel_id=1, source_target_pairs={{0,1},{1,0},{2,3},{3,2},{4,5},{5,4},{6,7},{7,6},{8,9},{9,8},{10,11... | collective-permute-start | bytes 3145736 | tf_op jit(solution)/shard_map/ppermute | solution.py:21
  360.2 5.4 %collective-permute-start.51 = (f32[3,256]{1,0:T(4,128)S(1)}, f32[3,256]{1,0:T(4,128)S(1)}, u32[]{:S(2)}, u32[]{:S(2)}) collective-permute-start(f32[3,256]{1,0:T(4,128)S(1)} %get-tuple-element.109), channel_id=1, source_target_pairs={{0,24},{2,26},{4,28},{6,30},{8,16},{10,18},{12,20},{14,22},{16,8},... | collective-permute-start | bytes 9224 | tf_op jit(solution)/shard_map/ppermute | solution.py:21
  (36 other events, 208.8 us)
Sparse Core Ops, SparseCore 0:
  10.1 206.1 all-gather.1

commit v3 on v2

--- a/solution.py
+++ b/solution.py
@@ -155,12 +155,9 @@
     head_idx = lax.axis_index("head")
     my_rows = lax.dynamic_slice_in_dim(attended, head_idx * share, share, 0)
     branch = jnp.dot(my_rows, out_full, preferred_element_type=jnp.float32)
-    sumsq = _all_reduce(jnp.sum(branch * branch, axis=1), "ctx", n_ctx, _add)
-    gain = lax.dynamic_slice_in_dim(norm_gain, lax.axis_index("ctx") * col_block, col_block, 0)
-    hidden = (
-        branch * lax.rsqrt(sumsq / width + 1e-06)[:, None] * gain
-    ).astype(jnp.bfloat16)
-    hidden = _all_gather(hidden, "ctx", n_ctx).transpose(1, 0, 2).reshape(share, width)
+    branch = _all_gather(branch, "ctx", n_ctx).transpose(1, 0, 2).reshape(share, width)
+    meansquare = jnp.mean(branch * branch, axis=1, keepdims=True)
+    hidden = (branch * lax.rsqrt(meansquare + 1e-06) * norm_gain).astype(jnp.bfloat16)
     hidden = _all_gather(hidden, "head", n_head).reshape(total_rows, width)
 
     logits = lax.dot_general(

time: 374 us -> 378 us (1.011)
  starting transfers between devices: 72.5 us -> 64 us
  waiting for transfers between devices: 231 us -> 239 us
    ppermute x52 -> x46, waiting for transfers between devices: 83.5 us -> 93.9 us  [_swap(): return lax.ppermute(x, axis, [(j, j ^ k) for j in range(n)])]
    ppermute x52 -> x46, starting transfers between devices: 64.2 us -> 55.6 us  [_swap(): return lax.ppermute(x, axis, [(j, j ^ k) for j in range(n)])]
  transfers between devices with their start and end apart: 54 -> 48, of which waited for: 43 -> 33; matrix products, arithmetic and copies ran while one was open for 2% -> 2% of each run, Pallas kernels for 0% -> 0%
where the time goes in v3:
time: 378 us; the launch traced here: 377 us
  waiting for transfers between devices  239 us (63%)
  starting transfers between devices  64 us (17%)
  matrix products  26.4 us (7%)
  local copies, waits for them, and re-layouts  21.5 us (6%)
  between operations  14.9 us (4%)
  other arithmetic  11.5 us (3%)
    all_gather x1, waiting for transfers between devices, shards(): kv_weight = lax.all_gather(keyval_weight, 'ctx', axis=0, tiled=True)  135 us
    ppermute x46, waiting for transfers between devices, _swap(): return lax.ppermute(x, axis, [(j, j ^ k) for j in range(n)])  93.9 us
    ppermute x46, starting transfers between devices, _swap(): return lax.ppermute(x, axis, [(j, j ^ k) for j in range(n)])  55.6 us
    dot_general x1, matrix products, shards(): jnp.einsum('td,djc->tjc', activations, kv_weight, preferred_element_type=...  12.6 us
    all_to_all x1, waiting for transfers between devices, shards(): row_blocks = lax.all_to_all(rows_here, 'ctx', 1, 0, tiled=True)  9.56 us
    dot_general x1, matrix products, shards(): lax.dot_general(hidden, vocab_weight, (((1,), (1,)), ((), ())), preferred...  8.63 us
    all_to_all x1, starting transfers between devices, shards(): row_blocks = lax.all_to_all(rows_here, 'ctx', 1, 0, tiled=True)  8.31 us
  transfers between devices with their start and end apart: 48, of which 33 were waited for; matrix products, arithmetic and copies ran while one was open for 2% of the time, Pallas kernels for 0%

profile of v3, /device:TPU:0, one launch (start us, length us, event | category | flops | bytes accessed | tf_op | source)
XLA Modules:
  0.0 377.2 jit_solution(8791531929773588572)
XLA Ops:
  9.2 3.3 gather_fusion
  13.2 8.3 %all-to-all-start = ((bf16[16,16,256]{2,0,1:T(8,128)(2,1)}), bf16[16,16,256]{2,0,1:T(8,128)(2,1)S(1)}, u32[]{:S(2)}, u32[]{:S(2)}) async-start(bf16[16,16,256]{2,0,1:T(8,128)(2,1)} %bitcast_select_fusion), calls=%async_computation | async-start | bytes 262144 | tf_op jit(solution)/shard_map/all_to_all | solution.py:103
  21.5 9.6 %all-to-all-done = bf16[16,16,256]{2,0,1:T(8,128)(2,1)S(1)} async-done(((bf16[16,16,256]{2,0,1:T(8,128)(2,1)}), bf16[16,16,256]{2,0,1:T(8,128)(2,1)S(1)}, u32[]{:S(2)}, u32[]{:S(2)}) %all-to-all-start) | async-done | bytes 131104 | tf_op jit(solution)/shard_map/all_to_all | solution.py:103
  35.0 5.8 %collective-permute-done = f32[4,16,1024]{2,1,0:T(8,128)S(1)} collective-permute-done((f32[4,16,1024]{2,1,0:T(8,128)S(1)}, f32[4,16,1024]{2,1,0:T(8,128)S(1)}, u32[]{:S(2)}, u32[]{:S(2)}) %collective-permute-start) | collective-permute-done | bytes 262176 | tf_op jit(solution)/shard_map/ppermute | solution.py:21
  40.8 4.6 %collective-permute-done.2 = f32[4,16,1024]{2,1,0:T(8,128)S(1)} collective-permute-done((f32[4,16,1024]{2,1,0:T(8,128)S(1)}, f32[4,16,1024]{2,1,0:T(8,128)S(1)}, u32[]{:S(2)}, u32[]{:S(2)}) %collective-permute-start.2) | collective-permute-done | bytes 262176 | tf_op jit(solution)/shard_map/ppermute | solution.py:21
  51.1 3.3 collective-permute-done.4
  56.9 3.2 collective-permute-start.8
  60.1 4.4 %collective-permute-done.7 = bf16[16,1024]{1,0:T(8,128)(2,1)S(1)} collective-permute-done((bf16[16,1024]{1,0:T(8,128)(2,1)S(1)}, bf16[16,1024]{1,0:T(8,128)(2,1)S(1)}, u32[]{:S(2)}, u32[]{:S(2)}) %collective-permute-start.7) | collective-permute-done | bytes 32800 | tf_op jit(solution)/shard_map/ppermute | solution.py:21
  68.1 5.3 %collective-permute-done.9 = bf16[4,16,1024]{2,1,0:T(8,128)(2,1)S(1)} collective-permute-done((bf16[4,16,1024]{2,1,0:T(8,128)(2,1)S(1)}, bf16[4,16,1024]{2,1,0:T(8,128)(2,1)S(1)}, u32[]{:S(2)}, u32[]{:S(2)}) %collective-permute-start.9) | collective-permute-done | bytes 131104 | tf_op jit(solution)/shard_map/ppermute | solution.py:21
  75.1 3.6 collective-permute-done.11
  79.0 135.4 %all-gather.2.cloned.1.call-done = bf16[4096,2,1024]{2,0,1:T(8,128)(2,1)} async-done(((bf16[256,2,1024]{2,0,1:T(8,128)(2,1)}), bf16[4096,2,1024]{2,0,1:T(8,128)(2,1)}) %all-gather.2.cloned.1.call-update) | async-done | bytes 16777232 | tf_op jit(solution)/shard_map/all_gather | solution.py:100
  214.4 12.6 %fusion.12 = bf16[448,2,1024]{2,0,1:T(8,128)(2,1)S(1)} fusion(bf16[4096,2,1024]{2,0,1:T(8,128)(2,1)} %all-gather.2.cloned.1.call-done, bf16[448,4096]{1,0:T(8,128)(2,1)} %param.9), kind=kOutput, calls=%fused_computation.26 | convolution fusion | flops 7517110272 | bytes 22282240 | tf_op jit(solution)/shard_map/td,djc->tjc/dot_general | solution.py:113
  230.8 2.9 fusion.15
  238.4 6.5 %collective-permute-done.12 = f32[4,16,1040]{2,1,0:T(8,128)S(1)} collective-permute-done((f32[4,16,1040]{2,1,0:T(8,128)S(1)}, f32[4,16,1040]{2,1,0:T(8,128)S(1)}, u32[]{:S(2)}, u32[]{:S(2)}) %collective-permute-start.12) | collective-permute-done | bytes 266272 | tf_op jit(solution)/shard_map/ppermute | solution.py:21
  244.8 4.0 %collective-permute-done.13 = f32[4,16,1040]{2,1,0:T(8,128)S(1)} collective-permute-done((f32[4,16,1040]{2,1,0:T(8,128)S(1)}, f32[4,16,1040]{2,1,0:T(8,128)S(1)}, u32[]{:S(2)}, u32[]{:S(2)}) %collective-permute-start.13) | collective-permute-done | bytes 266272 | tf_op jit(solution)/shard_map/ppermute | solution.py:21
  252.2 2.6 collective-permute-start.16
  258.0 3.0 collective-permute-done.17
  267.8 3.2 collective-permute-done.20
  297.2 4.0 %collective-permute-done.34 = s32[16]{0:T(128)S(1)} collective-permute-done((s32[16]{0:T(128)S(1)}, s32[16]{0:T(128)S(1)}, u32[]{:S(2)}, u32[]{:S(2)}) %collective-permute-start.34) | collective-permute-done | bytes 96 | tf_op jit(solution)/shard_map/ppermute | solution.py:21
  306.8 18.8 %collective-permute-done.36 = s32[4,16]{1,0:T(4,128)S(1)} collective-permute-done((s32[4,16]{1,0:T(4,128)S(1)}, s32[4,16]{1,0:T(4,128)S(1)}, u32[]{:S(2)}, u32[]{:S(2)}) %collective-permute-start.36) | collective-permute-done | bytes 288 | tf_op jit(solution)/shard_map/ppermute | solution.py:21
  326.8 3.3 collective-permute-done.38
  340.7 2.9 copy.133
  343.6 8.6 %fusion.125 = (f32[256]{0:T(256)S(1)}, f32[256,1984]{0,1:T(8,128)S(1)}) fusion(bf16[256,4096]{1,0:T(8,128)(2,1)} %bitcast.348, bf16[1984,4096]{1,0:T(8,128)(2,1)} %param.14), kind=kOutput, calls=%fused_computation.295 | convolution fusion | flops 4161257216 | bytes 20382720 | tf_op jit(solution)/shard_map/dot_general | solution.py:163
  366.4 2.6 collective-permute-done.45
  (228 shorter events, 100.7 us)
Async XLA Ops:
  6.5 207.9 %all-gather.2.cloned.1.call-start = ((), (), s32[]{:S(2)}) async-start(), calls=%async_computation.1 | async-start | bytes 17825792 | tf_op jit(solution)/shard_map/all_gather | solution.py:100
  13.2 17.9 %all-to-all-start = ((bf16[16,16,256]{2,0,1:T(8,128)(2,1)}), bf16[16,16,256]{2,0,1:T(8,128)(2,1)S(1)}, u32[]{:S(2)}, u32[]{:S(2)}) async-start(bf16[16,16,256]{2,0,1:T(8,128)(2,1)} %bitcast_select_fusion), calls=%async_computation | async-start | bytes 262144 | tf_op jit(solution)/shard_map/all_to_all | solution.py:103
  31.5 9.3 %collective-permute-start = (f32[4,16,1024]{2,1,0:T(8,128)S(1)}, f32[4,16,1024]{2,1,0:T(8,128)S(1)}, u32[]{:S(2)}, u32[]{:S(2)}) collective-permute-start(f32[4,16,1024]{2,1,0:T(8,128)S(1)} %get-tuple-element.50), channel_id=1, source_target_pairs={{0,2},{2,0},{4,6},{6,4},{8,10},{10,8},{12,14},{14,12},{16,18},{18,... | collective-permute-start | bytes 786440 | tf_op jit(solution)/shard_map/ppermute | solution.py:21
  33.0 7.8 %collective-permute-start.1 = (f32[4,16,1024]{2,1,0:T(8,128)S(1)}, f32[4,16,1024]{2,1,0:T(8,128)S(1)}, u32[]{:S(2)}, u32[]{:S(2)}) collective-permute-start(f32[4,16,1024]{2,1,0:T(8,128)S(1)} %get-tuple-element.52), channel_id=1, source_target_pairs={{0,4},{2,6},{4,0},{6,2},{8,12},{10,14},{12,8},{14,10},{16,20},{18,... | collective-permute-start | bytes 786440 | tf_op jit(solution)/shard_map/ppermute | solution.py:21
  33.0 12.4 %collective-permute-start.2 = (f32[4,16,1024]{2,1,0:T(8,128)S(1)}, f32[4,16,1024]{2,1,0:T(8,128)S(1)}, u32[]{:S(2)}, u32[]{:S(2)}) collective-permute-start(f32[4,16,1024]{2,1,0:T(8,128)S(1)} %get-tuple-element.51), channel_id=1, source_target_pairs={{0,6},{2,4},{4,2},{6,0},{8,14},{10,12},{12,10},{14,8},{16,22},{18,... | collective-permute-start | bytes 786440 | tf_op jit(solution)/shard_map/ppermute | solution.py:21
  46.9 7.6 %collective-permute-start.4 = (f32[1,16,1024]{2,1,0:T(8,128)S(1)}, f32[1,16,1024]{2,1,0:T(8,128)S(1)}, u32[]{:S(2)}, u32[]{:S(2)}) collective-permute-start(f32[1,16,1024]{2,1,0:T(8,128)S(1)} %get-tuple-element.76), channel_id=1, source_target_pairs={{0,16},{2,18},{4,20},{6,22},{8,24},{10,26},{12,28},{14,30},{16,0},... | collective-permute-start | bytes 196616 | tf_op jit(solution)/shard_map/ppermute | solution.py:21
  49.2 6.4 %collective-permute-start.5 = (f32[1,16,1024]{2,1,0:T(8,128)S(1)}, f32[1,16,1024]{2,1,0:T(8,128)S(1)}, u32[]{:S(2)}, u32[]{:S(2)}) collective-permute-start(f32[1,16,1024]{2,1,0:T(8,128)S(1)} %get-tuple-element.75), channel_id=1, source_target_pairs={{0,24},{2,26},{4,28},{6,30},{8,16},{10,18},{12,20},{14,22},{16,8},... | collective-permute-start | bytes 196616 | tf_op jit(solution)/shard_map/ppermute | solution.py:21
  56.5 8.0 %collective-permute-start.7 = (bf16[16,1024]{1,0:T(8,128)(2,1)S(1)}, bf16[16,1024]{1,0:T(8,128)(2,1)S(1)}, u32[]{:S(2)}, u32[]{:S(2)}) collective-permute-start(bf16[16,1024]{1,0:T(8,128)(2,1)S(1)} %bitcast.367), channel_id=1, source_target_pairs={{0,16},{2,18},{4,20},{6,22},{8,24},{10,26},{12,28},{14,30},{16,0},... | collective-permute-start | bytes 98312 | tf_op jit(solution)/shard_map/ppermute | solution.py:21
  56.9 7.5 %collective-permute-start.8 = (bf16[16,1024]{1,0:T(8,128)(2,1)S(1)}, bf16[16,1024]{1,0:T(8,128)(2,1)S(1)}, u32[]{:S(2)}, u32[]{:S(2)}) collective-permute-start(bf16[16,1024]{1,0:T(8,128)(2,1)S(1)} %bitcast.368), channel_id=1, source_target_pairs={{0,24},{2,26},{4,28},{6,30},{8,16},{10,18},{12,20},{14,22},{16,8},... | collective-permute-start | bytes 98312 | tf_op jit(solution)/shard_map/ppermute | solution.py:21
  64.6 8.8 %collective-permute-start.9 = (bf16[4,16,1024]{2,1,0:T(8,128)(2,1)S(1)}, bf16[4,16,1024]{2,1,0:T(8,128)(2,1)S(1)}, u32[]{:S(2)}, u32[]{:S(2)}) collective-permute-start(bf16[4,16,1024]{2,1,0:T(8,128)(2,1)S(1)} %get-tuple-element.84), channel_id=1, source_target_pairs={{0,2},{2,0},{4,6},{6,4},{8,10},{10,8},{12,14},{14,12},{16,18},{18,... | collective-permute-start | bytes 393224 | tf_op jit(solution)/shard_map/ppermute | solution.py:21
  66.2 8.9 %collective-permute-start.10 = (bf16[4,16,1024]{2,1,0:T(8,128)(2,1)S(1)}, bf16[4,16,1024]{2,1,0:T(8,128)(2,1)S(1)}, u32[]{:S(2)}, u32[]{:S(2)}) collective-permute-start(bf16[4,16,1024]{2,1,0:T(8,128)(2,1)S(1)} %get-tuple-element.84), channel_id=1, source_target_pairs={{0,4},{2,6},{4,0},{6,2},{8,12},{10,14},{12,8},{14,10},{16,20},{18,... | collective-permute-start | bytes 393224 | tf_op jit(solution)/shard_map/ppermute | solution.py:21
  67.6 11.0 %collective-permute-start.11 = (bf16[4,16,1024]{2,1,0:T(8,128)(2,1)S(1)}, bf16[4,16,1024]{2,1,0:T(8,128)(2,1)S(1)}, u32[]{:S(2)}, u32[]{:S(2)}) collective-permute-start(bf16[4,16,1024]{2,1,0:T(8,128)(2,1)S(1)} %get-tuple-element.84), channel_id=1, source_target_pairs={{0,6},{2,4},{4,2},{6,0},{8,14},{10,12},{12,10},{14,8},{16,22},{18,... | collective-permute-start | bytes 393224 | tf_op jit(solution)/shard_map/ppermute | solution.py:21
  234.8 10.0 %collective-permute-start.12 = (f32[4,16,1040]{2,1,0:T(8,128)S(1)}, f32[4,16,1040]{2,1,0:T(8,128)S(1)}, u32[]{:S(2)}, u32[]{:S(2)}) collective-permute-start(f32[4,16,1040]{2,1,0:T(8,128)S(1)} %get-tuple-element.47), channel_id=1, source_target_pairs={{0,2},{2,0},{4,6},{6,4},{8,10},{10,8},{12,14},{14,12},{16,18},{18,... | collective-permute-start | bytes 798728 | tf_op jit(solution)/shard_map/ppermute | solution.py:21
  236.0 12.9 %collective-permute-start.13 = (f32[4,16,1040]{2,1,0:T(8,128)S(1)}, f32[4,16,1040]{2,1,0:T(8,128)S(1)}, u32[]{:S(2)}, u32[]{:S(2)}) collective-permute-start(f32[4,16,1040]{2,1,0:T(8,128)S(1)} %get-tuple-element.46), channel_id=1, source_target_pairs={{0,4},{2,6},{4,0},{6,2},{8,12},{10,14},{12,8},{14,10},{16,20},{18,... | collective-permute-start | bytes 798728 | tf_op jit(solution)/shard_map/ppermute | solution.py:21
  236.9 13.5 %collective-permute-start.14 = (f32[4,16,1040]{2,1,0:T(8,128)S(1)}, f32[4,16,1040]{2,1,0:T(8,128)S(1)}, u32[]{:S(2)}, u32[]{:S(2)}) collective-permute-start(f32[4,16,1040]{2,1,0:T(8,128)S(1)} %get-tuple-element.45), channel_id=1, source_target_pairs={{0,6},{2,4},{4,2},{6,0},{8,14},{10,12},{12,10},{14,8},{16,22},{18,... | collective-permute-start | bytes 798728 | tf_op jit(solution)/shard_map/ppermute | solution.py:21
  286.1 15.1 %collective-permute-start.26 = (f32[128,256]{1,0:T(8,128)S(1)}, f32[128,256]{1,0:T(8,128)S(1)}, u32[]{:S(2)}, u32[]{:S(2)}) collective-permute-start(f32[128,256]{1,0:T(8,128)S(1)} %fusion.33), channel_id=1, source_target_pairs={{0,8},{2,10},{4,12},{6,14},{8,0},{10,2},{12,4},{14,6},{16,24},{18,... | collective-permute-start | bytes 393224 | tf_op jit(solution)/shard_map/ppermute | solution.py:21
  286.2 15.0 %collective-permute-start.27 = (f32[128,256]{1,0:T(8,128)S(1)}, f32[128,256]{1,0:T(8,128)S(1)}, u32[]{:S(2)}, u32[]{:S(2)}) collective-permute-start(f32[128,256]{1,0:T(8,128)S(1)} %fusion.33), channel_id=1, source_target_pairs={{0,16},{2,18},{4,20},{6,22},{8,24},{10,26},{12,28},{14,30},{16,0},... | collective-permute-start | bytes 393224 | tf_op jit(solution)/shard_map/ppermute | solution.py:21
  288.7 12.6 %collective-permute-start.28 = (f32[128,256]{1,0:T(8,128)S(1)}, f32[128,256]{1,0:T(8,128)S(1)}, u32[]{:S(2)}, u32[]{:S(2)}) collective-permute-start(f32[128,256]{1,0:T(8,128)S(1)} %fusion.33), channel_id=1, source_target_pairs={{0,24},{2,26},{4,28},{6,30},{8,16},{10,18},{12,20},{14,22},{16,8},... | collective-permute-start | bytes 393224 | tf_op jit(solution)/shard_map/ppermute | solution.py:21
  290.6 10.6 %collective-permute-start.34 = (s32[16]{0:T(128)S(1)}, s32[16]{0:T(128)S(1)}, u32[]{:S(2)}, u32[]{:S(2)}) collective-permute-start(s32[16]{0:T(128)S(1)} %bitcast.400), channel_id=1, source_target_pairs={{0,16},{2,18},{4,20},{6,22},{8,24},{10,26},{12,28},{14,30},{16,0},... | collective-permute-start | bytes 200 | tf_op jit(solution)/shard_map/ppermute | solution.py:21
  301.4 28.7 %collective-permute-start.29 = (f32[4,128,256]{2,1,0:T(8,128)S(1)}, f32[4,128,256]{2,1,0:T(8,128)S(1)}, u32[]{:S(2)}, u32[]{:S(2)}) collective-permute-start(f32[4,128,256]{2,1,0:T(8,128)S(1)} %get-tuple-element.56), channel_id=1, source_target_pairs={{0,2},{2,0},{4,6},{6,4},{8,10},{10,8},{12,14},{14,12},{16,18},{18,... | collective-permute-start | bytes 1572872 | tf_op jit(solution)/shard_map/ppermute | solution.py:21
  302.1 28.1 %collective-permute-start.30 = (f32[4,128,256]{2,1,0:T(8,128)S(1)}, f32[4,128,256]{2,1,0:T(8,128)S(1)}, u32[]{:S(2)}, u32[]{:S(2)}) collective-permute-start(f32[4,128,256]{2,1,0:T(8,128)S(1)} %get-tuple-element.56), channel_id=1, source_target_pairs={{0,4},{2,6},{4,0},{6,2},{8,12},{10,14},{12,8},{14,10},{16,20},{18,... | collective-permute-start | bytes 1572872 | tf_op jit(solution)/shard_map/ppermute | solution.py:21
  303.2 26.9 %collective-permute-start.31 = (f32[4,128,256]{2,1,0:T(8,128)S(1)}, f32[4,128,256]{2,1,0:T(8,128)S(1)}, u32[]{:S(2)}, u32[]{:S(2)}) collective-permute-start(f32[4,128,256]{2,1,0:T(8,128)S(1)} %get-tuple-element.56), channel_id=1, source_target_pairs={{0,6},{2,4},{4,2},{6,0},{8,14},{10,12},{12,10},{14,8},{16,22},{18,... | collective-permute-start | bytes 1572872 | tf_op jit(solution)/shard_map/ppermute | solution.py:21
  305.0 20.6 %collective-permute-start.36 = (s32[4,16]{1,0:T(4,128)S(1)}, s32[4,16]{1,0:T(4,128)S(1)}, u32[]{:S(2)}, u32[]{:S(2)}) collective-permute-start(s32[4,16]{1,0:T(4,128)S(1)} %get-tuple-element.115), channel_id=1, source_target_pairs={{0,2},{2,0},{4,6},{6,4},{8,10},{10,8},{12,14},{14,12},{16,18},{18,... | collective-permute-start | bytes 776 | tf_op jit(solution)/shard_map/ppermute | solution.py:21
  305.6 21.2 %collective-permute-start.37 = (s32[4,16]{1,0:T(4,128)S(1)}, s32[4,16]{1,0:T(4,128)S(1)}, u32[]{:S(2)}, u32[]{:S(2)}) collective-permute-start(s32[4,16]{1,0:T(4,128)S(1)} %get-tuple-element.115), channel_id=1, source_target_pairs={{0,4},{2,6},{4,0},{6,2},{8,12},{10,14},{12,8},{14,10},{16,20},{18,... | collective-permute-start | bytes 776 | tf_op jit(solution)/shard_map/ppermute | solution.py:21
  (32 other events, 189.5 us)
Sparse Core Ops, SparseCore 0:
  10.1 204.2 all-gather.1

commit v4 on v2

--- a/solution.py
+++ b/solution.py
@@ -97,7 +97,8 @@
     in_rows = query_weight.shape[0]
     col_block = out_weight.shape[1]
 
-    kv_weight = lax.all_gather(keyval_weight, "ctx", axis=0, tiled=True)
+    k_weight = lax.all_gather(keyval_weight[:, 0], "ctx", axis=0, tiled=True)
+    v_weight = _all_gather(keyval_weight[:, 1], "ctx", n_ctx).reshape(width, head_columns)
 
     rows_here = jnp.take(activations, mask_positions[0], axis=0)
     row_blocks = lax.all_to_all(rows_here, "ctx", 1, 0, tiled=True)
@@ -110,11 +111,16 @@
     wanted = _all_gather(targets[0], "ctx", n_ctx).reshape(total_rows)
     out_full = _all_gather(out_weight, "head", n_head).reshape(n_head * head_columns, col_block)
 
-    keyval = jnp.einsum(
-        "td,djc->tjc", activations, kv_weight, preferred_element_type=jnp.float32
-    ).astype(jnp.bfloat16)
-    key_heads = keyval[:, 0].reshape(block_len, heads_here, HDIM)
-    value_heads = keyval[:, 1].reshape(block_len, heads_here, HDIM)
+    key_heads = (
+        jnp.dot(activations, k_weight, preferred_element_type=jnp.float32)
+        .astype(jnp.bfloat16)
+        .reshape(block_len, heads_here, HDIM)
+    )
+    value_heads = (
+        jnp.dot(activations, v_weight, preferred_element_type=jnp.float32)
+        .astype(jnp.bfloat16)
+        .reshape(block_len, heads_here, HDIM)
+    )
     query_heads = queries.reshape(total_rows, heads_here, HDIM)
     scores = jnp.einsum(
         "rhc,thc->hrt", query_heads, key_heads, preferred_element_type=jnp.float32

time: 374 us -> 432 us (1.16)
  starting transfers between devices: 72.5 us -> 108 us
  waiting for transfers between devices: 231 us -> 248 us
  other arithmetic: 8.3 us -> 15.7 us
    ppermute x52 -> x58, waiting for transfers between devices: 83.5 us -> 242 us  [_swap(): return lax.ppermute(x, axis, [(j, j ^ k) for j in range(n)])]
    all_gather x1, waiting for transfers between devices: 138 us -> 0.02 us  [shards(): k_weight = lax.all_gather(keyval_weight[:, 0], 'ctx', axis=0, tiled=True)]
    ppermute x52 -> x58, starting transfers between devices: 64.2 us -> 99.6 us  [_swap(): return lax.ppermute(x, axis, [(j, j ^ k) for j in range(n)])]
    another operation x16 -> x19, other arithmetic: 3.13 us -> 8.89 us  [_all_gather(): stacked = jnp.stack(got)]
    dot_general x1 -> x2, matrix products: 12.5 us -> 12.4 us  [the longest x1 8.45 us: shards(): jnp.dot(activations, k_weight, preferred_element_type=jnp.float32)]
  transfers between devices with their start and end apart: 54 -> 60, of which waited for: 43 -> 41; matrix products, arithmetic and copies ran while one was open for 2% -> 5% of each run, Pallas kernels for 0% -> 0%
where the time goes in v4:
time: 432 us; the launch traced here: 431 us
  waiting for transfers between devices  248 us (57%)
  starting transfers between devices  108 us (25%)
  matrix products  23.3 us (5%)
  local copies, waits for them, and re-layouts  21.7 us (5%)
  other arithmetic  15.7 us (4%)
  between operations  15 us (3%)
    ppermute x58, waiting for transfers between devices, _swap(): return lax.ppermute(x, axis, [(j, j ^ k) for j in range(n)])  242 us
    ppermute x58, starting transfers between devices, _swap(): return lax.ppermute(x, axis, [(j, j ^ k) for j in range(n)])  99.6 us
    another operation x19, other arithmetic, _all_gather(): stacked = jnp.stack(got)  8.89 us
  transfers between devices with their start and end apart: 60, of which 41 were waited for; matrix products, arithmetic and copies ran while one was open for 5% of the time, Pallas kernels for 0%

profile of v4, /device:TPU:0, one launch (start us, length us, event | category | flops | bytes accessed | tf_op | source)
XLA Modules:
  0.0 431.3 jit_solution(13932741564283654434)
XLA Ops:
  6.5 3.3 fusion.131
  10.9 3.3 gather_fusion
  14.9 8.3 %all-to-all-start = ((bf16[16,16,256]{2,0,1:T(8,128)(2,1)}), bf16[16,16,256]{2,0,1:T(8,128)(2,1)S(1)}, u32[]{:S(2)}, u32[]{:S(2)}) async-start(bf16[16,16,256]{2,0,1:T(8,128)(2,1)} %bitcast_select_fusion), calls=%async_computation | async-start | bytes 262144 | tf_op jit(solution)/shard_map/all_to_all | solution.py:104
  27.9 5.7 %all-to-all-done = bf16[16,16,256]{2,0,1:T(8,128)(2,1)S(1)} async-done(((bf16[16,16,256]{2,0,1:T(8,128)(2,1)}), bf16[16,16,256]{2,0,1:T(8,128)(2,1)S(1)}, u32[]{:S(2)}, u32[]{:S(2)}) %all-to-all-start) | async-done | bytes 131104 | tf_op jit(solution)/shard_map/all_to_all | solution.py:104
  36.2 24.9 %collective-permute-done = bf16[256,1024]{1,0:T(8,128)(2,1)S(1)} collective-permute-done((bf16[256,1024]{1,0:T(8,128)(2,1)S(1)}, bf16[256,1024]{1,0:T(8,128)(2,1)S(1)}, u32[]{:S(2)}, u32[]{:S(2)}) %collective-permute-start) | collective-permute-done | bytes 524320 | tf_op jit(solution)/shard_map/ppermute | solution.py:21
  61.1 4.6 %collective-permute-done.1 = bf16[256,1024]{1,0:T(8,128)(2,1)S(1)} collective-permute-done((bf16[256,1024]{1,0:T(8,128)(2,1)S(1)}, bf16[256,1024]{1,0:T(8,128)(2,1)S(1)}, u32[]{:S(2)}, u32[]{:S(2)}) %collective-permute-start.1) | collective-permute-done | bytes 524320 | tf_op jit(solution)/shard_map/ppermute | solution.py:21
  65.7 19.7 %collective-permute-done.2 = bf16[256,1024]{1,0:T(8,128)(2,1)} collective-permute-done((bf16[256,1024]{1,0:T(8,128)(2,1)S(1)}, bf16[256,1024]{1,0:T(8,128)(2,1)}, u32[]{:S(2)}, u32[]{:S(2)}) %collective-permute-start.2) | collective-permute-done | bytes 524320 | tf_op jit(solution)/shard_map/ppermute | solution.py:21
  94.9 127.6 %collective-permute-done.7 = f32[4,16,1024]{2,1,0:T(8,128)} collective-permute-done((f32[4,16,1024]{2,1,0:T(8,128)}, f32[4,16,1024]{2,1,0:T(8,128)}, u32[]{:S(2)}, u32[]{:S(2)}) %collective-permute-start.7) | collective-permute-done | bytes 262176 | tf_op jit(solution)/shard_map/ppermute | solution.py:21
  223.6 24.2 %collective-permute-start.10 = (f32[1,16,1024]{2,1,0:T(8,128)S(1)}, f32[1,16,1024]{2,1,0:T(8,128)S(1)}, u32[]{:S(2)}, u32[]{:S(2)}) collective-permute-start(f32[1,16,1024]{2,1,0:T(8,128)S(1)} %get-tuple-element.88), channel_id=1, source_target_pairs={{0,16},{2,18},{4,20},{6,22},{8,24},{10,26},{12,28},{14,30},{16,0},... | collective-permute-start | bytes 196616 | tf_op jit(solution)/shard_map/ppermute | solution.py:21
  262.5 2.8 collective-permute-done.14
  272.6 3.7 collective-permute-done.17
  276.7 3.8 pad_maximum_fusion
  283.9 3.9 fusion.17
  287.9 8.5 %fusion.14 = bf16[56,8,8,128]{3,2,1,0:T(8,128)(2,1)S(1)} fusion(bf16[448,4096]{1,0:T(8,128)(2,1)} %param.9, bf16[4096,1,1024]{2,0,1:T(8,128)(2,1)} %all-gather.3.cloned.1.call-done), kind=kOutput, calls=%fused_computation.28 | convolution fusion | flops 3758555136 | bytes 12976128 | tf_op jit(solution)/shard_map/dot_general | solution.py:115
  306.9 3.4 collective-permute-done.19
  320.0 2.7 collective-permute-done.23
  329.4 3.2 collective-permute-done.26
  355.4 3.4 collective-permute-done.37
  364.3 3.2 collective-permute-done.40
  371.2 2.9 collective-permute-done.41
  374.1 3.8 collective-permute-done.42
  383.7 3.5 collective-permute-done.47
  394.7 2.9 copy.137
  397.5 8.6 %fusion.135 = (f32[256]{0:T(256)S(1)}, f32[256,1984]{0,1:T(8,128)S(1)}) fusion(bf16[256,4096]{1,0:T(8,128)(2,1)} %bitcast.379, bf16[1984,4096]{1,0:T(8,128)(2,1)} %param.14), kind=kOutput, calls=%fused_computation.325 | convolution fusion | flops 4161257216 | bytes 20382720 | tf_op jit(solution)/shard_map/dot_general | solution.py:172
  (258 shorter events, 134.5 us)
Async XLA Ops:
  6.5 281.4 %all-gather.3.cloned.1.call-start = ((), (), s32[]{:S(2)}) async-start(), calls=%async_computation.1 | async-start | bytes 8912896 | tf_op jit(solution)/shard_map/all_gather | solution.py:100
  14.9 18.7 %all-to-all-start = ((bf16[16,16,256]{2,0,1:T(8,128)(2,1)}), bf16[16,16,256]{2,0,1:T(8,128)(2,1)S(1)}, u32[]{:S(2)}, u32[]{:S(2)}) async-start(bf16[16,16,256]{2,0,1:T(8,128)(2,1)} %bitcast_select_fusion), calls=%async_computation | async-start | bytes 262144 | tf_op jit(solution)/shard_map/all_to_all | solution.py:104
  23.4 37.7 %collective-permute-start = (bf16[256,1024]{1,0:T(8,128)(2,1)S(1)}, bf16[256,1024]{1,0:T(8,128)(2,1)S(1)}, u32[]{:S(2)}, u32[]{:S(2)}) collective-permute-start(bf16[256,1024]{1,0:T(8,128)(2,1)S(1)} %bitcast.383), channel_id=1, source_target_pairs={{0,8},{2,10},{4,12},{6,14},{8,0},{10,2},{12,4},{14,6},{16,24},{18,... | collective-permute-start | bytes 1572872 | tf_op jit(solution)/shard_map/ppermute | solution.py:21
  25.4 40.3 %collective-permute-start.1 = (bf16[256,1024]{1,0:T(8,128)(2,1)S(1)}, bf16[256,1024]{1,0:T(8,128)(2,1)S(1)}, u32[]{:S(2)}, u32[]{:S(2)}) collective-permute-start(bf16[256,1024]{1,0:T(8,128)(2,1)S(1)} %bitcast.384), channel_id=1, source_target_pairs={{0,16},{2,18},{4,20},{6,22},{8,24},{10,26},{12,28},{14,30},{16,0},... | collective-permute-start | bytes 1572872 | tf_op jit(solution)/shard_map/ppermute | solution.py:21
  27.8 57.6 %collective-permute-start.2 = (bf16[256,1024]{1,0:T(8,128)(2,1)S(1)}, bf16[256,1024]{1,0:T(8,128)(2,1)}, u32[]{:S(2)}, u32[]{:S(2)}) collective-permute-start(bf16[256,1024]{1,0:T(8,128)(2,1)S(1)} %bitcast.385), channel_id=1, source_target_pairs={{0,24},{2,26},{4,28},{6,30},{8,16},{10,18},{12,20},{14,22},{16,8},... | collective-permute-start | bytes 1572872 | tf_op jit(solution)/shard_map/ppermute | solution.py:21
  34.8 58.7 %collective-permute-start.6 = (f32[4,16,1024]{2,1,0:T(8,128)S(1)}, f32[4,16,1024]{2,1,0:T(8,128)S(1)}, u32[]{:S(2)}, u32[]{:S(2)}) collective-permute-start(f32[4,16,1024]{2,1,0:T(8,128)S(1)} %get-tuple-element.62), channel_id=1, source_target_pairs={{0,2},{2,0},{4,6},{6,4},{8,10},{10,8},{12,14},{14,12},{16,18},{18,... | collective-permute-start | bytes 786440 | tf_op jit(solution)/shard_map/ppermute | solution.py:21
  88.5 188.2 %collective-permute-start.3 = (bf16[4,256,1024]{2,1,0:T(8,128)(2,1)}, bf16[4,256,1024]{2,1,0:T(8,128)(2,1)}, u32[]{:S(2)}, u32[]{:S(2)}) collective-permute-start(bf16[4,256,1024]{2,1,0:T(8,128)(2,1)} %get-tuple-element.43), channel_id=1, source_target_pairs={{0,2},{2,0},{4,6},{6,4},{8,10},{10,8},{12,14},{14,12},{16,18},{18,... | collective-permute-start | bytes 6291464 | tf_op jit(solution)/shard_map/ppermute | solution.py:21
  90.0 186.7 %collective-permute-start.4 = (bf16[4,256,1024]{2,1,0:T(8,128)(2,1)}, bf16[4,256,1024]{2,1,0:T(8,128)(2,1)}, u32[]{:S(2)}, u32[]{:S(2)}) collective-permute-start(bf16[4,256,1024]{2,1,0:T(8,128)(2,1)} %get-tuple-element.43), channel_id=1, source_target_pairs={{0,4},{2,6},{4,0},{6,2},{8,12},{10,14},{12,8},{14,10},{16,20},{18,... | collective-permute-start | bytes 6291464 | tf_op jit(solution)/shard_map/ppermute | solution.py:21
  91.4 185.2 %collective-permute-start.5 = (bf16[4,256,1024]{2,1,0:T(8,128)(2,1)}, bf16[4,256,1024]{2,1,0:T(8,128)(2,1)}, u32[]{:S(2)}, u32[]{:S(2)}) collective-permute-start(bf16[4,256,1024]{2,1,0:T(8,128)(2,1)} %get-tuple-element.43), channel_id=1, source_target_pairs={{0,6},{2,4},{4,2},{6,0},{8,14},{10,12},{12,10},{14,8},{16,22},{18,... | collective-permute-start | bytes 6291464 | tf_op jit(solution)/shard_map/ppermute | solution.py:21
  92.0 130.5 %collective-permute-start.7 = (f32[4,16,1024]{2,1,0:T(8,128)}, f32[4,16,1024]{2,1,0:T(8,128)}, u32[]{:S(2)}, u32[]{:S(2)}) collective-permute-start(f32[4,16,1024]{2,1,0:T(8,128)} %get-tuple-element.64), channel_id=1, source_target_pairs={{0,4},{2,6},{4,0},{6,2},{8,12},{10,14},{12,8},{14,10},{16,20},{18,... | collective-permute-start | bytes 786440 | tf_op jit(solution)/shard_map/ppermute | solution.py:21
  93.5 129.0 %collective-permute-start.8 = (f32[4,16,1024]{2,1,0:T(8,128)}, f32[4,16,1024]{2,1,0:T(8,128)}, u32[]{:S(2)}, u32[]{:S(2)}) collective-permute-start(f32[4,16,1024]{2,1,0:T(8,128)} %get-tuple-element.63), channel_id=1, source_target_pairs={{0,6},{2,4},{4,2},{6,0},{8,14},{10,12},{12,10},{14,8},{16,22},{18,... | collective-permute-start | bytes 786440 | tf_op jit(solution)/shard_map/ppermute | solution.py:21
  223.6 27.1 %collective-permute-start.10 = (f32[1,16,1024]{2,1,0:T(8,128)S(1)}, f32[1,16,1024]{2,1,0:T(8,128)S(1)}, u32[]{:S(2)}, u32[]{:S(2)}) collective-permute-start(f32[1,16,1024]{2,1,0:T(8,128)S(1)} %get-tuple-element.88), channel_id=1, source_target_pairs={{0,16},{2,18},{4,20},{6,22},{8,24},{10,26},{12,28},{14,30},{16,0},... | collective-permute-start | bytes 196616 | tf_op jit(solution)/shard_map/ppermute | solution.py:21
  247.8 6.5 %collective-permute-start.11 = (f32[1,16,1024]{2,1,0:T(8,128)S(1)}, f32[1,16,1024]{2,1,0:T(8,128)S(1)}, u32[]{:S(2)}, u32[]{:S(2)}) collective-permute-start(f32[1,16,1024]{2,1,0:T(8,128)S(1)} %get-tuple-element.87), channel_id=1, source_target_pairs={{0,24},{2,26},{4,28},{6,30},{8,16},{10,18},{12,20},{14,22},{16,8},... | collective-permute-start | bytes 196616 | tf_op jit(solution)/shard_map/ppermute | solution.py:21
  265.7 6.9 %collective-permute-start.16 = (bf16[4,16,1024]{2,1,0:T(8,128)(2,1)S(1)}, bf16[4,16,1024]{2,1,0:T(8,128)(2,1)S(1)}, u32[]{:S(2)}, u32[]{:S(2)}) collective-permute-start(bf16[4,16,1024]{2,1,0:T(8,128)(2,1)S(1)} %get-tuple-element.96), channel_id=1, source_target_pairs={{0,4},{2,6},{4,0},{6,2},{8,12},{10,14},{12,8},{14,10},{16,20},{18,... | collective-permute-start | bytes 393224 | tf_op jit(solution)/shard_map/ppermute | solution.py:21
  300.1 6.8 %collective-permute-start.18 = (f32[4,16,1040]{2,1,0:T(8,128)S(1)}, f32[4,16,1040]{2,1,0:T(8,128)S(1)}, u32[]{:S(2)}, u32[]{:S(2)}) collective-permute-start(f32[4,16,1040]{2,1,0:T(8,128)S(1)} %get-tuple-element.51), channel_id=1, source_target_pairs={{0,2},{2,0},{4,6},{6,4},{8,10},{10,8},{12,14},{14,12},{16,18},{18,... | collective-permute-start | bytes 798728 | tf_op jit(solution)/shard_map/ppermute | solution.py:21
  301.3 8.9 %collective-permute-start.19 = (f32[4,16,1040]{2,1,0:T(8,128)S(1)}, f32[4,16,1040]{2,1,0:T(8,128)S(1)}, u32[]{:S(2)}, u32[]{:S(2)}) collective-permute-start(f32[4,16,1040]{2,1,0:T(8,128)S(1)} %get-tuple-element.50), channel_id=1, source_target_pairs={{0,4},{2,6},{4,0},{6,2},{8,12},{10,14},{12,8},{14,10},{16,20},{18,... | collective-permute-start | bytes 798728 | tf_op jit(solution)/shard_map/ppermute | solution.py:21
  302.9 9.2 %collective-permute-start.20 = (f32[4,16,1040]{2,1,0:T(8,128)S(1)}, f32[4,16,1040]{2,1,0:T(8,128)S(1)}, u32[]{:S(2)}, u32[]{:S(2)}) collective-permute-start(f32[4,16,1040]{2,1,0:T(8,128)S(1)} %get-tuple-element.49), channel_id=1, source_target_pairs={{0,6},{2,4},{4,2},{6,0},{8,14},{10,12},{12,10},{14,8},{16,22},{18,... | collective-permute-start | bytes 798728 | tf_op jit(solution)/shard_map/ppermute | solution.py:21
  316.5 6.2 %collective-permute-start.23 = (f32[1,16,1040]{2,1,0:T(8,128)S(1)}, f32[1,16,1040]{2,1,0:T(8,128)S(1)}, u32[]{:S(2)}, u32[]{:S(2)}) collective-permute-start(f32[1,16,1040]{2,1,0:T(8,128)S(1)} %get-tuple-element.78), channel_id=1, source_target_pairs={{0,24},{2,26},{4,28},{6,30},{8,16},{10,18},{12,20},{14,22},{16,8},... | collective-permute-start | bytes 199688 | tf_op jit(solution)/shard_map/ppermute | solution.py:21
  333.3 5.9 %collective-permute-start.28 = (bf16[4,16,1024]{2,1,0:T(8,128)(2,1)S(1)}, bf16[4,16,1024]{2,1,0:T(8,128)(2,1)S(1)}, u32[]{:S(2)}, u32[]{:S(2)}) collective-permute-start(bf16[4,16,1024]{2,1,0:T(8,128)(2,1)S(1)} %get-tuple-element.90), channel_id=1, source_target_pairs={{0,4},{2,6},{4,0},{6,2},{8,12},{10,14},{12,8},{14,10},{16,20},{18,... | collective-permute-start | bytes 393224 | tf_op jit(solution)/shard_map/ppermute | solution.py:21
  361.4 6.1 %collective-permute-start.40 = (bf16[128,256]{1,0:T(8,128)(2,1)S(1)}, bf16[128,256]{1,0:T(8,128)(2,1)S(1)}, u32[]{:S(2)}, u32[]{:S(2)}) collective-permute-start(bf16[128,256]{1,0:T(8,128)(2,1)S(1)} %multiply_convert_fusion), channel_id=1, source_target_pairs={{0,24},{2,26},{4,28},{6,30},{8,16},{10,18},{12,20},{14,22},{16,8},... | collective-permute-start | bytes 196616 | tf_op jit(solution)/shard_map/ppermute | solution.py:21
  367.6 6.5 %collective-permute-start.41 = (bf16[4,128,256]{2,1,0:T(8,128)(2,1)S(1)}, bf16[4,128,256]{2,1,0:T(8,128)(2,1)S(1)}, u32[]{:S(2)}, u32[]{:S(2)}) collective-permute-start(bf16[4,128,256]{2,1,0:T(8,128)(2,1)S(1)} %get-tuple-element.81), channel_id=1, source_target_pairs={{0,2},{2,0},{4,6},{6,4},{8,10},{10,8},{12,14},{14,12},{16,18},{18,... | collective-permute-start | bytes 786440 | tf_op jit(solution)/shard_map/ppermute | solution.py:21
  368.8 9.2 %collective-permute-start.42 = (bf16[4,128,256]{2,1,0:T(8,128)(2,1)S(1)}, bf16[4,128,256]{2,1,0:T(8,128)(2,1)S(1)}, u32[]{:S(2)}, u32[]{:S(2)}) collective-permute-start(bf16[4,128,256]{2,1,0:T(8,128)(2,1)S(1)} %get-tuple-element.81), channel_id=1, source_target_pairs={{0,4},{2,6},{4,0},{6,2},{8,12},{10,14},{12,8},{14,10},{16,20},{18,... | collective-permute-start | bytes 786440 | tf_op jit(solution)/shard_map/ppermute | solution.py:21
  370.3 7.7 %collective-permute-start.43 = (bf16[4,128,256]{2,1,0:T(8,128)(2,1)S(1)}, bf16[4,128,256]{2,1,0:T(8,128)(2,1)S(1)}, u32[]{:S(2)}, u32[]{:S(2)}) collective-permute-start(bf16[4,128,256]{2,1,0:T(8,128)(2,1)S(1)} %get-tuple-element.81), channel_id=1, source_target_pairs={{0,6},{2,4},{4,2},{6,0},{8,14},{10,12},{12,10},{14,8},{16,22},{18,... | collective-permute-start | bytes 786440 | tf_op jit(solution)/shard_map/ppermute | solution.py:21
  379.0 14.7 %collective-permute-start.44 = (bf16[128,4096]{0,1:T(8,128)(2,1)S(1)}, bf16[128,4096]{0,1:T(8,128)(2,1)S(1)}, u32[]{:S(2)}, u32[]{:S(2)}) collective-permute-start(bf16[128,4096]{0,1:T(8,128)(2,1)S(1)} %bitcast.373), channel_id=1, source_target_pairs={{0,1},{1,0},{2,3},{3,2},{4,5},{5,4},{6,7},{7,6},{8,9},{9,8},{10,11... | collective-permute-start | bytes 3145736 | tf_op jit(solution)/shard_map/ppermute | solution.py:21
  (42 other events, 236.2 us)
Sparse Core Ops, SparseCore 0:
  11.0 227.3 all-gather.2

commit v5 on v2

--- a/solution.py
+++ b/solution.py
@@ -108,6 +108,7 @@
     queries = _all_gather(own_q, "ctx", n_ctx).reshape(total_rows, head_columns)
 
     wanted = _all_gather(targets[0], "ctx", n_ctx).reshape(total_rows)
+    other_vocab = _swap(vocab_weight, "head", n_head, 1) if n_head == 2 else None
     out_full = _all_gather(out_weight, "head", n_head).reshape(n_head * head_columns, col_block)
 
     keyval = jnp.einsum(
@@ -161,27 +162,44 @@
         branch * lax.rsqrt(sumsq / width + 1e-06)[:, None] * gain
     ).astype(jnp.bfloat16)
     hidden = _all_gather(hidden, "ctx", n_ctx).transpose(1, 0, 2).reshape(share, width)
-    hidden = _all_gather(hidden, "head", n_head).reshape(total_rows, width)
-
-    logits = lax.dot_general(
-        hidden, vocab_weight, (((1,), (1,)), ((), ())), preferred_element_type=jnp.float32
-    )
-    vocab_start = lax.axis_index(("ctx", "head")) * vocab_weight.shape[0]
-    vocab_ids = vocab_start + jnp.arange(vocab_weight.shape[0], dtype=jnp.int32)
-    local_max = jnp.max(logits, axis=1)
-    expsum = jnp.sum(jnp.exp(logits - local_max[:, None]), axis=1)
-    picked = jnp.sum(jnp.where(vocab_ids[None, :] == wanted[:, None], logits, 0.0), axis=1)
-    stats = jnp.stack([local_max, expsum, picked])
-
     def lse_combine(a, b):
         top = jnp.maximum(a[0], b[0])
         total = a[1] * jnp.exp(a[0] - top) + b[1] * jnp.exp(b[0] - top)
         return jnp.stack([top, total, a[2] + b[2]])
 
-    stats = _all_reduce(stats, "head", n_head, lse_combine)
-    stats = _all_reduce(stats, "ctx", n_ctx, lse_combine)
-    losses = (stats[0] + jnp.log(stats[1]) - stats[2]).reshape(n_ctx, slot_count)
-    block_losses = lax.dynamic_slice_in_dim(losses, lax.axis_index("ctx"), 1, 0)[0]
+    def shard_stats(rows, shard, shard_index, row_targets):
+        logits = lax.dot_general(
+            rows, shard, (((1,), (1,)), ((), ())), preferred_element_type=jnp.float32
+        )
+        ids = shard_index * shard.shape[0] + jnp.arange(shard.shape[0], dtype=jnp.int32)
+        top = jnp.max(logits, axis=1)
+        total = jnp.sum(jnp.exp(logits - top[:, None]), axis=1)
+        picked = jnp.sum(jnp.where(ids[None, :] == row_targets[:, None], logits, 0.0), axis=1)
+        return jnp.stack([top, total, picked])
+
+    flat_index = lax.axis_index(("ctx", "head"))
+    ctx_idx = lax.axis_index("ctx")
+    if other_vocab is not None:
+        share_targets = lax.dynamic_slice_in_dim(wanted, head_idx * share, share, 0)
+        stats = lse_combine(
+            shard_stats(hidden, vocab_weight, flat_index, share_targets),
+            shard_stats(hidden, other_vocab, flat_index + 1 - 2 * head_idx, share_targets),
+        )
+        stats = _all_reduce(stats, "ctx", n_ctx, lse_combine)
+        share_losses = stats[0] + jnp.log(stats[1]) - stats[2]
+        owner = (ctx_idx * slot_count) // share
+        mine = lax.dynamic_slice_in_dim(
+            share_losses, ctx_idx * slot_count - owner * share, slot_count, 0
+        )
+        theirs = _swap(mine, "head", n_head, 1)
+        block_losses = jnp.where(owner == head_idx, mine, theirs)
+    else:
+        hidden = _all_gather(hidden, "head", n_head).reshape(total_rows, width)
+        stats = shard_stats(hidden, vocab_weight, flat_index, wanted)
+        stats = _all_reduce(stats, "head", n_head, lse_combine)
+        stats = _all_reduce(stats, "ctx", n_ctx, lse_combine)
+        losses = (stats[0] + jnp.log(stats[1]) - stats[2]).reshape(n_ctx, slot_count)
+        block_losses = lax.dynamic_slice_in_dim(losses, ctx_idx, 1, 0)[0]
     active = jnp.arange(slot_count, dtype=jnp.int32) < mask_count[0]
     return jnp.where(active, block_losses, jnp.zeros_like(block_losses))[None, :]
 

time: 374 us -> 368 us (0.984)
  matrix products: 26.5 us -> 33.7 us
  waiting for transfers between devices: 231 us -> 224 us
    dot_general x1 -> x2, matrix products: 8.63 us -> 15.9 us  [shard_stats(): lax.dot_general(rows, shard, (((1,), (1,)), ((), ())), preferred_element_...]
    ppermute x52, waiting for transfers between devices: 83.5 us -> 77.8 us  [_swap(): return lax.ppermute(x, axis, [(j, j ^ k) for j in range(n)])]
  transfers between devices with their start and end apart: 54 -> 54, of which waited for: 43 -> 34; matrix products, arithmetic and copies ran while one was open for 2% -> 12% of each run, Pallas kernels for 0% -> 0%
where the time goes in v5:
time: 368 us
  waiting for transfers between devices  224 us (61%)
  starting transfers between devices  70.1 us (19%)
  matrix products  33.7 us (9%)
  local copies, waits for them, and re-layouts  17.2 us (5%)
  between operations  14.9 us (4%)
  other arithmetic  7.51 us (2%)
    all_gather x1, waiting for transfers between devices, shards(): kv_weight = lax.all_gather(keyval_weight, 'ctx', axis=0, tiled=True)  136 us
    ppermute x52, waiting for transfers between devices, _swap(): return lax.ppermute(x, axis, [(j, j ^ k) for j in range(n)])  77.8 us
    ppermute x52, starting transfers between devices, _swap(): return lax.ppermute(x, axis, [(j, j ^ k) for j in range(n)])  62.3 us
    dot_general x2, matrix products, shard_stats(): lax.dot_general(rows, shard, (((1,), (1,)), ((), ())), preferred_element_...  15.9 us
    dot_general x1, matrix products, shards(): jnp.einsum('td,djc->tjc', activations, kv_weight, preferred_element_type=...  12.5 us
    all_to_all x1, waiting for transfers between devices, shards(): row_blocks = lax.all_to_all(rows_here, 'ctx', 1, 0, tiled=True)  9.96 us
    all_to_all x1, starting transfers between devices, shards(): row_blocks = lax.all_to_all(rows_here, 'ctx', 1, 0, tiled=True)  7.88 us
  transfers between devices with their start and end apart: 54, of which 34 were waited for; matrix products, arithmetic and copies ran while one was open for 12% of the time, Pallas kernels for 0%

profile of v5, /device:TPU:0, one launch (start us, length us, event | category | flops | bytes accessed | tf_op | source)
XLA Modules:
  0.0 367.6 jit_solution(12064347277832755258)
XLA Ops:
  10.3 3.3 gather_fusion
  14.3 7.9 %all-to-all-start = ((bf16[16,16,256]{2,0,1:T(8,128)(2,1)}), bf16[16,16,256]{2,0,1:T(8,128)(2,1)S(1)}, u32[]{:S(2)}, u32[]{:S(2)}) async-start(bf16[16,16,256]{2,0,1:T(8,128)(2,1)} %bitcast_select_fusion), calls=%async_computation | async-start | bytes 262144 | tf_op jit(solution)/shard_map/all_to_all | solution.py:103
  22.3 10.0 %all-to-all-done = bf16[16,16,256]{2,0,1:T(8,128)(2,1)S(1)} async-done(((bf16[16,16,256]{2,0,1:T(8,128)(2,1)}), bf16[16,16,256]{2,0,1:T(8,128)(2,1)S(1)}, u32[]{:S(2)}, u32[]{:S(2)}) %all-to-all-start) | async-done | bytes 131104 | tf_op jit(solution)/shard_map/all_to_all | solution.py:103
  36.2 5.7 %collective-permute-done = f32[4,16,1024]{2,1,0:T(8,128)S(1)} collective-permute-done((f32[4,16,1024]{2,1,0:T(8,128)S(1)}, f32[4,16,1024]{2,1,0:T(8,128)S(1)}, u32[]{:S(2)}, u32[]{:S(2)}) %collective-permute-start) | collective-permute-done | bytes 262176 | tf_op jit(solution)/shard_map/ppermute | solution.py:21
  41.9 5.7 %collective-permute-done.1 = f32[4,16,1024]{2,1,0:T(8,128)S(1)} collective-permute-done((f32[4,16,1024]{2,1,0:T(8,128)S(1)}, f32[4,16,1024]{2,1,0:T(8,128)S(1)}, u32[]{:S(2)}, u32[]{:S(2)}) %collective-permute-start.1) | collective-permute-done | bytes 262176 | tf_op jit(solution)/shard_map/ppermute | solution.py:21
  52.8 2.6 collective-permute-done.4
  60.9 4.5 %collective-permute-done.7 = bf16[16,1024]{1,0:T(8,128)(2,1)S(1)} collective-permute-done((bf16[16,1024]{1,0:T(8,128)(2,1)S(1)}, bf16[16,1024]{1,0:T(8,128)(2,1)S(1)}, u32[]{:S(2)}, u32[]{:S(2)}) %collective-permute-start.7) | collective-permute-done | bytes 32800 | tf_op jit(solution)/shard_map/ppermute | solution.py:21
  69.0 5.1 %collective-permute-done.9 = bf16[4,16,1024]{2,1,0:T(8,128)(2,1)S(1)} collective-permute-done((bf16[4,16,1024]{2,1,0:T(8,128)(2,1)S(1)}, bf16[4,16,1024]{2,1,0:T(8,128)(2,1)S(1)}, u32[]{:S(2)}, u32[]{:S(2)}) %collective-permute-start.9) | collective-permute-done | bytes 131104 | tf_op jit(solution)/shard_map/ppermute | solution.py:21
  76.1 3.1 collective-permute-done.11
  79.5 136.3 %all-gather.2.cloned.1.call-done = bf16[4096,2,1024]{2,0,1:T(8,128)(2,1)} async-done(((bf16[256,2,1024]{2,0,1:T(8,128)(2,1)}), bf16[4096,2,1024]{2,0,1:T(8,128)(2,1)}) %all-gather.2.cloned.1.call-update) | async-done | bytes 16777232 | tf_op jit(solution)/shard_map/all_gather | solution.py:100
  215.9 12.5 %fusion.8 = bf16[448,2,1024]{2,0,1:T(8,128)(2,1)S(1)} fusion(bf16[4096,2,1024]{2,0,1:T(8,128)(2,1)} %all-gather.2.cloned.1.call-done, bf16[448,4096]{1,0:T(8,128)(2,1)} %param.9), kind=kOutput, calls=%fused_computation.10 | convolution fusion | flops 7517110272 | bytes 22282240 | tf_op jit(solution)/shard_map/td,djc->tjc/dot_general | solution.py:114
  232.2 2.9 fusion.11
  240.7 6.7 %collective-permute-done.12 = f32[4,16,1040]{2,1,0:T(8,128)S(1)} collective-permute-done((f32[4,16,1040]{2,1,0:T(8,128)}, f32[4,16,1040]{2,1,0:T(8,128)S(1)}, u32[]{:S(2)}, u32[]{:S(2)}) %collective-permute-start.12) | collective-permute-done | bytes 266272 | tf_op jit(solution)/shard_map/ppermute | solution.py:21
  247.6 5.3 %collective-permute-done.14 = f32[4,16,1040]{2,1,0:T(8,128)S(1)} collective-permute-done((f32[4,16,1040]{2,1,0:T(8,128)S(1)}, f32[4,16,1040]{2,1,0:T(8,128)S(1)}, u32[]{:S(2)}, u32[]{:S(2)}) %collective-permute-start.14) | collective-permute-done | bytes 266272 | tf_op jit(solution)/shard_map/ppermute | solution.py:21
  254.8 2.6 collective-permute-start.16
  260.5 3.0 collective-permute-done.17
  270.3 3.2 collective-permute-done.20
  284.7 3.4 collective-permute-done.41
  304.1 3.4 collective-permute-done.31
  320.1 2.7 collective-permute-done.35
  322.7 3.4 collective-permute-done.36
  327.2 7.9 %fusion.100 = (f32[128]{0:T(128)S(1)}, f32[128,1984]{0,1:T(8,128)S(1)}) fusion(bf16[1984,4096]{1,0:T(8,128)(2,1)} %param.14, bf16[128,4096]{0,1:T(8,128)(2,1)S(1)} %bitcast.442), kind=kOutput, calls=%fused_computation.274 | convolution fusion | flops 2080628608 | bytes 18317824 | tf_op jit(solution)/shard_map/dot_general | solution.py:171
  335.1 8.0 %fusion.99 = (f32[128]{0:T(128)S(1)}, f32[128,1984]{0,1:T(8,128)S(1)}) fusion(bf16[1984,4096]{1,0:T(8,128)(2,1)} %collective-permute-done.38, bf16[128,4096]{0,1:T(8,128)(2,1)S(1)} %bitcast.443), kind=kOutput, calls=%fused_computation.273 | convolution fusion | flops 2080628608 | bytes 18317824 | tf_op jit(solution)/shard_map/dot_general | solution.py:171
  355.8 3.1 collective-permute-done.50
  (228 shorter events, 100.4 us)
Async XLA Ops:
  6.5 209.3 %all-gather.2.cloned.1.call-start = ((), (), s32[]{:S(2)}) async-start(), calls=%async_computation.1 | async-start | bytes 17825792 | tf_op jit(solution)/shard_map/all_gather | solution.py:100
  9.1 326.0 %collective-permute-start.38 = (bf16[1984,4096]{1,0:T(8,128)(2,1)}, bf16[1984,4096]{1,0:T(8,128)(2,1)}, u32[]{:S(2)}, u32[]{:S(2)}) collective-permute-start(bf16[1984,4096]{1,0:T(8,128)(2,1)} %param.14), channel_id=1, source_target_pairs={{0,1},{1,0},{2,3},{3,2},{4,5},{5,4},{6,7},{7,6},{8,9},{9,8},{10,11... | collective-permute-start | bytes 48758792 | tf_op jit(solution)/shard_map/ppermute | solution.py:21
  14.3 17.9 %all-to-all-start = ((bf16[16,16,256]{2,0,1:T(8,128)(2,1)}), bf16[16,16,256]{2,0,1:T(8,128)(2,1)S(1)}, u32[]{:S(2)}, u32[]{:S(2)}) async-start(bf16[16,16,256]{2,0,1:T(8,128)(2,1)} %bitcast_select_fusion), calls=%async_computation | async-start | bytes 262144 | tf_op jit(solution)/shard_map/all_to_all | solution.py:103
  32.6 9.3 %collective-permute-start = (f32[4,16,1024]{2,1,0:T(8,128)S(1)}, f32[4,16,1024]{2,1,0:T(8,128)S(1)}, u32[]{:S(2)}, u32[]{:S(2)}) collective-permute-start(f32[4,16,1024]{2,1,0:T(8,128)S(1)} %get-tuple-element.35), channel_id=1, source_target_pairs={{0,2},{2,0},{4,6},{6,4},{8,10},{10,8},{12,14},{14,12},{16,18},{18,... | collective-permute-start | bytes 786440 | tf_op jit(solution)/shard_map/ppermute | solution.py:21
  34.1 13.4 %collective-permute-start.1 = (f32[4,16,1024]{2,1,0:T(8,128)S(1)}, f32[4,16,1024]{2,1,0:T(8,128)S(1)}, u32[]{:S(2)}, u32[]{:S(2)}) collective-permute-start(f32[4,16,1024]{2,1,0:T(8,128)S(1)} %get-tuple-element.37), channel_id=1, source_target_pairs={{0,4},{2,6},{4,0},{6,2},{8,12},{10,14},{12,8},{14,10},{16,20},{18,... | collective-permute-start | bytes 786440 | tf_op jit(solution)/shard_map/ppermute | solution.py:21
  34.1 13.4 %collective-permute-start.2 = (f32[4,16,1024]{2,1,0:T(8,128)S(1)}, f32[4,16,1024]{2,1,0:T(8,128)S(1)}, u32[]{:S(2)}, u32[]{:S(2)}) collective-permute-start(f32[4,16,1024]{2,1,0:T(8,128)S(1)} %get-tuple-element.36), channel_id=1, source_target_pairs={{0,6},{2,4},{4,2},{6,0},{8,14},{10,12},{12,10},{14,8},{16,22},{18,... | collective-permute-start | bytes 786440 | tf_op jit(solution)/shard_map/ppermute | solution.py:21
  47.8 7.7 %collective-permute-start.4 = (f32[1,16,1024]{2,1,0:T(8,128)S(1)}, f32[1,16,1024]{2,1,0:T(8,128)S(1)}, u32[]{:S(2)}, u32[]{:S(2)}) collective-permute-start(f32[1,16,1024]{2,1,0:T(8,128)S(1)} %get-tuple-element.61), channel_id=1, source_target_pairs={{0,16},{2,18},{4,20},{6,22},{8,24},{10,26},{12,28},{14,30},{16,0},... | collective-permute-start | bytes 196616 | tf_op jit(solution)/shard_map/ppermute | solution.py:21
  57.5 7.9 %collective-permute-start.7 = (bf16[16,1024]{1,0:T(8,128)(2,1)S(1)}, bf16[16,1024]{1,0:T(8,128)(2,1)S(1)}, u32[]{:S(2)}, u32[]{:S(2)}) collective-permute-start(bf16[16,1024]{1,0:T(8,128)(2,1)S(1)} %bitcast.458), channel_id=1, source_target_pairs={{0,16},{2,18},{4,20},{6,22},{8,24},{10,26},{12,28},{14,30},{16,0},... | collective-permute-start | bytes 98312 | tf_op jit(solution)/shard_map/ppermute | solution.py:21
  59.0 6.4 %collective-permute-start.8 = (bf16[16,1024]{1,0:T(8,128)(2,1)S(1)}, bf16[16,1024]{1,0:T(8,128)(2,1)S(1)}, u32[]{:S(2)}, u32[]{:S(2)}) collective-permute-start(bf16[16,1024]{1,0:T(8,128)(2,1)S(1)} %bitcast.459), channel_id=1, source_target_pairs={{0,24},{2,26},{4,28},{6,30},{8,16},{10,18},{12,20},{14,22},{16,8},... | collective-permute-start | bytes 98312 | tf_op jit(solution)/shard_map/ppermute | solution.py:21
  65.5 8.7 %collective-permute-start.9 = (bf16[4,16,1024]{2,1,0:T(8,128)(2,1)S(1)}, bf16[4,16,1024]{2,1,0:T(8,128)(2,1)S(1)}, u32[]{:S(2)}, u32[]{:S(2)}) collective-permute-start(bf16[4,16,1024]{2,1,0:T(8,128)(2,1)S(1)} %get-tuple-element.69), channel_id=1, source_target_pairs={{0,2},{2,0},{4,6},{6,4},{8,10},{10,8},{12,14},{14,12},{16,18},{18,... | collective-permute-start | bytes 393224 | tf_op jit(solution)/shard_map/ppermute | solution.py:21
  67.0 9.1 %collective-permute-start.10 = (bf16[4,16,1024]{2,1,0:T(8,128)(2,1)S(1)}, bf16[4,16,1024]{2,1,0:T(8,128)(2,1)S(1)}, u32[]{:S(2)}, u32[]{:S(2)}) collective-permute-start(bf16[4,16,1024]{2,1,0:T(8,128)(2,1)S(1)} %get-tuple-element.69), channel_id=1, source_target_pairs={{0,4},{2,6},{4,0},{6,2},{8,12},{10,14},{12,8},{14,10},{16,20},{18,... | collective-permute-start | bytes 393224 | tf_op jit(solution)/shard_map/ppermute | solution.py:21
  68.6 10.6 %collective-permute-start.11 = (bf16[4,16,1024]{2,1,0:T(8,128)(2,1)S(1)}, bf16[4,16,1024]{2,1,0:T(8,128)(2,1)S(1)}, u32[]{:S(2)}, u32[]{:S(2)}) collective-permute-start(bf16[4,16,1024]{2,1,0:T(8,128)(2,1)S(1)} %get-tuple-element.69), channel_id=1, source_target_pairs={{0,6},{2,4},{4,2},{6,0},{8,14},{10,12},{12,10},{14,8},{16,22},{18,... | collective-permute-start | bytes 393224 | tf_op jit(solution)/shard_map/ppermute | solution.py:21
  237.2 10.2 %collective-permute-start.12 = (f32[4,16,1040]{2,1,0:T(8,128)}, f32[4,16,1040]{2,1,0:T(8,128)S(1)}, u32[]{:S(2)}, u32[]{:S(2)}) collective-permute-start(f32[4,16,1040]{2,1,0:T(8,128)} %get-tuple-element.28), channel_id=1, source_target_pairs={{0,2},{2,0},{4,6},{6,4},{8,10},{10,8},{12,14},{14,12},{16,18},{18,... | collective-permute-start | bytes 798728 | tf_op jit(solution)/shard_map/ppermute | solution.py:21
  238.3 9.4 %collective-permute-start.13 = (f32[4,16,1040]{2,1,0:T(8,128)S(1)}, f32[4,16,1040]{2,1,0:T(8,128)S(1)}, u32[]{:S(2)}, u32[]{:S(2)}) collective-permute-start(f32[4,16,1040]{2,1,0:T(8,128)S(1)} %get-tuple-element.27), channel_id=1, source_target_pairs={{0,4},{2,6},{4,0},{6,2},{8,12},{10,14},{12,8},{14,10},{16,20},{18,... | collective-permute-start | bytes 798728 | tf_op jit(solution)/shard_map/ppermute | solution.py:21
  239.2 13.7 %collective-permute-start.14 = (f32[4,16,1040]{2,1,0:T(8,128)S(1)}, f32[4,16,1040]{2,1,0:T(8,128)S(1)}, u32[]{:S(2)}, u32[]{:S(2)}) collective-permute-start(f32[4,16,1040]{2,1,0:T(8,128)S(1)} %get-tuple-element.26), channel_id=1, source_target_pairs={{0,6},{2,4},{4,2},{6,0},{8,14},{10,12},{12,10},{14,8},{16,22},{18,... | collective-permute-start | bytes 798728 | tf_op jit(solution)/shard_map/ppermute | solution.py:21
  257.4 6.2 %collective-permute-start.17 = (f32[1,16,1040]{2,1,0:T(8,128)S(1)}, f32[1,16,1040]{2,1,0:T(8,128)S(1)}, u32[]{:S(2)}, u32[]{:S(2)}) collective-permute-start(f32[1,16,1040]{2,1,0:T(8,128)S(1)} %get-tuple-element.51), channel_id=1, source_target_pairs={{0,24},{2,26},{4,28},{6,30},{8,16},{10,18},{12,20},{14,22},{16,8},... | collective-permute-start | bytes 199688 | tf_op jit(solution)/shard_map/ppermute | solution.py:21
  279.7 8.5 %collective-permute-start.25 = (bf16[1024,256]{1,0:T(8,128)(2,1)S(1)}, bf16[1024,256]{1,0:T(8,128)(2,1)S(1)}, u32[]{:S(2)}, u32[]{:S(2)}) collective-permute-start(bf16[1024,256]{1,0:T(8,128)(2,1)S(1)} %copy-done.3), channel_id=1, source_target_pairs={{0,1},{1,0},{2,3},{3,2},{4,5},{5,4},{6,7},{7,6},{8,9},{9,8},{10,11... | collective-permute-start | bytes 1572872 | tf_op jit(solution)/shard_map/ppermute | solution.py:21
  281.9 6.8 %collective-permute-start.24 = (bf16[256,1024]{1,0:T(8,128)(2,1)S(1)}, bf16[256,1024]{1,0:T(8,128)(2,1)}, u32[]{:S(2)}, u32[]{:S(2)}) collective-permute-start(bf16[256,1024]{1,0:T(8,128)(2,1)S(1)} %bitcast.440), channel_id=1, source_target_pairs={{0,1},{1,0},{2,3},{3,2},{4,5},{5,4},{6,7},{7,6},{8,9},{9,8},{10,11... | collective-permute-start | bytes 1572872 | tf_op jit(solution)/shard_map/ppermute | solution.py:21
  296.6 20.4 %collective-permute-start.42 = (s32[4,16]{1,0:T(4,128)S(1)}, s32[4,16]{1,0:T(4,128)S(1)}, u32[]{:S(2)}, u32[]{:S(2)}) collective-permute-start(s32[4,16]{1,0:T(4,128)S(1)} %get-tuple-element.99), channel_id=1, source_target_pairs={{0,2},{2,0},{4,6},{6,4},{8,10},{10,8},{12,14},{14,12},{16,18},{18,... | collective-permute-start | bytes 776 | tf_op jit(solution)/shard_map/ppermute | solution.py:21
  312.2 6.3 %collective-permute-start.43 = (s32[4,16]{1,0:T(4,128)S(1)}, s32[4,16]{1,0:T(4,128)S(1)}, u32[]{:S(2)}, u32[]{:S(2)}) collective-permute-start(s32[4,16]{1,0:T(4,128)S(1)} %get-tuple-element.99), channel_id=1, source_target_pairs={{0,4},{2,6},{4,0},{6,2},{8,12},{10,14},{12,8},{14,10},{16,20},{18,... | collective-permute-start | bytes 776 | tf_op jit(solution)/shard_map/ppermute | solution.py:21
  312.9 6.9 %collective-permute-start.44 = (s32[4,16]{1,0:T(4,128)S(1)}, s32[4,16]{1,0:T(4,128)S(1)}, u32[]{:S(2)}, u32[]{:S(2)}) collective-permute-start(s32[4,16]{1,0:T(4,128)S(1)} %get-tuple-element.99), channel_id=1, source_target_pairs={{0,6},{2,4},{4,2},{6,0},{8,14},{10,12},{12,10},{14,8},{16,22},{18,... | collective-permute-start | bytes 776 | tf_op jit(solution)/shard_map/ppermute | solution.py:21
  316.3 6.4 %collective-permute-start.35 = (bf16[4,128,256]{2,1,0:T(8,128)(2,1)S(1)}, bf16[4,128,256]{2,1,0:T(8,128)(2,1)S(1)}, u32[]{:S(2)}, u32[]{:S(2)}) collective-permute-start(bf16[4,128,256]{2,1,0:T(8,128)(2,1)S(1)} %get-tuple-element.54), channel_id=1, source_target_pairs={{0,2},{2,0},{4,6},{6,4},{8,10},{10,8},{12,14},{14,12},{16,18},{18,... | collective-permute-start | bytes 786440 | tf_op jit(solution)/shard_map/ppermute | solution.py:21
  317.0 9.2 %collective-permute-start.36 = (bf16[4,128,256]{2,1,0:T(8,128)(2,1)S(1)}, bf16[4,128,256]{2,1,0:T(8,128)(2,1)S(1)}, u32[]{:S(2)}, u32[]{:S(2)}) collective-permute-start(bf16[4,128,256]{2,1,0:T(8,128)(2,1)S(1)} %get-tuple-element.54), channel_id=1, source_target_pairs={{0,4},{2,6},{4,0},{6,2},{8,12},{10,14},{12,8},{14,10},{16,20},{18,... | collective-permute-start | bytes 786440 | tf_op jit(solution)/shard_map/ppermute | solution.py:21
  318.5 7.7 %collective-permute-start.37 = (bf16[4,128,256]{2,1,0:T(8,128)(2,1)S(1)}, bf16[4,128,256]{2,1,0:T(8,128)(2,1)S(1)}, u32[]{:S(2)}, u32[]{:S(2)}) collective-permute-start(bf16[4,128,256]{2,1,0:T(8,128)(2,1)S(1)} %get-tuple-element.54), channel_id=1, source_target_pairs={{0,6},{2,4},{4,2},{6,0},{8,14},{10,12},{12,10},{14,8},{16,22},{18,... | collective-permute-start | bytes 786440 | tf_op jit(solution)/shard_map/ppermute | solution.py:21
  (36 other events, 242.3 us)
Sparse Core Ops, SparseCore 0:
  10.1 205.6 all-gather.1

commit v6 on v5

--- a/solution.py
+++ b/solution.py
@@ -109,7 +109,6 @@
 
     wanted = _all_gather(targets[0], "ctx", n_ctx).reshape(total_rows)
     other_vocab = _swap(vocab_weight, "head", n_head, 1) if n_head == 2 else None
-    out_full = _all_gather(out_weight, "head", n_head).reshape(n_head * head_columns, col_block)
 
     keyval = jnp.einsum(
         "td,djc->tjc", activations, kv_weight, preferred_element_type=jnp.float32
@@ -149,13 +148,13 @@
     den = combined[:, head_columns + heads_here :]
     attended = (num / den[:, :, None]).reshape(slot_count, head_columns).astype(jnp.bfloat16)
     attended = _all_gather(attended, "ctx", n_ctx).reshape(total_rows, head_columns)
-    attended = _all_gather(attended, "head", n_head)
-    attended = attended.transpose(1, 0, 2).reshape(total_rows, n_head * head_columns)
 
     share = total_rows // n_head
     head_idx = lax.axis_index("head")
-    my_rows = lax.dynamic_slice_in_dim(attended, head_idx * share, share, 0)
-    branch = jnp.dot(my_rows, out_full, preferred_element_type=jnp.float32)
+    partial_branch = jnp.dot(attended, out_weight, preferred_element_type=jnp.float32)
+    branch = _reduce_scatter(
+        partial_branch.reshape(n_head, share, col_block), "head", n_head, _add
+    )
     sumsq = _all_reduce(jnp.sum(branch * branch, axis=1), "ctx", n_ctx, _add)
     gain = lax.dynamic_slice_in_dim(norm_gain, lax.axis_index("ctx") * col_block, col_block, 0)
     hidden = (

time: 368 us -> 361 us (0.981)
    ppermute x52 -> x51, waiting for transfers between devices: 77.8 us -> 74.6 us  [_swap(): return lax.ppermute(x, axis, [(j, j ^ k) for j in range(n)])]
    ppermute x52 -> x51, starting transfers between devices: 62.3 us -> 62.9 us  [_swap(): return lax.ppermute(x, axis, [(j, j ^ k) for j in range(n)])]
  transfers between devices with their start and end apart: 54 -> 53, of which waited for: 34 -> 33; matrix products, arithmetic and copies ran while one was open for 12% -> 11% of each run, Pallas kernels for 0% -> 0%
where the time goes in v6:
time: 361 us
  waiting for transfers between devices  221 us (61%)
  starting transfers between devices  70.8 us (20%)
  matrix products  32.6 us (9%)
  local copies, waits for them, and re-layouts  16 us (4%)
  between operations  14.9 us (4%)
  other arithmetic  5.59 us (2%)
    all_gather x1, waiting for transfers between devices, shards(): kv_weight = lax.all_gather(keyval_weight, 'ctx', axis=0, tiled=True)  136 us
    ppermute x51, waiting for transfers between devices, _swap(): return lax.ppermute(x, axis, [(j, j ^ k) for j in range(n)])  74.6 us
    ppermute x51, starting transfers between devices, _swap(): return lax.ppermute(x, axis, [(j, j ^ k) for j in range(n)])  62.9 us
    dot_general x2, matrix products, shard_stats(): lax.dot_general(rows, shard, (((1,), (1,)), ((), ())), preferred_element_...  15.9 us
    dot_general x1, matrix products, shards(): jnp.einsum('td,djc->tjc', activations, kv_weight, preferred_element_type=...  12.6 us
    all_to_all x1, waiting for transfers between devices, shards(): row_blocks = lax.all_to_all(rows_here, 'ctx', 1, 0, tiled=True)  9.92 us
    all_to_all x1, starting transfers between devices, shards(): row_blocks = lax.all_to_all(rows_here, 'ctx', 1, 0, tiled=True)  7.88 us
  transfers between devices with their start and end apart: 53, of which 33 were waited for; matrix products, arithmetic and copies ran while one was open for 11% of the time, Pallas kernels for 0%

profile of v6, /device:TPU:0, one launch (start us, length us, event | category | flops | bytes accessed | tf_op | source)
XLA Modules:
  0.0 360.7 jit_solution(2878516902926336104)
XLA Ops:
  10.3 3.3 gather_fusion
  14.3 7.9 %all-to-all-start = ((bf16[16,16,256]{2,0,1:T(8,128)(2,1)}), bf16[16,16,256]{2,0,1:T(8,128)(2,1)S(1)}, u32[]{:S(2)}, u32[]{:S(2)}) async-start(bf16[16,16,256]{2,0,1:T(8,128)(2,1)} %bitcast_select_fusion), calls=%async_computation | async-start | bytes 262144 | tf_op jit(solution)/shard_map/all_to_all | solution.py:103
  22.2 9.9 %all-to-all-done = bf16[16,16,256]{2,0,1:T(8,128)(2,1)S(1)} async-done(((bf16[16,16,256]{2,0,1:T(8,128)(2,1)}), bf16[16,16,256]{2,0,1:T(8,128)(2,1)S(1)}, u32[]{:S(2)}, u32[]{:S(2)}) %all-to-all-start) | async-done | bytes 131104 | tf_op jit(solution)/shard_map/all_to_all | solution.py:103
  36.1 5.7 %collective-permute-done = f32[4,16,1024]{2,1,0:T(8,128)S(1)} collective-permute-done((f32[4,16,1024]{2,1,0:T(8,128)S(1)}, f32[4,16,1024]{2,1,0:T(8,128)S(1)}, u32[]{:S(2)}, u32[]{:S(2)}) %collective-permute-start) | collective-permute-done | bytes 262176 | tf_op jit(solution)/shard_map/ppermute | solution.py:21
  41.8 5.7 %collective-permute-done.1 = f32[4,16,1024]{2,1,0:T(8,128)S(1)} collective-permute-done((f32[4,16,1024]{2,1,0:T(8,128)S(1)}, f32[4,16,1024]{2,1,0:T(8,128)S(1)}, u32[]{:S(2)}, u32[]{:S(2)}) %collective-permute-start.1) | collective-permute-done | bytes 262176 | tf_op jit(solution)/shard_map/ppermute | solution.py:21
  47.6 2.6 collective-permute-start.4
  52.8 2.6 collective-permute-done.4
  60.9 4.3 %collective-permute-done.7 = bf16[16,1024]{1,0:T(8,128)(2,1)S(1)} collective-permute-done((bf16[16,1024]{1,0:T(8,128)(2,1)S(1)}, bf16[16,1024]{1,0:T(8,128)(2,1)S(1)}, u32[]{:S(2)}, u32[]{:S(2)}) %collective-permute-start.7) | collective-permute-done | bytes 32800 | tf_op jit(solution)/shard_map/ppermute | solution.py:21
  68.8 5.2 %collective-permute-done.9 = bf16[4,16,1024]{2,1,0:T(8,128)(2,1)S(1)} collective-permute-done((bf16[4,16,1024]{2,1,0:T(8,128)(2,1)S(1)}, bf16[4,16,1024]{2,1,0:T(8,128)(2,1)S(1)}, u32[]{:S(2)}, u32[]{:S(2)}) %collective-permute-start.9) | collective-permute-done | bytes 131104 | tf_op jit(solution)/shard_map/ppermute | solution.py:21
  75.9 3.3 collective-permute-done.11
  79.5 136.4 %all-gather.2.cloned.1.call-done = bf16[4096,2,1024]{2,0,1:T(8,128)(2,1)} async-done(((bf16[256,2,1024]{2,0,1:T(8,128)(2,1)}), bf16[4096,2,1024]{2,0,1:T(8,128)(2,1)}) %all-gather.2.cloned.1.call-update) | async-done | bytes 16777232 | tf_op jit(solution)/shard_map/all_gather | solution.py:100
  215.9 12.6 %fusion.8 = bf16[448,2,1024]{2,0,1:T(8,128)(2,1)S(1)} fusion(bf16[4096,2,1024]{2,0,1:T(8,128)(2,1)} %all-gather.2.cloned.1.call-done, bf16[448,4096]{1,0:T(8,128)(2,1)} %param.9), kind=kOutput, calls=%fused_computation.10 | convolution fusion | flops 7517110272 | bytes 22282240 | tf_op jit(solution)/shard_map/td,djc->tjc/dot_general | solution.py:113
  232.3 2.9 fusion.11
  240.7 6.7 %collective-permute-done.12 = f32[4,16,1040]{2,1,0:T(8,128)S(1)} collective-permute-done((f32[4,16,1040]{2,1,0:T(8,128)}, f32[4,16,1040]{2,1,0:T(8,128)S(1)}, u32[]{:S(2)}, u32[]{:S(2)}) %collective-permute-start.12) | collective-permute-done | bytes 266272 | tf_op jit(solution)/shard_map/ppermute | solution.py:21
  247.6 5.3 %collective-permute-done.14 = f32[4,16,1040]{2,1,0:T(8,128)S(1)} collective-permute-done((f32[4,16,1040]{2,1,0:T(8,128)S(1)}, f32[4,16,1040]{2,1,0:T(8,128)S(1)}, u32[]{:S(2)}, u32[]{:S(2)}) %collective-permute-start.14) | collective-permute-done | bytes 266272 | tf_op jit(solution)/shard_map/ppermute | solution.py:21
  260.5 3.0 collective-permute-done.17
  270.3 3.2 collective-permute-done.20
  283.1 2.8 collective-permute-done.40
  297.2 3.3 collective-permute-done.30
  313.2 2.7 collective-permute-done.34
  315.8 3.4 collective-permute-done.35
  320.3 7.9 %fusion.98 = (f32[128]{0:T(128)S(1)}, f32[128,1984]{0,1:T(8,128)S(1)}) fusion(bf16[1984,4096]{1,0:T(8,128)(2,1)} %param.14, bf16[128,4096]{0,1:T(8,128)(2,1)S(1)} %bitcast.441), kind=kOutput, calls=%fused_computation.265 | convolution fusion | flops 2080628608 | bytes 18317824 | tf_op jit(solution)/shard_map/dot_general | solution.py:170
  328.3 8.0 %fusion.97 = (f32[128]{0:T(128)S(1)}, f32[128,1984]{0,1:T(8,128)S(1)}) fusion(bf16[1984,4096]{1,0:T(8,128)(2,1)} %collective-permute-done.37, bf16[128,4096]{0,1:T(8,128)(2,1)S(1)} %bitcast.442), kind=kOutput, calls=%fused_computation.264 | convolution fusion | flops 2080628608 | bytes 18317824 | tf_op jit(solution)/shard_map/dot_general | solution.py:170
  348.9 3.2 collective-permute-done.49
  (223 shorter events, 94.3 us)
Async XLA Ops:
  6.5 209.3 %all-gather.2.cloned.1.call-start = ((), (), s32[]{:S(2)}) async-start(), calls=%async_computation.1 | async-start | bytes 17825792 | tf_op jit(solution)/shard_map/all_gather | solution.py:100
  9.1 319.1 %collective-permute-start.37 = (bf16[1984,4096]{1,0:T(8,128)(2,1)}, bf16[1984,4096]{1,0:T(8,128)(2,1)}, u32[]{:S(2)}, u32[]{:S(2)}) collective-permute-start(bf16[1984,4096]{1,0:T(8,128)(2,1)} %param.14), channel_id=1, source_target_pairs={{0,1},{1,0},{2,3},{3,2},{4,5},{5,4},{6,7},{7,6},{8,9},{9,8},{10,11... | collective-permute-start | bytes 48758792 | tf_op jit(solution)/shard_map/ppermute | solution.py:21
  14.3 17.8 %all-to-all-start = ((bf16[16,16,256]{2,0,1:T(8,128)(2,1)}), bf16[16,16,256]{2,0,1:T(8,128)(2,1)S(1)}, u32[]{:S(2)}, u32[]{:S(2)}) async-start(bf16[16,16,256]{2,0,1:T(8,128)(2,1)} %bitcast_select_fusion), calls=%async_computation | async-start | bytes 262144 | tf_op jit(solution)/shard_map/all_to_all | solution.py:103
  32.5 9.3 %collective-permute-start = (f32[4,16,1024]{2,1,0:T(8,128)S(1)}, f32[4,16,1024]{2,1,0:T(8,128)S(1)}, u32[]{:S(2)}, u32[]{:S(2)}) collective-permute-start(f32[4,16,1024]{2,1,0:T(8,128)S(1)} %get-tuple-element.35), channel_id=1, source_target_pairs={{0,2},{2,0},{4,6},{6,4},{8,10},{10,8},{12,14},{14,12},{16,18},{18,... | collective-permute-start | bytes 786440 | tf_op jit(solution)/shard_map/ppermute | solution.py:21
  34.1 13.4 %collective-permute-start.1 = (f32[4,16,1024]{2,1,0:T(8,128)S(1)}, f32[4,16,1024]{2,1,0:T(8,128)S(1)}, u32[]{:S(2)}, u32[]{:S(2)}) collective-permute-start(f32[4,16,1024]{2,1,0:T(8,128)S(1)} %get-tuple-element.37), channel_id=1, source_target_pairs={{0,4},{2,6},{4,0},{6,2},{8,12},{10,14},{12,8},{14,10},{16,20},{18,... | collective-permute-start | bytes 786440 | tf_op jit(solution)/shard_map/ppermute | solution.py:21
  34.1 13.4 %collective-permute-start.2 = (f32[4,16,1024]{2,1,0:T(8,128)S(1)}, f32[4,16,1024]{2,1,0:T(8,128)S(1)}, u32[]{:S(2)}, u32[]{:S(2)}) collective-permute-start(f32[4,16,1024]{2,1,0:T(8,128)S(1)} %get-tuple-element.36), channel_id=1, source_target_pairs={{0,6},{2,4},{4,2},{6,0},{8,14},{10,12},{12,10},{14,8},{16,22},{18,... | collective-permute-start | bytes 786440 | tf_op jit(solution)/shard_map/ppermute | solution.py:21
  47.6 7.8 %collective-permute-start.4 = (f32[1,16,1024]{2,1,0:T(8,128)S(1)}, f32[1,16,1024]{2,1,0:T(8,128)S(1)}, u32[]{:S(2)}, u32[]{:S(2)}) collective-permute-start(f32[1,16,1024]{2,1,0:T(8,128)S(1)} %get-tuple-element.59), channel_id=1, source_target_pairs={{0,16},{2,18},{4,20},{6,22},{8,24},{10,26},{12,28},{14,30},{16,0},... | collective-permute-start | bytes 196616 | tf_op jit(solution)/shard_map/ppermute | solution.py:21
  57.5 7.7 %collective-permute-start.7 = (bf16[16,1024]{1,0:T(8,128)(2,1)S(1)}, bf16[16,1024]{1,0:T(8,128)(2,1)S(1)}, u32[]{:S(2)}, u32[]{:S(2)}) collective-permute-start(bf16[16,1024]{1,0:T(8,128)(2,1)S(1)} %bitcast.455), channel_id=1, source_target_pairs={{0,16},{2,18},{4,20},{6,22},{8,24},{10,26},{12,28},{14,30},{16,0},... | collective-permute-start | bytes 98312 | tf_op jit(solution)/shard_map/ppermute | solution.py:21
  58.8 6.4 %collective-permute-start.8 = (bf16[16,1024]{1,0:T(8,128)(2,1)S(1)}, bf16[16,1024]{1,0:T(8,128)(2,1)S(1)}, u32[]{:S(2)}, u32[]{:S(2)}) collective-permute-start(bf16[16,1024]{1,0:T(8,128)(2,1)S(1)} %bitcast.456), channel_id=1, source_target_pairs={{0,24},{2,26},{4,28},{6,30},{8,16},{10,18},{12,20},{14,22},{16,8},... | collective-permute-start | bytes 98312 | tf_op jit(solution)/shard_map/ppermute | solution.py:21
  65.3 8.7 %collective-permute-start.9 = (bf16[4,16,1024]{2,1,0:T(8,128)(2,1)S(1)}, bf16[4,16,1024]{2,1,0:T(8,128)(2,1)S(1)}, u32[]{:S(2)}, u32[]{:S(2)}) collective-permute-start(bf16[4,16,1024]{2,1,0:T(8,128)(2,1)S(1)} %get-tuple-element.67), channel_id=1, source_target_pairs={{0,2},{2,0},{4,6},{6,4},{8,10},{10,8},{12,14},{14,12},{16,18},{18,... | collective-permute-start | bytes 393224 | tf_op jit(solution)/shard_map/ppermute | solution.py:21
  66.8 9.1 %collective-permute-start.10 = (bf16[4,16,1024]{2,1,0:T(8,128)(2,1)S(1)}, bf16[4,16,1024]{2,1,0:T(8,128)(2,1)S(1)}, u32[]{:S(2)}, u32[]{:S(2)}) collective-permute-start(bf16[4,16,1024]{2,1,0:T(8,128)(2,1)S(1)} %get-tuple-element.67), channel_id=1, source_target_pairs={{0,4},{2,6},{4,0},{6,2},{8,12},{10,14},{12,8},{14,10},{16,20},{18,... | collective-permute-start | bytes 393224 | tf_op jit(solution)/shard_map/ppermute | solution.py:21
  68.5 10.6 %collective-permute-start.11 = (bf16[4,16,1024]{2,1,0:T(8,128)(2,1)S(1)}, bf16[4,16,1024]{2,1,0:T(8,128)(2,1)S(1)}, u32[]{:S(2)}, u32[]{:S(2)}) collective-permute-start(bf16[4,16,1024]{2,1,0:T(8,128)(2,1)S(1)} %get-tuple-element.67), channel_id=1, source_target_pairs={{0,6},{2,4},{4,2},{6,0},{8,14},{10,12},{12,10},{14,8},{16,22},{18,... | collective-permute-start | bytes 393224 | tf_op jit(solution)/shard_map/ppermute | solution.py:21
  237.2 10.2 %collective-permute-start.12 = (f32[4,16,1040]{2,1,0:T(8,128)}, f32[4,16,1040]{2,1,0:T(8,128)S(1)}, u32[]{:S(2)}, u32[]{:S(2)}) collective-permute-start(f32[4,16,1040]{2,1,0:T(8,128)} %get-tuple-element.30), channel_id=1, source_target_pairs={{0,2},{2,0},{4,6},{6,4},{8,10},{10,8},{12,14},{14,12},{16,18},{18,... | collective-permute-start | bytes 798728 | tf_op jit(solution)/shard_map/ppermute | solution.py:21
  238.3 9.4 %collective-permute-start.13 = (f32[4,16,1040]{2,1,0:T(8,128)S(1)}, f32[4,16,1040]{2,1,0:T(8,128)S(1)}, u32[]{:S(2)}, u32[]{:S(2)}) collective-permute-start(f32[4,16,1040]{2,1,0:T(8,128)S(1)} %get-tuple-element.29), channel_id=1, source_target_pairs={{0,4},{2,6},{4,0},{6,2},{8,12},{10,14},{12,8},{14,10},{16,20},{18,... | collective-permute-start | bytes 798728 | tf_op jit(solution)/shard_map/ppermute | solution.py:21
  239.2 13.7 %collective-permute-start.14 = (f32[4,16,1040]{2,1,0:T(8,128)S(1)}, f32[4,16,1040]{2,1,0:T(8,128)S(1)}, u32[]{:S(2)}, u32[]{:S(2)}) collective-permute-start(f32[4,16,1040]{2,1,0:T(8,128)S(1)} %get-tuple-element.28), channel_id=1, source_target_pairs={{0,6},{2,4},{4,2},{6,0},{8,14},{10,12},{12,10},{14,8},{16,22},{18,... | collective-permute-start | bytes 798728 | tf_op jit(solution)/shard_map/ppermute | solution.py:21
  257.3 6.2 %collective-permute-start.17 = (f32[1,16,1040]{2,1,0:T(8,128)S(1)}, f32[1,16,1040]{2,1,0:T(8,128)S(1)}, u32[]{:S(2)}, u32[]{:S(2)}) collective-permute-start(f32[1,16,1040]{2,1,0:T(8,128)S(1)} %get-tuple-element.49), channel_id=1, source_target_pairs={{0,24},{2,26},{4,28},{6,30},{8,16},{10,18},{12,20},{14,22},{16,8},... | collective-permute-start | bytes 199688 | tf_op jit(solution)/shard_map/ppermute | solution.py:21
  274.3 6.2 %collective-permute-start.22 = (bf16[4,16,1024]{2,1,0:T(8,128)(2,1)S(1)}, bf16[4,16,1024]{2,1,0:T(8,128)(2,1)S(1)}, u32[]{:S(2)}, u32[]{:S(2)}) collective-permute-start(bf16[4,16,1024]{2,1,0:T(8,128)(2,1)S(1)} %get-tuple-element.61), channel_id=1, source_target_pairs={{0,4},{2,6},{4,0},{6,2},{8,12},{10,14},{12,8},{14,10},{16,20},{18,... | collective-permute-start | bytes 393224 | tf_op jit(solution)/shard_map/ppermute | solution.py:21
  275.8 6.6 %collective-permute-start.23 = (bf16[4,16,1024]{2,1,0:T(8,128)(2,1)S(1)}, bf16[4,16,1024]{2,1,0:T(8,128)(2,1)S(1)}, u32[]{:S(2)}, u32[]{:S(2)}) collective-permute-start(bf16[4,16,1024]{2,1,0:T(8,128)(2,1)S(1)} %get-tuple-element.61), channel_id=1, source_target_pairs={{0,6},{2,4},{4,2},{6,0},{8,14},{10,12},{12,10},{14,8},{16,22},{18,... | collective-permute-start | bytes 393224 | tf_op jit(solution)/shard_map/ppermute | solution.py:21
  289.6 20.4 %collective-permute-start.41 = (s32[4,16]{1,0:T(4,128)S(1)}, s32[4,16]{1,0:T(4,128)S(1)}, u32[]{:S(2)}, u32[]{:S(2)}) collective-permute-start(s32[4,16]{1,0:T(4,128)S(1)} %get-tuple-element.97), channel_id=1, source_target_pairs={{0,2},{2,0},{4,6},{6,4},{8,10},{10,8},{12,14},{14,12},{16,18},{18,... | collective-permute-start | bytes 776 | tf_op jit(solution)/shard_map/ppermute | solution.py:21
  305.2 6.3 %collective-permute-start.42 = (s32[4,16]{1,0:T(4,128)S(1)}, s32[4,16]{1,0:T(4,128)S(1)}, u32[]{:S(2)}, u32[]{:S(2)}) collective-permute-start(s32[4,16]{1,0:T(4,128)S(1)} %get-tuple-element.97), channel_id=1, source_target_pairs={{0,4},{2,6},{4,0},{6,2},{8,12},{10,14},{12,8},{14,10},{16,20},{18,... | collective-permute-start | bytes 776 | tf_op jit(solution)/shard_map/ppermute | solution.py:21
  305.9 7.0 %collective-permute-start.43 = (s32[4,16]{1,0:T(4,128)S(1)}, s32[4,16]{1,0:T(4,128)S(1)}, u32[]{:S(2)}, u32[]{:S(2)}) collective-permute-start(s32[4,16]{1,0:T(4,128)S(1)} %get-tuple-element.97), channel_id=1, source_target_pairs={{0,6},{2,4},{4,2},{6,0},{8,14},{10,12},{12,10},{14,8},{16,22},{18,... | collective-permute-start | bytes 776 | tf_op jit(solution)/shard_map/ppermute | solution.py:21
  309.4 6.4 %collective-permute-start.34 = (bf16[4,128,256]{2,1,0:T(8,128)(2,1)S(1)}, bf16[4,128,256]{2,1,0:T(8,128)(2,1)S(1)}, u32[]{:S(2)}, u32[]{:S(2)}) collective-permute-start(bf16[4,128,256]{2,1,0:T(8,128)(2,1)S(1)} %get-tuple-element.52), channel_id=1, source_target_pairs={{0,2},{2,0},{4,6},{6,4},{8,10},{10,8},{12,14},{14,12},{16,18},{18,... | collective-permute-start | bytes 786440 | tf_op jit(solution)/shard_map/ppermute | solution.py:21
  310.0 9.2 %collective-permute-start.35 = (bf16[4,128,256]{2,1,0:T(8,128)(2,1)S(1)}, bf16[4,128,256]{2,1,0:T(8,128)(2,1)S(1)}, u32[]{:S(2)}, u32[]{:S(2)}) collective-permute-start(bf16[4,128,256]{2,1,0:T(8,128)(2,1)S(1)} %get-tuple-element.52), channel_id=1, source_target_pairs={{0,4},{2,6},{4,0},{6,2},{8,12},{10,14},{12,8},{14,10},{16,20},{18,... | collective-permute-start | bytes 786440 | tf_op jit(solution)/shard_map/ppermute | solution.py:21
  311.5 7.7 %collective-permute-start.36 = (bf16[4,128,256]{2,1,0:T(8,128)(2,1)S(1)}, bf16[4,128,256]{2,1,0:T(8,128)(2,1)S(1)}, u32[]{:S(2)}, u32[]{:S(2)}) collective-permute-start(bf16[4,128,256]{2,1,0:T(8,128)(2,1)S(1)} %get-tuple-element.52), channel_id=1, source_target_pairs={{0,6},{2,4},{4,2},{6,0},{8,14},{10,12},{12,10},{14,8},{16,22},{18,... | collective-permute-start | bytes 786440 | tf_op jit(solution)/shard_map/ppermute | solution.py:21
  (35 other events, 230.0 us)
Sparse Core Ops, SparseCore 0:
  10.1 205.6 all-gather.1

commit v7 on v6

--- a/solution.py
+++ b/solution.py
@@ -1,6 +1,8 @@
 import jax
 import jax.numpy as jnp
 from jax import lax
+from jax.experimental import pallas as pl
+from jax.experimental.pallas import tpu as pltpu
 from jax.sharding import PartitionSpec as P
 
 HDIM = 128
@@ -69,6 +71,65 @@
             axis=k,
         )
     return x.reshape((n,) + rest)
+
+
+def _stats_kernel(h_ref, v_ref, t_ref, m_out, s_out, p_out, m_sc, s_sc, p_sc):
+    j = pl.program_id(0)
+    tile = v_ref.shape[0]
+
+    @pl.when(j == 0)
+    def _():
+        m_sc[...] = jnp.full(m_sc.shape, -jnp.inf, jnp.float32)
+        s_sc[...] = jnp.zeros(s_sc.shape, jnp.float32)
+        p_sc[...] = jnp.zeros(p_sc.shape, jnp.float32)
+
+    lt = lax.dot_general(
+        v_ref[...], h_ref[...], (((1,), (1,)), ((), ())), preferred_element_type=jnp.float32
+    )
+    ids = j * tile + lax.broadcasted_iota(jnp.int32, lt.shape, 0)
+    m_old = m_sc[...]
+    m_new = jnp.maximum(m_old, jnp.max(lt, axis=0, keepdims=True))
+    s_sc[...] = s_sc[...] * jnp.exp(m_old - m_new) + jnp.sum(
+        jnp.exp(lt - m_new), axis=0, keepdims=True
+    )
+    p_sc[...] += jnp.sum(jnp.where(ids == t_ref[...], lt, 0.0), axis=0, keepdims=True)
+    m_sc[...] = m_new
+
+    @pl.when(j == pl.num_programs(0) - 1)
+    def _():
+        m_out[...] = m_sc[...]
+        s_out[...] = s_sc[...]
+        p_out[...] = p_sc[...]
+
+
+def _shard_stats_kernel(rows, shard, local_targets):
+    n_rows, width = rows.shape
+    n_vocab = shard.shape[0]
+    tile = n_vocab
+    for cand in range(512, 7, -8):
+        if n_vocab % cand == 0:
+            tile = cand
+            break
+    row_spec = pl.BlockSpec((1, n_rows), lambda j: (0, 0))
+    outs = pl.pallas_call(
+        _stats_kernel,
+        grid=(n_vocab // tile,),
+        in_specs=[
+            pl.BlockSpec((n_rows, width), lambda j: (0, 0)),
+            pl.BlockSpec((tile, width), lambda j: (j, 0)),
+            row_spec,
+        ],
+        out_specs=[row_spec] * 3,
+        out_shape=[jax.ShapeDtypeStruct((1, n_rows), jnp.float32)] * 3,
+        scratch_shapes=[pltpu.VMEM((1, n_rows), jnp.float32)] * 3,
+        compiler_params=pltpu.CompilerParams(dimension_semantics=("arbitrary",)),
+        cost_estimate=pl.CostEstimate(
+            flops=2 * n_rows * n_vocab * width,
+            transcendentals=n_rows * n_vocab,
+            bytes_accessed=2 * (n_vocab + n_rows) * width,
+        ),
+    )(rows, shard, local_targets[None, :])
+    return jnp.concatenate(outs, axis=0)
 
 
 def _add(a, b):
@@ -180,9 +241,11 @@
     ctx_idx = lax.axis_index("ctx")
     if other_vocab is not None:
         share_targets = lax.dynamic_slice_in_dim(wanted, head_idx * share, share, 0)
+        n_vocab = vocab_weight.shape[0]
+        other_index = flat_index + 1 - 2 * head_idx
         stats = lse_combine(
-            shard_stats(hidden, vocab_weight, flat_index, share_targets),
-            shard_stats(hidden, other_vocab, flat_index + 1 - 2 * head_idx, share_targets),
+            _shard_stats_kernel(hidden, vocab_weight, share_targets - flat_index * n_vocab),
+            _shard_stats_kernel(hidden, other_vocab, share_targets - other_index * n_vocab),
         )
         stats = _all_reduce(stats, "ctx", n_ctx, lse_combine)
         share_losses = stats[0] + jnp.log(stats[1]) - stats[2]

time: 361 us -> 369 us (1.022)
  Pallas kernels: 0 us -> 18.7 us
  matrix products: 32.6 us -> 14.6 us
  waiting for transfers between devices: 221 us -> 226 us
    pallas_call x0 -> x2, Pallas kernels: none -> 18.7 us  [_shard_stats_kernel(): pl.pallas_call(_stats_kernel, grid=(n_vocab // tile,), in_specs=[pl.Block...]
    dot_general x2 -> x0, matrix products: 15.9 us -> none  [shard_stats(): lax.dot_general(rows, shard, (((1,), (1,)), ((), ())), preferred_element_...]
    ppermute x51, waiting for transfers between devices: 74.6 us -> 78.8 us  [_swap(): return lax.ppermute(x, axis, [(j, j ^ k) for j in range(n)])]
  transfers between devices with their start and end apart: 53 -> 53, of which waited for: 33 -> 38; matrix products, arithmetic and copies ran while one was open for 11% -> 9% of each run, Pallas kernels for 0% -> 3%
where the time goes in v7:
time: 369 us
  waiting for transfers between devices  226 us (61%)
  starting transfers between devices  70 us (19%)
  Pallas kernels  18.7 us (5%)
  local copies, waits for them, and re-layouts  16.3 us (4%)
  between operations  14.8 us (4%)
  matrix products  14.6 us (4%)
  other arithmetic  8.44 us (2%)
    all_gather x1, waiting for transfers between devices, shards(): kv_weight = lax.all_gather(keyval_weight, 'ctx', axis=0, tiled=True)  137 us
    ppermute x51, waiting for transfers between devices, _swap(): return lax.ppermute(x, axis, [(j, j ^ k) for j in range(n)])  78.8 us
    ppermute x51, starting transfers between devices, _swap(): return lax.ppermute(x, axis, [(j, j ^ k) for j in range(n)])  62.1 us
    pallas_call x2, Pallas kernels, _shard_stats_kernel(): pl.pallas_call(_stats_kernel, grid=(n_vocab // tile,), in_specs=[pl.Block...  18.7 us
    dot_general x1, matrix products, shards(): jnp.einsum('td,djc->tjc', activations, kv_weight, preferred_element_type=...  12.5 us
    all_to_all x1, waiting for transfers between devices, shards(): row_blocks = lax.all_to_all(rows_here, 'ctx', 1, 0, tiled=True)  9.95 us
    all_to_all x1, starting transfers between devices, shards(): row_blocks = lax.all_to_all(rows_here, 'ctx', 1, 0, tiled=True)  7.88 us
  transfers between devices with their start and end apart: 53, of which 38 were waited for; matrix products, arithmetic and copies ran while one was open for 9% of the time, Pallas kernels for 3%

profile of v7, /device:TPU:0, one launch (start us, length us, event | category | flops | bytes accessed | tf_op | source)
XLA Modules:
  0.0 368.9 jit_solution(11986386093858252623)
XLA Ops:
  6.5 2.6 copy.100
  10.3 3.3 gather_fusion
  14.3 7.9 %all-to-all-start = ((bf16[16,16,256]{2,0,1:T(8,128)(2,1)}), bf16[16,16,256]{2,0,1:T(8,128)(2,1)S(1)}, u32[]{:S(2)}, u32[]{:S(2)}) async-start(bf16[16,16,256]{2,0,1:T(8,128)(2,1)} %bitcast_select_fusion), calls=%async_computation | async-start | bytes 262144 | tf_op jit(solution)/shard_map/all_to_all | solution.py:164
  22.3 10.0 %all-to-all-done = bf16[16,16,256]{2,0,1:T(8,128)(2,1)S(1)} async-done(((bf16[16,16,256]{2,0,1:T(8,128)(2,1)}), bf16[16,16,256]{2,0,1:T(8,128)(2,1)S(1)}, u32[]{:S(2)}, u32[]{:S(2)}) %all-to-all-start) | async-done | bytes 131104 | tf_op jit(solution)/shard_map/all_to_all | solution.py:164
  36.2 6.6 %collective-permute-done.2 = f32[4,16,1024]{2,1,0:T(8,128)S(1)} collective-permute-done((f32[4,16,1024]{2,1,0:T(8,128)S(1)}, f32[4,16,1024]{2,1,0:T(8,128)S(1)}, u32[]{:S(2)}, u32[]{:S(2)}) %collective-permute-start.2) | collective-permute-done | bytes 262176 | tf_op jit(solution)/shard_map/ppermute | solution.py:23
  42.8 4.5 %collective-permute-done.1 = f32[4,16,1024]{2,1,0:T(8,128)S(1)} collective-permute-done((f32[4,16,1024]{2,1,0:T(8,128)S(1)}, f32[4,16,1024]{2,1,0:T(8,128)S(1)}, u32[]{:S(2)}, u32[]{:S(2)}) %collective-permute-start.1) | collective-permute-done | bytes 262176 | tf_op jit(solution)/shard_map/ppermute | solution.py:23
  54.2 2.7 collective-permute-done.4
  58.3 3.0 collective-permute-start.6
  68.6 6.5 %collective-permute-done.11 = bf16[4,16,1024]{2,1,0:T(8,128)(2,1)S(1)} collective-permute-done((bf16[4,16,1024]{2,1,0:T(8,128)(2,1)S(1)}, bf16[4,16,1024]{2,1,0:T(8,128)(2,1)S(1)}, u32[]{:S(2)}, u32[]{:S(2)}) %collective-permute-start.11) | collective-permute-done | bytes 131104 | tf_op jit(solution)/shard_map/ppermute | solution.py:23
  76.8 2.5 collective-permute-done.9
  79.7 137.2 %all-gather.2.cloned.1.call-done = bf16[4096,2,1024]{2,0,1:T(8,128)(2,1)} async-done(((bf16[256,2,1024]{2,0,1:T(8,128)(2,1)}), bf16[4096,2,1024]{2,0,1:T(8,128)(2,1)}) %all-gather.2.cloned.1.call-update) | async-done | bytes 16777232 | tf_op jit(solution)/shard_map/all_gather | solution.py:161
  216.9 12.5 %fusion.8 = bf16[448,2,1024]{2,0,1:T(8,128)(2,1)S(1)} fusion(bf16[4096,2,1024]{2,0,1:T(8,128)(2,1)} %all-gather.2.cloned.1.call-done, bf16[448,4096]{1,0:T(8,128)(2,1)} %param.9), kind=kOutput, calls=%fused_computation.10 | convolution fusion | flops 7517110272 | bytes 22282240 | tf_op jit(solution)/shard_map/td,djc->tjc/dot_general | solution.py:174
  234.0 2.7 fusion.2
  241.6 7.6 %collective-permute-done.14 = f32[4,16,1040]{2,1,0:T(8,128)S(1)} collective-permute-done((f32[4,16,1040]{2,1,0:T(8,128)}, f32[4,16,1040]{2,1,0:T(8,128)S(1)}, u32[]{:S(2)}, u32[]{:S(2)}) %collective-permute-start.14) | collective-permute-done | bytes 266272 | tf_op jit(solution)/shard_map/ppermute | solution.py:23
  249.2 4.7 %collective-permute-done.13 = f32[4,16,1040]{2,1,0:T(8,128)S(1)} collective-permute-done((f32[4,16,1040]{2,1,0:T(8,128)S(1)}, f32[4,16,1040]{2,1,0:T(8,128)S(1)}, u32[]{:S(2)}, u32[]{:S(2)}) %collective-permute-start.13) | collective-permute-done | bytes 266272 | tf_op jit(solution)/shard_map/ppermute | solution.py:23
  266.5 2.5 collective-permute-start.20
  279.2 3.6 collective-permute-done.39
  283.8 3.5 collective-permute-done.38
  287.2 3.5 collective-permute-done.37
  303.3 2.6 collective-permute-start.28
  320.4 3.1 collective-permute-done.36
  323.5 2.7 collective-permute-done.35
  327.8 9.3 %shard_map.91 = (f32[1,128]{1,0:T(1,128)}, f32[1,128]{1,0:T(1,128)}, f32[1,128]{1,0:T(1,128)}) custom-call(bf16[128,4096]{1,0:T(8,128)(2,1)} %bitcast.408, bf16[1984,4096]{1,0:T(8,128)(2,1)} %v_ref.1, s32[1,128]{1,0:T(1,128)} %get-tuple-element.117.t_ref), custom_call_target="tpu_custom_call" | custom-call | flops 2080374784 | bytes 17301504 | tf_op jit(solution)/shard_map/pallas_call | solution.py:114
  337.1 9.4 %shard_map.92 = (f32[1,128]{1,0:T(1,128)}, f32[1,128]{1,0:T(1,128)}, f32[1,128]{1,0:T(1,128)}) custom-call(bf16[128,4096]{1,0:T(8,128)(2,1)} %bitcast.409, bf16[1984,4096]{1,0:T(8,128)(2,1)} %collective-permute-done.43.v_ref, s32[1,128]{1,0:T(1,128)} %get-tuple-element.116.t_ref), custom_call_target="tpu_custom_call" | custom-call | flops 2080374784 | bytes 17301504 | tf_op jit(solution)/shard_map/pallas_call | solution.py:114
  (228 shorter events, 99.8 us)
Async XLA Ops:
  6.5 210.3 %all-gather.2.cloned.1.call-start = ((), (), s32[]{:S(2)}) async-start(), calls=%async_computation.1 | async-start | bytes 17825792 | tf_op jit(solution)/shard_map/all_gather | solution.py:161
  9.1 327.9 %collective-permute-start.43 = (bf16[1984,4096]{1,0:T(8,128)(2,1)}, bf16[1984,4096]{1,0:T(8,128)(2,1)}, u32[]{:S(2)}, u32[]{:S(2)}) collective-permute-start(bf16[1984,4096]{1,0:T(8,128)(2,1)} %v_ref.1), channel_id=1, source_target_pairs={{0,1},{1,0},{2,3},{3,2},{4,5},{5,4},{6,7},{7,6},{8,9},{9,8},{10,11... | collective-permute-start | bytes 48758792 | tf_op jit(solution)/shard_map/ppermute | solution.py:23
  14.3 17.9 %all-to-all-start = ((bf16[16,16,256]{2,0,1:T(8,128)(2,1)}), bf16[16,16,256]{2,0,1:T(8,128)(2,1)S(1)}, u32[]{:S(2)}, u32[]{:S(2)}) async-start(bf16[16,16,256]{2,0,1:T(8,128)(2,1)} %bitcast_select_fusion), calls=%async_computation | async-start | bytes 262144 | tf_op jit(solution)/shard_map/all_to_all | solution.py:164
  32.6 10.2 %collective-permute-start.2 = (f32[4,16,1024]{2,1,0:T(8,128)S(1)}, f32[4,16,1024]{2,1,0:T(8,128)S(1)}, u32[]{:S(2)}, u32[]{:S(2)}) collective-permute-start(f32[4,16,1024]{2,1,0:T(8,128)S(1)} %get-tuple-element.46), channel_id=1, source_target_pairs={{0,6},{2,4},{4,2},{6,0},{8,14},{10,12},{12,10},{14,8},{16,22},{18,... | collective-permute-start | bytes 786440 | tf_op jit(solution)/shard_map/ppermute | solution.py:23
  33.5 13.7 %collective-permute-start.1 = (f32[4,16,1024]{2,1,0:T(8,128)S(1)}, f32[4,16,1024]{2,1,0:T(8,128)S(1)}, u32[]{:S(2)}, u32[]{:S(2)}) collective-permute-start(f32[4,16,1024]{2,1,0:T(8,128)S(1)} %get-tuple-element.47), channel_id=1, source_target_pairs={{0,4},{2,6},{4,0},{6,2},{8,12},{10,14},{12,8},{14,10},{16,20},{18,... | collective-permute-start | bytes 786440 | tf_op jit(solution)/shard_map/ppermute | solution.py:23
  35.6 11.7 %collective-permute-start = (f32[4,16,1024]{2,1,0:T(8,128)S(1)}, f32[4,16,1024]{2,1,0:T(8,128)S(1)}, u32[]{:S(2)}, u32[]{:S(2)}) collective-permute-start(f32[4,16,1024]{2,1,0:T(8,128)S(1)} %get-tuple-element.45), channel_id=1, source_target_pairs={{0,2},{2,0},{4,6},{6,4},{8,10},{10,8},{12,14},{14,12},{16,18},{18,... | collective-permute-start | bytes 786440 | tf_op jit(solution)/shard_map/ppermute | solution.py:23
  47.4 6.8 %collective-permute-start.5 = (f32[1,16,1024]{2,1,0:T(8,128)S(1)}, f32[1,16,1024]{2,1,0:T(8,128)S(1)}, u32[]{:S(2)}, u32[]{:S(2)}) collective-permute-start(f32[1,16,1024]{2,1,0:T(8,128)S(1)} %get-tuple-element.68), channel_id=1, source_target_pairs={{0,24},{2,26},{4,28},{6,30},{8,16},{10,18},{12,20},{14,22},{16,8},... | collective-permute-start | bytes 196616 | tf_op jit(solution)/shard_map/ppermute | solution.py:23
  49.5 7.4 %collective-permute-start.4 = (f32[1,16,1024]{2,1,0:T(8,128)S(1)}, f32[1,16,1024]{2,1,0:T(8,128)S(1)}, u32[]{:S(2)}, u32[]{:S(2)}) collective-permute-start(f32[1,16,1024]{2,1,0:T(8,128)S(1)} %get-tuple-element.69), channel_id=1, source_target_pairs={{0,16},{2,18},{4,20},{6,22},{8,24},{10,26},{12,28},{14,30},{16,0},... | collective-permute-start | bytes 196616 | tf_op jit(solution)/shard_map/ppermute | solution.py:23
  49.5 7.4 %collective-permute-start.3 = (f32[1,16,1024]{2,1,0:T(8,128)S(1)}, f32[1,16,1024]{2,1,0:T(8,128)S(1)}, u32[]{:S(2)}, u32[]{:S(2)}) collective-permute-start(f32[1,16,1024]{2,1,0:T(8,128)S(1)} %get-tuple-element.67), channel_id=1, source_target_pairs={{0,8},{2,10},{4,12},{6,14},{8,0},{10,2},{12,4},{14,6},{16,24},{18,... | collective-permute-start | bytes 196616 | tf_op jit(solution)/shard_map/ppermute | solution.py:23
  65.1 10.1 %collective-permute-start.11 = (bf16[4,16,1024]{2,1,0:T(8,128)(2,1)S(1)}, bf16[4,16,1024]{2,1,0:T(8,128)(2,1)S(1)}, u32[]{:S(2)}, u32[]{:S(2)}) collective-permute-start(bf16[4,16,1024]{2,1,0:T(8,128)(2,1)S(1)} %get-tuple-element.77), channel_id=1, source_target_pairs={{0,6},{2,4},{4,2},{6,0},{8,14},{10,12},{12,10},{14,8},{16,22},{18,... | collective-permute-start | bytes 393224 | tf_op jit(solution)/shard_map/ppermute | solution.py:23
  67.1 9.7 %collective-permute-start.10 = (bf16[4,16,1024]{2,1,0:T(8,128)(2,1)S(1)}, bf16[4,16,1024]{2,1,0:T(8,128)(2,1)S(1)}, u32[]{:S(2)}, u32[]{:S(2)}) collective-permute-start(bf16[4,16,1024]{2,1,0:T(8,128)(2,1)S(1)} %get-tuple-element.77), channel_id=1, source_target_pairs={{0,4},{2,6},{4,0},{6,2},{8,12},{10,14},{12,8},{14,10},{16,20},{18,... | collective-permute-start | bytes 393224 | tf_op jit(solution)/shard_map/ppermute | solution.py:23
  67.7 11.7 %collective-permute-start.9 = (bf16[4,16,1024]{2,1,0:T(8,128)(2,1)S(1)}, bf16[4,16,1024]{2,1,0:T(8,128)(2,1)S(1)}, u32[]{:S(2)}, u32[]{:S(2)}) collective-permute-start(bf16[4,16,1024]{2,1,0:T(8,128)(2,1)S(1)} %get-tuple-element.77), channel_id=1, source_target_pairs={{0,2},{2,0},{4,6},{6,4},{8,10},{10,8},{12,14},{14,12},{16,18},{18,... | collective-permute-start | bytes 393224 | tf_op jit(solution)/shard_map/ppermute | solution.py:23
  238.1 11.1 %collective-permute-start.14 = (f32[4,16,1040]{2,1,0:T(8,128)}, f32[4,16,1040]{2,1,0:T(8,128)S(1)}, u32[]{:S(2)}, u32[]{:S(2)}) collective-permute-start(f32[4,16,1040]{2,1,0:T(8,128)} %get-tuple-element.38), channel_id=1, source_target_pairs={{0,6},{2,4},{4,2},{6,0},{8,14},{10,12},{12,10},{14,8},{16,22},{18,... | collective-permute-start | bytes 798728 | tf_op jit(solution)/shard_map/ppermute | solution.py:23
  239.6 14.3 %collective-permute-start.13 = (f32[4,16,1040]{2,1,0:T(8,128)S(1)}, f32[4,16,1040]{2,1,0:T(8,128)S(1)}, u32[]{:S(2)}, u32[]{:S(2)}) collective-permute-start(f32[4,16,1040]{2,1,0:T(8,128)S(1)} %get-tuple-element.39), channel_id=1, source_target_pairs={{0,4},{2,6},{4,0},{6,2},{8,12},{10,14},{12,8},{14,10},{16,20},{18,... | collective-permute-start | bytes 798728 | tf_op jit(solution)/shard_map/ppermute | solution.py:23
  240.7 13.3 %collective-permute-start.12 = (f32[4,16,1040]{2,1,0:T(8,128)S(1)}, f32[4,16,1040]{2,1,0:T(8,128)S(1)}, u32[]{:S(2)}, u32[]{:S(2)}) collective-permute-start(f32[4,16,1040]{2,1,0:T(8,128)S(1)} %get-tuple-element.40), channel_id=1, source_target_pairs={{0,2},{2,0},{4,6},{6,4},{8,10},{10,8},{12,14},{14,12},{16,18},{18,... | collective-permute-start | bytes 798728 | tf_op jit(solution)/shard_map/ppermute | solution.py:23
  255.5 7.0 %collective-permute-start.17 = (f32[1,16,1040]{2,1,0:T(8,128)S(1)}, f32[1,16,1040]{2,1,0:T(8,128)S(1)}, u32[]{:S(2)}, u32[]{:S(2)}) collective-permute-start(f32[1,16,1040]{2,1,0:T(8,128)S(1)} %get-tuple-element.59), channel_id=1, source_target_pairs={{0,24},{2,26},{4,28},{6,30},{8,16},{10,18},{12,20},{14,22},{16,8},... | collective-permute-start | bytes 199688 | tf_op jit(solution)/shard_map/ppermute | solution.py:23
  257.6 7.1 %collective-permute-start.16 = (f32[1,16,1040]{2,1,0:T(8,128)S(1)}, f32[1,16,1040]{2,1,0:T(8,128)S(1)}, u32[]{:S(2)}, u32[]{:S(2)}) collective-permute-start(f32[1,16,1040]{2,1,0:T(8,128)S(1)} %get-tuple-element.60), channel_id=1, source_target_pairs={{0,16},{2,18},{4,20},{6,22},{8,24},{10,26},{12,28},{14,30},{16,0},... | collective-permute-start | bytes 199688 | tf_op jit(solution)/shard_map/ppermute | solution.py:23
  257.6 7.3 %collective-permute-start.15 = (f32[1,16,1040]{2,1,0:T(8,128)S(1)}, f32[1,16,1040]{2,1,0:T(8,128)S(1)}, u32[]{:S(2)}, u32[]{:S(2)}) collective-permute-start(f32[1,16,1040]{2,1,0:T(8,128)S(1)} %get-tuple-element.58), channel_id=1, source_target_pairs={{0,8},{2,10},{4,12},{6,14},{8,0},{10,2},{12,4},{14,6},{16,24},{18,... | collective-permute-start | bytes 199688 | tf_op jit(solution)/shard_map/ppermute | solution.py:23
  273.9 16.9 %collective-permute-start.23 = (bf16[4,16,1024]{2,1,0:T(8,128)(2,1)S(1)}, bf16[4,16,1024]{2,1,0:T(8,128)(2,1)S(1)}, u32[]{:S(2)}, u32[]{:S(2)}) collective-permute-start(bf16[4,16,1024]{2,1,0:T(8,128)(2,1)S(1)} %get-tuple-element.71), channel_id=1, source_target_pairs={{0,6},{2,4},{4,2},{6,0},{8,14},{10,12},{12,10},{14,8},{16,22},{18,... | collective-permute-start | bytes 393224 | tf_op jit(solution)/shard_map/ppermute | solution.py:23
  275.4 15.4 %collective-permute-start.22 = (bf16[4,16,1024]{2,1,0:T(8,128)(2,1)S(1)}, bf16[4,16,1024]{2,1,0:T(8,128)(2,1)S(1)}, u32[]{:S(2)}, u32[]{:S(2)}) collective-permute-start(bf16[4,16,1024]{2,1,0:T(8,128)(2,1)S(1)} %get-tuple-element.71), channel_id=1, source_target_pairs={{0,4},{2,6},{4,0},{6,2},{8,12},{10,14},{12,8},{14,10},{16,20},{18,... | collective-permute-start | bytes 393224 | tf_op jit(solution)/shard_map/ppermute | solution.py:23
  276.5 14.3 %collective-permute-start.21 = (bf16[4,16,1024]{2,1,0:T(8,128)(2,1)S(1)}, bf16[4,16,1024]{2,1,0:T(8,128)(2,1)S(1)}, u32[]{:S(2)}, u32[]{:S(2)}) collective-permute-start(bf16[4,16,1024]{2,1,0:T(8,128)(2,1)S(1)} %get-tuple-element.71), channel_id=1, source_target_pairs={{0,2},{2,0},{4,6},{6,4},{8,10},{10,8},{12,14},{14,12},{16,18},{18,... | collective-permute-start | bytes 393224 | tf_op jit(solution)/shard_map/ppermute | solution.py:23
  316.1 7.4 %collective-permute-start.36 = (bf16[4,128,256]{2,1,0:T(8,128)(2,1)S(1)}, bf16[4,128,256]{2,1,0:T(8,128)(2,1)S(1)}, u32[]{:S(2)}, u32[]{:S(2)}) collective-permute-start(bf16[4,128,256]{2,1,0:T(8,128)(2,1)S(1)} %get-tuple-element.62), channel_id=1, source_target_pairs={{0,6},{2,4},{4,2},{6,0},{8,14},{10,12},{12,10},{14,8},{16,22},{18,... | collective-permute-start | bytes 786440 | tf_op jit(solution)/shard_map/ppermute | solution.py:23
  317.7 8.5 %collective-permute-start.35 = (bf16[4,128,256]{2,1,0:T(8,128)(2,1)S(1)}, bf16[4,128,256]{2,1,0:T(8,128)(2,1)S(1)}, u32[]{:S(2)}, u32[]{:S(2)}) collective-permute-start(bf16[4,128,256]{2,1,0:T(8,128)(2,1)S(1)} %get-tuple-element.62), channel_id=1, source_target_pairs={{0,4},{2,6},{4,0},{6,2},{8,12},{10,14},{12,8},{14,10},{16,20},{18,... | collective-permute-start | bytes 786440 | tf_op jit(solution)/shard_map/ppermute | solution.py:23
  318.6 7.6 %collective-permute-start.34 = (bf16[4,128,256]{2,1,0:T(8,128)(2,1)S(1)}, bf16[4,128,256]{2,1,0:T(8,128)(2,1)S(1)}, u32[]{:S(2)}, u32[]{:S(2)}) collective-permute-start(bf16[4,128,256]{2,1,0:T(8,128)(2,1)S(1)} %get-tuple-element.62), channel_id=1, source_target_pairs={{0,2},{2,0},{4,6},{6,4},{8,10},{10,8},{12,14},{14,12},{16,18},{18,... | collective-permute-start | bytes 786440 | tf_op jit(solution)/shard_map/ppermute | solution.py:23
  (38 other events, 266.8 us)
Sparse Core Ops, SparseCore 0:
  10.1 206.6 all-gather.1

commit v8 on v6

--- a/solution.py
+++ b/solution.py
@@ -160,7 +160,6 @@
     hidden = (
         branch * lax.rsqrt(sumsq / width + 1e-06)[:, None] * gain
     ).astype(jnp.bfloat16)
-    hidden = _all_gather(hidden, "ctx", n_ctx).transpose(1, 0, 2).reshape(share, width)
     def lse_combine(a, b):
         top = jnp.maximum(a[0], b[0])
         total = a[1] * jnp.exp(a[0] - top) + b[1] * jnp.exp(b[0] - top)
@@ -180,9 +179,57 @@
     ctx_idx = lax.axis_index("ctx")
     if other_vocab is not None:
         share_targets = lax.dynamic_slice_in_dim(wanted, head_idx * share, share, 0)
+        rounds = list(reversed(_digits(n_ctx)))
+        p0, r0 = rounds[0]
+        low_count = 1 << p0
+        low = ctx_idx % low_count
+        others = [(low + j) % low_count for j in range(1, low_count)]
+        dig0 = (ctx_idx // low_count) % r0
+        got = _exchange(lambda s: hidden, "ctx", n_ctx, p0, r0, dig0)
+        got[0] = hidden
+        stacked = jnp.stack(got)
+        first = jnp.stack(
+            [lax.dynamic_index_in_dim(stacked, a ^ dig0, 0, keepdims=False) for a in range(r0)]
+        )
+        x = first
+        for k, (p, r) in enumerate(rounds[1:]):
+            digit = (ctx_idx // (1 << p)) % r
+            got = _exchange(lambda s: x, "ctx", n_ctx, p, r, digit)
+            got[0] = x
+            stacked = jnp.stack(got)
+            x = jnp.stack(
+                [lax.dynamic_index_in_dim(stacked, a ^ digit, 0, keepdims=False) for a in range(r)],
+                axis=k + 1,
+            )
+        full = x.reshape((r0, low_count, share, col_block))
+        hid_a = first.transpose(1, 0, 2).reshape(share, r0 * col_block)
+        hid_b = jnp.stack(
+            [lax.dynamic_index_in_dim(full, o, 1, keepdims=False) for o in others], axis=1
+        )
+        hid_b = hid_b.transpose(2, 0, 1, 3).reshape(share, width - r0 * col_block)
+
+        def split_stats(shard, shard_index):
+            n_vocab = shard.shape[0]
+            v4 = shard.reshape(n_vocab, r0, low_count, col_block)
+            voc_a = lax.dynamic_index_in_dim(v4, low, 2, keepdims=False).reshape(n_vocab, -1)
+            voc_b = jnp.stack(
+                [lax.dynamic_index_in_dim(v4, o, 2, keepdims=False) for o in others], axis=2
+            ).reshape(n_vocab, -1)
+            dims = (((1,), (1,)), ((), ()))
+            logits = lax.dot_general(
+                hid_a, voc_a, dims, preferred_element_type=jnp.float32
+            ) + lax.dot_general(hid_b, voc_b, dims, preferred_element_type=jnp.float32)
+            ids = shard_index * n_vocab + jnp.arange(n_vocab, dtype=jnp.int32)
+            top = jnp.max(logits, axis=1)
+            total = jnp.sum(jnp.exp(logits - top[:, None]), axis=1)
+            picked = jnp.sum(
+                jnp.where(ids[None, :] == share_targets[:, None], logits, 0.0), axis=1
+            )
+            return jnp.stack([top, total, picked])
+
         stats = lse_combine(
-            shard_stats(hidden, vocab_weight, flat_index, share_targets),
-            shard_stats(hidden, other_vocab, flat_index + 1 - 2 * head_idx, share_targets),
+            split_stats(vocab_weight, flat_index),
+            split_stats(other_vocab, flat_index + 1 - 2 * head_idx),
         )
         stats = _all_reduce(stats, "ctx", n_ctx, lse_combine)
         share_losses = stats[0] + jnp.log(stats[1]) - stats[2]
@@ -193,6 +240,7 @@
         theirs = _swap(mine, "head", n_head, 1)
         block_losses = jnp.where(owner == head_idx, mine, theirs)
     else:
+        hidden = _all_gather(hidden, "ctx", n_ctx).transpose(1, 0, 2).reshape(share, width)
         hidden = _all_gather(hidden, "head", n_head).reshape(total_rows, width)
         stats = shard_stats(hidden, vocab_weight, flat_index, wanted)
         stats = _all_reduce(stats, "head", n_head, lse_combine)

time: 361 us -> 443 us (1.23)
  local copies, waits for them, and re-layouts: 16 us -> 122 us
  waiting for transfers between devices: 221 us -> 197 us
  matrix products: 32.6 us -> 27.4 us
    unnamed x26 -> x45, local copies, waits for them, and re-layouts: 5.8 us -> 67.8 us
    ppermute x51, waiting for transfers between devices: 74.6 us -> 49.8 us  [_swap(): return lax.ppermute(x, axis, [(j, j ^ k) for j in range(n)])]
    dynamic_slice x0 -> x3, local copies, waits for them, and re-layouts: none -> 23.1 us  [the longest x1 23 us: split_stats(): lax.dynamic_index_in_dim(v4, low, 2, keepdims=False).reshape(n_vocab, -1)]
    ppermute x0 -> x1, local copies, waits for them, and re-layouts: none -> 22.5 us  [_swap(): return lax.ppermute(x, axis, [(j, j ^ k) for j in range(n)])]
    dot_general x2 -> x4, matrix products: 15.9 us -> 12.9 us  [the longest x2 9.46 us: split_stats(): lax.dot_general(hid_b, voc_b, dims, preferred_element_type=jnp.float32)]
  transfers between devices with their start and end apart: 53 -> 53, of which waited for: 33 -> 30; matrix products, arithmetic and copies ran while one was open for 11% -> 31% of each run, Pallas kernels for 0% -> 0%
where the time goes in v8:
time: 443 us; the launch traced here: 440 us
  waiting for transfers between devices  197 us (44%)
  local copies, waits for them, and re-layouts  122 us (28%)
  starting transfers between devices  71.4 us (16%)
  matrix products  27.4 us (6%)
  between operations  14.9 us (3%)
  other arithmetic  7.65 us (2%)
    all_gather x1, waiting for transfers between devices, shards(): kv_weight = lax.all_gather(keyval_weight, 'ctx', axis=0, tiled=True)  137 us
    unnamed x45, local copies, waits for them, and re-layouts  67.8 us
    ppermute x51, starting transfers between devices, _swap(): return lax.ppermute(x, axis, [(j, j ^ k) for j in range(n)])  63.5 us
    ppermute x51, waiting for transfers between devices, _swap(): return lax.ppermute(x, axis, [(j, j ^ k) for j in range(n)])  49.8 us
    dynamic_slice x1, local copies, waits for them, and re-layouts, split_stats(): lax.dynamic_index_in_dim(v4, low, 2, keepdims=False).reshape(n_vocab, -1)  23 us
    ppermute x1, local copies, waits for them, and re-layouts, _swap(): return lax.ppermute(x, axis, [(j, j ^ k) for j in range(n)])  22.5 us
    dot_general x1, matrix products, shards(): jnp.einsum('td,djc->tjc', activations, kv_weight, preferred_element_type=...  12.4 us
    all_to_all x1, waiting for transfers between devices, shards(): row_blocks = lax.all_to_all(rows_here, 'ctx', 1, 0, tiled=True)  9.96 us
  transfers between devices with their start and end apart: 53, of which 30 were waited for; matrix products, arithmetic and copies ran while one was open for 31% of the time, Pallas kernels for 0%

profile of v8, /device:TPU:0, one launch (start us, length us, event | category | flops | bytes accessed | tf_op | source)
XLA Modules:
  0.0 440.3 jit_solution(11050339183831283779)
XLA Ops:
  6.5 2.6 copy.130
  10.3 3.3 gather_fusion
  14.3 7.9 %all-to-all-start = ((bf16[16,16,256]{2,0,1:T(8,128)(2,1)}), bf16[16,16,256]{2,0,1:T(8,128)(2,1)S(1)}, u32[]{:S(2)}, u32[]{:S(2)}) async-start(bf16[16,16,256]{2,0,1:T(8,128)(2,1)} %bitcast_select_fusion), calls=%async_computation | async-start | bytes 262144 | tf_op jit(solution)/shard_map/all_to_all | solution.py:103
  22.2 10.0 %all-to-all-done = bf16[16,16,256]{2,0,1:T(8,128)(2,1)S(1)} async-done(((bf16[16,16,256]{2,0,1:T(8,128)(2,1)}), bf16[16,16,256]{2,0,1:T(8,128)(2,1)S(1)}, u32[]{:S(2)}, u32[]{:S(2)}) %all-to-all-start) | async-done | bytes 131104 | tf_op jit(solution)/shard_map/all_to_all | solution.py:103
  36.1 6.6 %collective-permute-done.2 = f32[4,16,1024]{2,1,0:T(8,128)S(1)} collective-permute-done((f32[4,16,1024]{2,1,0:T(8,128)S(1)}, f32[4,16,1024]{2,1,0:T(8,128)S(1)}, u32[]{:S(2)}, u32[]{:S(2)}) %collective-permute-start.2) | collective-permute-done | bytes 262176 | tf_op jit(solution)/shard_map/ppermute | solution.py:21
  42.7 4.5 %collective-permute-done.1 = f32[4,16,1024]{2,1,0:T(8,128)S(1)} collective-permute-done((f32[4,16,1024]{2,1,0:T(8,128)S(1)}, f32[4,16,1024]{2,1,0:T(8,128)S(1)}, u32[]{:S(2)}, u32[]{:S(2)}) %collective-permute-start.1) | collective-permute-done | bytes 262176 | tf_op jit(solution)/shard_map/ppermute | solution.py:21
  54.2 2.7 collective-permute-done.4
  58.3 3.0 collective-permute-start.6
  68.6 6.5 %collective-permute-done.11 = bf16[4,16,1024]{2,1,0:T(8,128)(2,1)S(1)} collective-permute-done((bf16[4,16,1024]{2,1,0:T(8,128)(2,1)S(1)}, bf16[4,16,1024]{2,1,0:T(8,128)(2,1)S(1)}, u32[]{:S(2)}, u32[]{:S(2)}) %collective-permute-start.11) | collective-permute-done | bytes 131104 | tf_op jit(solution)/shard_map/ppermute | solution.py:21
  76.9 2.5 collective-permute-done.9
  79.7 137.2 %all-gather.2.cloned.1.call-done = bf16[4096,2,1024]{2,0,1:T(8,128)(2,1)} async-done(((bf16[256,2,1024]{2,0,1:T(8,128)(2,1)}), bf16[4096,2,1024]{2,0,1:T(8,128)(2,1)}) %all-gather.2.cloned.1.call-update) | async-done | bytes 16777232 | tf_op jit(solution)/shard_map/all_gather | solution.py:100
  216.9 12.4 %fusion.26 = bf16[448,2,1024]{2,0,1:T(8,128)(2,1)S(1)} fusion(bf16[4096,2,1024]{2,0,1:T(8,128)(2,1)} %all-gather.2.cloned.1.call-done, bf16[448,4096]{1,0:T(8,128)(2,1)} %param.9), kind=kOutput, calls=%fused_computation.26 | convolution fusion | flops 7517110272 | bytes 22282240 | tf_op jit(solution)/shard_map/td,djc->tjc/dot_general | solution.py:113
  233.9 2.7 fusion.14
  242.1 22.5 %copy.153 = bf16[1984,4096]{0,1:T(8,128)(2,1)} copy(bf16[1984,4096]{1,0:T(8,128)(2,1)} %param.14) | data formatting | bytes 32505856 | tf_op args[5]
  300.6 22.5 %copy.157 = bf16[1984,4096]{0,1:T(8,128)(2,1)} copy(bf16[1984,4096]{1,0:T(8,128)(2,1)} %collective-permute-done.37) | data formatting | bytes 32505856 | tf_op jit(solution)/shard_map/ppermute | solution.py:21
  341.3 23.0 %constant_dynamic-slice_fusion.21 = (bf16[1984,4,1,256]{0,3,2,1:T(8,128)(2,1)}, bf16[1984,4,1,256]{0,3,2,1:T(8,128)(2,1)}, bf16[1984,4,1,256]{0,3,2,1:T(8,128)(2...) fusion(bf16[1984,4,4,256]{0,3,2,1:T(8,128)(2,1)} %bitcast.451, ...), kind=kLoop, calls=%fused_computation.145 | loop fusion | bytes 65011728 | tf_op jit(solution)/shard_map/jit(dynamic_index_in_dim)/dynamic_slice | solution.py:214
  364.2 6.2 %copy.181 = bf16[1984,4,1,256]{3,0,2,1:T(8,128)(2,1)} copy(bf16[1984,4,1,256]{0,3,2,1:T(8,128)(2,1)} %get-tuple-element.28) | data formatting | bytes 8126464
  370.4 6.2 %copy.180 = bf16[1984,4,1,256]{3,0,2,1:T(8,128)(2,1)} copy(bf16[1984,4,1,256]{0,3,2,1:T(8,128)(2,1)} %get-tuple-element.26) | data formatting | bytes 8126464
  376.6 6.2 %copy.179 = bf16[1984,4,1,256]{3,0,2,1:T(8,128)(2,1)} copy(bf16[1984,4,1,256]{0,3,2,1:T(8,128)(2,1)} %get-tuple-element.27) | data formatting | bytes 8126464
  382.8 6.3 %copy.178 = bf16[1984,4,1,256]{3,0,2,1:T(8,128)(2,1)} copy(bf16[1984,4,1,256]{0,3,2,1:T(8,128)(2,1)} %get-tuple-element.128) | data formatting | bytes 8126464
  389.0 6.2 %copy.177 = bf16[1984,4,1,256]{3,0,2,1:T(8,128)(2,1)} copy(bf16[1984,4,1,256]{0,3,2,1:T(8,128)(2,1)} %get-tuple-element.130) | data formatting | bytes 8126464
  395.2 6.2 %copy.176 = bf16[1984,4,1,256]{3,0,2,1:T(8,128)(2,1)} copy(bf16[1984,4,1,256]{0,3,2,1:T(8,128)(2,1)} %get-tuple-element.129) | data formatting | bytes 8126464
  403.7 6.1 %fusion.16 = f32[128,1984]{0,1:T(8,128)S(1)} fusion(bf16[1984,4,1,256]{3,0,2,1:T(8,128)(2,1)S(1)} %copy-done.8, bf16[1984,4,1,256]{3,0,2,1:T(8,128)(2,1)} %copy.180, bf16[1984,4,1,256]{3,0,2,1:T(8,128)(2,1)} %copy.179, bf16[4,1,128,256]{3,2,1,0:T(8,128)(2,1)S(1)} %get-tuple-element.40, bf16[4,1,128,256]{3,2,1,0:T(8,128)(2,1)S(1)} %get-tuple-element.41, ...), kind=kOutput, calls=%fused_computation.21 | convolution fusion | flops 1573257216 | bytes 13991936 | tf_op jit(solution)/shard_map/dot_general | solution.py:221
  412.2 3.4 fusion.19
  (247 shorter events, 109.1 us)
Async XLA Ops:
  6.5 210.3 %all-gather.2.cloned.1.call-start = ((), (), s32[]{:S(2)}) async-start(), calls=%async_computation.1 | async-start | bytes 17825792 | tf_op jit(solution)/shard_map/all_gather | solution.py:100
  9.1 291.5 %collective-permute-start.37 = (bf16[1984,4096]{1,0:T(8,128)(2,1)}, bf16[1984,4096]{1,0:T(8,128)(2,1)}, u32[]{:S(2)}, u32[]{:S(2)}) collective-permute-start(bf16[1984,4096]{1,0:T(8,128)(2,1)} %param.14), channel_id=1, source_target_pairs={{0,1},{1,0},{2,3},{3,2},{4,5},{5,4},{6,7},{7,6},{8,9},{9,8},{10,11... | collective-permute-start | bytes 48758792 | tf_op jit(solution)/shard_map/ppermute | solution.py:21
  14.3 17.9 %all-to-all-start = ((bf16[16,16,256]{2,0,1:T(8,128)(2,1)}), bf16[16,16,256]{2,0,1:T(8,128)(2,1)S(1)}, u32[]{:S(2)}, u32[]{:S(2)}) async-start(bf16[16,16,256]{2,0,1:T(8,128)(2,1)} %bitcast_select_fusion), calls=%async_computation | async-start | bytes 262144 | tf_op jit(solution)/shard_map/all_to_all | solution.py:103
  32.6 10.1 %collective-permute-start.2 = (f32[4,16,1024]{2,1,0:T(8,128)S(1)}, f32[4,16,1024]{2,1,0:T(8,128)S(1)}, u32[]{:S(2)}, u32[]{:S(2)}) collective-permute-start(f32[4,16,1024]{2,1,0:T(8,128)S(1)} %get-tuple-element.47), channel_id=1, source_target_pairs={{0,6},{2,4},{4,2},{6,0},{8,14},{10,12},{12,10},{14,8},{16,22},{18,... | collective-permute-start | bytes 786440 | tf_op jit(solution)/shard_map/ppermute | solution.py:21
  33.5 13.8 %collective-permute-start.1 = (f32[4,16,1024]{2,1,0:T(8,128)S(1)}, f32[4,16,1024]{2,1,0:T(8,128)S(1)}, u32[]{:S(2)}, u32[]{:S(2)}) collective-permute-start(f32[4,16,1024]{2,1,0:T(8,128)S(1)} %get-tuple-element.48), channel_id=1, source_target_pairs={{0,4},{2,6},{4,0},{6,2},{8,12},{10,14},{12,8},{14,10},{16,20},{18,... | collective-permute-start | bytes 786440 | tf_op jit(solution)/shard_map/ppermute | solution.py:21
  35.6 11.7 %collective-permute-start = (f32[4,16,1024]{2,1,0:T(8,128)S(1)}, f32[4,16,1024]{2,1,0:T(8,128)S(1)}, u32[]{:S(2)}, u32[]{:S(2)}) collective-permute-start(f32[4,16,1024]{2,1,0:T(8,128)S(1)} %get-tuple-element.46), channel_id=1, source_target_pairs={{0,2},{2,0},{4,6},{6,4},{8,10},{10,8},{12,14},{14,12},{16,18},{18,... | collective-permute-start | bytes 786440 | tf_op jit(solution)/shard_map/ppermute | solution.py:21
  49.5 7.4 %collective-permute-start.4 = (f32[1,16,1024]{2,1,0:T(8,128)S(1)}, f32[1,16,1024]{2,1,0:T(8,128)S(1)}, u32[]{:S(2)}, u32[]{:S(2)}) collective-permute-start(f32[1,16,1024]{2,1,0:T(8,128)S(1)} %get-tuple-element.71), channel_id=1, source_target_pairs={{0,16},{2,18},{4,20},{6,22},{8,24},{10,26},{12,28},{14,30},{16,0},... | collective-permute-start | bytes 196616 | tf_op jit(solution)/shard_map/ppermute | solution.py:21
  49.5 7.4 %collective-permute-start.3 = (f32[1,16,1024]{2,1,0:T(8,128)S(1)}, f32[1,16,1024]{2,1,0:T(8,128)S(1)}, u32[]{:S(2)}, u32[]{:S(2)}) collective-permute-start(f32[1,16,1024]{2,1,0:T(8,128)S(1)} %get-tuple-element.69), channel_id=1, source_target_pairs={{0,8},{2,10},{4,12},{6,14},{8,0},{10,2},{12,4},{14,6},{16,24},{18,... | collective-permute-start | bytes 196616 | tf_op jit(solution)/shard_map/ppermute | solution.py:21
  65.1 10.1 %collective-permute-start.11 = (bf16[4,16,1024]{2,1,0:T(8,128)(2,1)S(1)}, bf16[4,16,1024]{2,1,0:T(8,128)(2,1)S(1)}, u32[]{:S(2)}, u32[]{:S(2)}) collective-permute-start(bf16[4,16,1024]{2,1,0:T(8,128)(2,1)S(1)} %get-tuple-element.79), channel_id=1, source_target_pairs={{0,6},{2,4},{4,2},{6,0},{8,14},{10,12},{12,10},{14,8},{16,22},{18,... | collective-permute-start | bytes 393224 | tf_op jit(solution)/shard_map/ppermute | solution.py:21
  67.1 9.7 %collective-permute-start.10 = (bf16[4,16,1024]{2,1,0:T(8,128)(2,1)S(1)}, bf16[4,16,1024]{2,1,0:T(8,128)(2,1)S(1)}, u32[]{:S(2)}, u32[]{:S(2)}) collective-permute-start(bf16[4,16,1024]{2,1,0:T(8,128)(2,1)S(1)} %get-tuple-element.79), channel_id=1, source_target_pairs={{0,4},{2,6},{4,0},{6,2},{8,12},{10,14},{12,8},{14,10},{16,20},{18,... | collective-permute-start | bytes 393224 | tf_op jit(solution)/shard_map/ppermute | solution.py:21
  67.7 11.7 %collective-permute-start.9 = (bf16[4,16,1024]{2,1,0:T(8,128)(2,1)S(1)}, bf16[4,16,1024]{2,1,0:T(8,128)(2,1)S(1)}, u32[]{:S(2)}, u32[]{:S(2)}) collective-permute-start(bf16[4,16,1024]{2,1,0:T(8,128)(2,1)S(1)} %get-tuple-element.79), channel_id=1, source_target_pairs={{0,2},{2,0},{4,6},{6,4},{8,10},{10,8},{12,14},{14,12},{16,18},{18,... | collective-permute-start | bytes 393224 | tf_op jit(solution)/shard_map/ppermute | solution.py:21
  237.1 28.3 %collective-permute-start.14 = (f32[4,16,1040]{2,1,0:T(8,128)S(1)}, f32[4,16,1040]{2,1,0:T(8,128)S(1)}, u32[]{:S(2)}, u32[]{:S(2)}) collective-permute-start(f32[4,16,1040]{2,1,0:T(8,128)S(1)} %get-tuple-element.36), channel_id=1, source_target_pairs={{0,6},{2,4},{4,2},{6,0},{8,14},{10,12},{12,10},{14,8},{16,22},{18,... | collective-permute-start | bytes 798728 | tf_op jit(solution)/shard_map/ppermute | solution.py:21
  238.7 26.7 %collective-permute-start.13 = (f32[4,16,1040]{2,1,0:T(8,128)S(1)}, f32[4,16,1040]{2,1,0:T(8,128)S(1)}, u32[]{:S(2)}, u32[]{:S(2)}) collective-permute-start(f32[4,16,1040]{2,1,0:T(8,128)S(1)} %get-tuple-element.37), channel_id=1, source_target_pairs={{0,4},{2,6},{4,0},{6,2},{8,12},{10,14},{12,8},{14,10},{16,20},{18,... | collective-permute-start | bytes 798728 | tf_op jit(solution)/shard_map/ppermute | solution.py:21
  239.8 25.6 %collective-permute-start.12 = (f32[4,16,1040]{2,1,0:T(8,128)S(1)}, f32[4,16,1040]{2,1,0:T(8,128)S(1)}, u32[]{:S(2)}, u32[]{:S(2)}) collective-permute-start(f32[4,16,1040]{2,1,0:T(8,128)S(1)} %get-tuple-element.38), channel_id=1, source_target_pairs={{0,2},{2,0},{4,6},{6,4},{8,10},{10,8},{12,14},{14,12},{16,18},{18,... | collective-permute-start | bytes 798728 | tf_op jit(solution)/shard_map/ppermute | solution.py:21
  240.7 39.7 %collective-permute-start.40 = (s32[16]{0:T(128)S(1)}, s32[16]{0:T(128)S(1)}, u32[]{:S(2)}, u32[]{:S(2)}) collective-permute-start(s32[16]{0:T(128)S(1)} %bitcast.502), channel_id=1, source_target_pairs={{0,24},{2,26},{4,28},{6,30},{8,16},{10,18},{12,20},{14,22},{16,8},... | collective-permute-start | bytes 200 | tf_op jit(solution)/shard_map/ppermute | solution.py:21
  269.4 7.5 %collective-permute-start.15 = (f32[1,16,1040]{2,1,0:T(8,128)S(1)}, f32[1,16,1040]{2,1,0:T(8,128)S(1)}, u32[]{:S(2)}, u32[]{:S(2)}) collective-permute-start(f32[1,16,1040]{2,1,0:T(8,128)S(1)} %get-tuple-element.59), channel_id=1, source_target_pairs={{0,8},{2,10},{4,12},{6,14},{8,0},{10,2},{12,4},{14,6},{16,24},{18,... | collective-permute-start | bytes 199688 | tf_op jit(solution)/shard_map/ppermute | solution.py:21
  273.7 7.6 %collective-permute-start.39 = (s32[16]{0:T(128)S(1)}, s32[16]{0:T(128)S(1)}, u32[]{:S(2)}, u32[]{:S(2)}) collective-permute-start(s32[16]{0:T(128)S(1)} %bitcast.503), channel_id=1, source_target_pairs={{0,16},{2,18},{4,20},{6,22},{8,24},{10,26},{12,28},{14,30},{16,0},... | collective-permute-start | bytes 200 | tf_op jit(solution)/shard_map/ppermute | solution.py:21
  275.9 7.2 %collective-permute-start.38 = (s32[16]{0:T(128)S(1)}, s32[16]{0:T(128)S(1)}, u32[]{:S(2)}, u32[]{:S(2)}) collective-permute-start(s32[16]{0:T(128)S(1)} %bitcast.504), channel_id=1, source_target_pairs={{0,8},{2,10},{4,12},{6,14},{8,0},{10,2},{12,4},{14,6},{16,24},{18,... | collective-permute-start | bytes 200 | tf_op jit(solution)/shard_map/ppermute | solution.py:21
  296.9 26.2 %collective-permute-start.27 = (f32[128]{0:T(128)S(1)}, f32[128]{0:T(128)S(1)}, u32[]{:S(2)}, u32[]{:S(2)}) collective-permute-start(f32[128]{0:T(128)S(1)} %get-tuple-element.11), channel_id=1, source_target_pairs={{0,6},{2,4},{4,2},{6,0},{8,14},{10,12},{12,10},{14,8},{16,22},{18,... | collective-permute-start | bytes 1544 | tf_op jit(solution)/shard_map/ppermute | solution.py:21
  298.3 24.9 %collective-permute-start.26 = (f32[128]{0:T(128)S(1)}, f32[128]{0:T(128)S(1)}, u32[]{:S(2)}, u32[]{:S(2)}) collective-permute-start(f32[128]{0:T(128)S(1)} %get-tuple-element.11), channel_id=1, source_target_pairs={{0,4},{2,6},{4,0},{6,2},{8,12},{10,14},{12,8},{14,10},{16,20},{18,... | collective-permute-start | bytes 1544 | tf_op jit(solution)/shard_map/ppermute | solution.py:21
  299.3 23.8 %collective-permute-start.25 = (f32[128]{0:T(128)S(1)}, f32[128]{0:T(128)S(1)}, u32[]{:S(2)}, u32[]{:S(2)}) collective-permute-start(f32[128]{0:T(128)S(1)} %get-tuple-element.11), channel_id=1, source_target_pairs={{0,2},{2,0},{4,6},{6,4},{8,10},{10,8},{12,14},{14,12},{16,18},{18,... | collective-permute-start | bytes 1544 | tf_op jit(solution)/shard_map/ppermute | solution.py:21
  337.7 63.8 %collective-permute-start.36 = (bf16[4,128,256]{2,1,0:T(8,128)(2,1)S(1)}, bf16[4,128,256]{2,1,0:T(8,128)(2,1)S(1)}, u32[]{:S(2)}, u32[]{:S(2)}) collective-permute-start(bf16[4,128,256]{2,1,0:T(8,128)(2,1)S(1)} %get-tuple-element.64), channel_id=1, source_target_pairs={{0,6},{2,4},{4,2},{6,0},{8,14},{10,12},{12,10},{14,8},{16,22},{18,... | collective-permute-start | bytes 786440 | tf_op jit(solution)/shard_map/ppermute | solution.py:21
  339.1 62.5 %collective-permute-start.35 = (bf16[4,128,256]{2,1,0:T(8,128)(2,1)S(1)}, bf16[4,128,256]{2,1,0:T(8,128)(2,1)S(1)}, u32[]{:S(2)}, u32[]{:S(2)}) collective-permute-start(bf16[4,128,256]{2,1,0:T(8,128)(2,1)S(1)} %get-tuple-element.64), channel_id=1, source_target_pairs={{0,4},{2,6},{4,0},{6,2},{8,12},{10,14},{12,8},{14,10},{16,20},{18,... | collective-permute-start | bytes 786440 | tf_op jit(solution)/shard_map/ppermute | solution.py:21
  340.2 61.4 %collective-permute-start.34 = (bf16[4,128,256]{2,1,0:T(8,128)(2,1)S(1)}, bf16[4,128,256]{2,1,0:T(8,128)(2,1)S(1)}, u32[]{:S(2)}, u32[]{:S(2)}) collective-permute-start(bf16[4,128,256]{2,1,0:T(8,128)(2,1)S(1)} %get-tuple-element.64), channel_id=1, source_target_pairs={{0,2},{2,0},{4,6},{6,4},{8,10},{10,8},{12,14},{14,12},{16,18},{18,... | collective-permute-start | bytes 786440 | tf_op jit(solution)/shard_map/ppermute | solution.py:21
  (41 other events, 248.6 us)
Sparse Core Ops, SparseCore 0:
  10.1 206.6 all-gather.1
